TPU v7x, 512 devices: a whole 4x8x8 slice. The times are simulated.
512 devices in a mesh: frame: 16 (over z_lo, y), space: 32 (over z_hi, x, core).
Axes of the slice: x: 4, y: 8, z: 8 (z_hi: 4, z_lo: 2; z = z_hi * 2 + z_lo), core: 2. Of those that a mesh axis runs over, the one named last changes fastest.
Arguments:
- features: bfloat16 [16, 64, 512, 256], P('frame', None, 'space'), may hold values from -6 to 6
- enc_w: bfloat16 [3, 3, 64, 64], replicated, may hold values from -0.25 to 0.25
- enc_b: float32 [64], replicated, may hold values from -3 to 3
- mix_w: bfloat16 [128, 1024], replicated, may hold values from -0.1875 to 0.1875
- mix_b: float32 [128], replicated, may hold values from -3 to 3
- branch3: bfloat16 [3, 3, 1024, 16], P(None, None, 'frame'), may hold values from -0.5 to 0.5
- branch5: bfloat16 [5, 5, 1024, 16], P(None, None, 'frame'), may hold values from -0.3125 to 0.3125
- branch7: bfloat16 [7, 7, 1024, 16], P(None, None, 'frame'), may hold values from -0.21875 to 0.21875
- branch11: bfloat16 [11, 11, 1024, 16], P(None, None, 'frame'), may hold values from -0.125 to 0.125
- branch_b: float32 [4, 1024], P(None, 'frame'), may hold values from -3 to 3
- dec_w: bfloat16 [3, 3, 64, 64], replicated, may hold values from -0.25 to 0.25
- dec_b: float32 [64], replicated, may hold values from -3 to 3
Outputs:
- decoded: bfloat16 [16, 64, 512, 256], P('frame', None, 'space')
All inputs are finite; a program needn't handle non-finite values.
Results may differ from a plain program's by a relative error of at most 0.019.
Values may be sent and summed in bfloat16 or wider, within the bound.
No kernel may reach another device: no remote copies, remote signals or barrier semaphores. Data moves between devices by JAX's collectives and lax.ppermute only.
A program may use at most 64 MiB of HBM per device.

v0:
```python
import jax
import jax.numpy as jnp
from jax import lax
from jax.sharding import PartitionSpec as P

GROUPS = 8


def padded_2(block, sides, width):
    for axis, dim in sides:
        count = lax.axis_size(axis)
        forward = [(i, i + 1) for i in range(count - 1)]
        backward = [(target, source) for source, target in forward]
        low = lax.ppermute(
            lax.slice_in_dim(block, block.shape[dim] - width, None, axis=dim), axis, forward
        )
        high = lax.ppermute(lax.slice_in_dim(block, 0, width, axis=dim), axis, backward)
        block = jnp.concatenate([low, block, high], axis=dim)
    return block


def sweep(padded, weight, kernel_size, start, row_count, col_count):
    summed = jnp.zeros((padded.shape[0], weight.shape[3], row_count, col_count), jnp.float32)
    for row_tap in range(kernel_size):
        band = lax.slice_in_dim(padded, start + row_tap, start + row_tap + row_count, axis=2)
        window = jnp.stack(
            [
                lax.slice_in_dim(band, start + col_tap, start + col_tap + col_count, axis=3)
                for col_tap in range(kernel_size)
            ],
            axis=2,
        )
        summed = summed + jnp.einsum(
            "dgoi,gidrw->gorw", weight[row_tap], window, preferred_element_type=jnp.float32
        )
    return summed


def finish(padded, weight, bias, row_count, col_count):
    padded = jnp.pad(padded, ((0, 0), (0, 0), (0, 0), (1, 1)))
    summed = sweep(padded, weight[:, :, None], 3, 0, row_count, col_count)
    return jax.nn.silu(summed + bias[None, :, None, None]).astype(jnp.bfloat16)


def per_device(
    features,
    enc_w,
    enc_b,
    mix_w,
    mix_b,
    branch3,
    branch5,
    branch7,
    branch11,
    branch_b,
    dec_w,
    dec_b,
):
    frame_index = lax.axis_index("frame")
    frames = lax.axis_size("frame")
    channels, row_count, col_count = (features.shape[1], features.shape[2], features.shape[3])
    padded = padded_2(features, (("space", 2),), 1)
    encoded = finish(padded, enc_w, enc_b, row_count, col_count)
    hidden_count = mix_w.shape[0]
    frame_weight = lax.dynamic_slice_in_dim(mix_w, frame_index * channels, channels, 1)
    partial_mix = jnp.einsum(
        "ji,irw->jrw", frame_weight, encoded[0], preferred_element_type=jnp.float32
    )
    mixed_hidden = (
        lax.psum(partial_mix.astype(jnp.bfloat16), "frame").astype(jnp.float32)
        + mix_b[:, None, None]
    ).astype(jnp.bfloat16)
    per_group = frames * channels // GROUPS
    group_width = hidden_count // GROUPS
    local_groups = max(1, channels // per_group)
    first_group = frame_index * channels // per_group
    own_groups = lax.dynamic_slice_in_dim(
        mixed_hidden, first_group * group_width, local_groups * group_width, 0
    )
    margin = padded_2(own_groups, (("space", 1),), 5)
    margin = jnp.pad(margin, ((0, 0), (0, 0), (5, 5)))
    group_block = margin.reshape(local_groups, group_width, row_count + 10, col_count + 10)
    summed = jnp.zeros((channels, row_count, col_count), jnp.float32)
    for branch_index, weight in enumerate((branch3, branch5, branch7, branch11)):
        kernel_size = weight.shape[0]
        shaped = weight.reshape(
            kernel_size, kernel_size, local_groups, channels // local_groups, group_width
        )
        branch = sweep(group_block, shaped, kernel_size, 5 - kernel_size // 2, row_count, col_count)
        branch = (
            branch.reshape(channels, row_count, col_count) + branch_b[branch_index][:, None, None]
        )
        summed = summed + jnp.where(branch > 0, branch, 0.2 * branch)
    joined = (summed + encoded[0].astype(jnp.float32)).astype(jnp.bfloat16)[None]
    padded_dec = padded_2(joined, (("space", 2),), 1)
    return finish(padded_dec, dec_w, dec_b, row_count, col_count)


def solution(mesh):
    placed = (
        P("frame", None, "space", None),
        P(),
        P(),
        P(),
        P(),
        P(None, None, "frame", None),
        P(None, None, "frame", None),
        P(None, None, "frame", None),
        P(None, None, "frame", None),
        P(None, "frame"),
        P(),
        P(),
    )
    return jax.shard_map(
        per_device,
        mesh=mesh,
        in_specs=placed,
        out_specs=P("frame", None, "space", None),
        check_vma=False,
    )
```

profile of v0, /device:TPU:135, one launch (start us, length us, event | category | flops | bytes accessed | tf_op | source)
XLA Modules:
  0.0 233.9 jit_solution(14983483738900956218)
XLA Ops:
  6.5 1.2 copy.119
  7.8 7.5 %collective-permute-start = (bf16[1,64,1,256]{3,1,2,0:T(8,128)(2,1)S(1)}, bf16[1,64,1,256]{3,1,2,0:T(8,128)(2,1)S(1)}, u32[]{:S(2)}, u32[]{:S(2)}) collective-permute-start(bf16[1,64,1,256]{3,1,2,0:T(8,128)(2,1)S(1)} %get-tuple-element.25), channel_id=1, source_target_pairs={{0,1},{1,2},{2,3},{3,4},{4,5},{5,6},{6,7},{7,8},{8,9},{9,10},{10,1... | collective-permute-start | bytes 98312 | tf_op jit(solution)/shard_map/ppermute | solution.py:14
  15.3 1.9 collective-permute-start.1
  17.2 7.5 %collective-permute-done.1 = bf16[1,64,1,256]{3,1,2,0:T(8,128)(2,1)S(1)} collective-permute-done((bf16[1,64,1,256]{3,1,2,0:T(8,128)(2,1)S(1)}, bf16[1,64,1,256]{3,1,2,0:T(8,128)(2,1)S(1)}, u32[]{:S(2)}, u32[]{:S(2)}) %collective-permute-start.1) | collective-permute-done | bytes 32800 | tf_op jit(solution)/shard_map/ppermute | solution.py:17
  24.8 0.5 fusion.172
  25.2 0.6 fusion.183
  25.8 0.3 copy-done.7
  26.1 0.4 fusion.57
  26.6 0.4 fusion.56
  27.2 0.6 multiply_convert_fusion.1
  27.9 1.5 convolution_convert_fusion
  29.5 130.7 %all-reduce.5.cloned.1.call-done = bf16[128,16,256]{2,0,1:T(8,128)(2,1)} async-done(((bf16[128,16,256]{2,0,1:T(8,128)(2,1)}), bf16[128,16,256]{2,0,1:T(8,128)(2,1)}) %all-reduce.5.cloned.1.call-update) | async-done | bytes 1048592 | tf_op jit(solution)/shard_map/psum | solution.py:70
  160.2 1.0 add_convert_fusion
  161.2 16.2 %collective-permute-start.2 = (bf16[16,5,256]{2,0,1:T(8,128)(2,1)S(1)}, bf16[16,5,256]{2,0,1:T(8,128)(2,1)S(1)}, u32[]{:S(2)}, u32[]{:S(2)}) collective-permute-start(bf16[16,5,256]{2,0,1:T(8,128)(2,1)S(1)} %get-tuple-element.222), channel_id=1, source_target_pairs={{0,1},{1,2},{2,3},{3,4},{4,5},{5,6},{6,7},{7,8},{8,9},{9,10},{10,1... | collective-permute-start | bytes 122888 | tf_op jit(solution)/shard_map/ppermute | solution.py:14
  177.4 2.1 collective-permute-start.3
  179.6 7.4 %collective-permute-done.3 = bf16[16,5,256]{2,0,1:T(8,128)(2,1)S(1)} collective-permute-done((bf16[16,5,256]{2,0,1:T(8,128)(2,1)S(1)}, bf16[16,5,256]{2,0,1:T(8,128)(2,1)S(1)}, u32[]{:S(2)}, u32[]{:S(2)}) %collective-permute-start.3) | collective-permute-done | bytes 40992 | tf_op jit(solution)/shard_map/ppermute | solution.py:17
  187.2 0.4 slice_bitcast_fusion.132
  188.4 0.4 constant_dynamic-update-slice_fusion.9
  189.4 0.5 constant_dynamic-update-slice_fusion.5
  190.0 0.3 copy-done.4
  190.3 0.3 convolution_bitcast_fusion.13
  190.6 0.3 convolution_bitcast_fusion.10
  191.0 0.3 convolution_bitcast_fusion.11
  192.2 0.5 constant_dynamic-update-slice_fusion.4
  192.7 0.4 copy-done.3
  193.1 0.3 convolution_bitcast_fusion.6
  193.5 0.3 convolution_bitcast_fusion.7
  193.8 0.3 convolution_bitcast_fusion.8
  194.9 0.4 constant_dynamic-update-slice_fusion.3
  195.3 0.3 convolution_bitcast_fusion.3
  195.7 0.3 convolution_bitcast_fusion.4
  196.0 0.3 convolution_bitcast_fusion.5
  196.4 0.4 constant_dynamic-update-slice_fusion.2
  198.7 0.4 constant_dynamic-update-slice_fusion.1
  200.1 0.4 constant_dynamic-update-slice_fusion
  201.9 0.3 convolution_bitcast_fusion.12
  202.3 0.4 copy-done.2
  202.7 0.4 fusion.59
  203.1 0.6 fusion.157
  203.7 0.4 fusion.154
  204.2 0.4 fusion.151
  204.6 0.4 fusion.148
  205.0 0.4 fusion.145
  205.5 0.4 fusion.142
  205.9 0.4 fusion.139
  206.3 0.4 fusion.136
  206.8 0.4 fusion.133
  207.2 0.3 copy-done.5
  207.5 0.3 convolution_bitcast_fusion
  207.9 0.3 convolution_bitcast_fusion.1
  208.2 0.4 compare_select_fusion
  208.7 0.6 compare_select_fusion.2
  209.3 0.7 compare_select_fusion.1
  210.0 0.8 fusion.160
  210.8 1.9 collective-permute-start.4
  212.7 2.4 %collective-permute-start.5 = (bf16[1,64,1,256]{3,1,2,0:T(8,128)(2,1)S(1)}, bf16[1,64,1,256]{3,1,2,0:T(8,128)(2,1)S(1)}, u32[]{:S(2)}, u32[]{:S(2)}) collective-permute-start(bf16[1,64,1,256]{3,1,2,0:T(8,128)(2,1)S(1)} %get-tuple-element.20), channel_id=1, source_target_pairs={{1,0},{2,1},{3,2},{4,3},{5,4},{6,5},{7,6},{8,7},{9,8},{10,9},{11,1... | collective-permute-start | bytes 98312 | tf_op jit(solution)/shard_map/ppermute | solution.py:17
  215.1 7.0 %collective-permute-done.5 = bf16[1,64,1,256]{3,1,2,0:T(8,128)(2,1)S(1)} collective-permute-done((bf16[1,64,1,256]{3,1,2,0:T(8,128)(2,1)S(1)}, bf16[1,64,1,256]{3,1,2,0:T(8,128)(2,1)S(1)}, u32[]{:S(2)}, u32[]{:S(2)}) %collective-permute-start.5) | collective-permute-done | bytes 32800 | tf_op jit(solution)/shard_map/ppermute | solution.py:17
  222.1 0.5 select_maximum_fusion
  222.6 0.7 slice_bitcast_fusion.5
  223.4 0.8 copy-done.8
  224.2 0.5 fusion.53
  224.7 0.5 fusion.54
  225.4 0.6 fusion.173
  226.0 1.1 copy.52
  (74 shorter events, 8.0 us)
Async XLA Ops:
  6.5 21.3 %copy-start = (bf16[128,1024]{1,0:T(8,128)(2,1)S(1)}, bf16[128,1024]{1,0:T(8,128)(2,1)}, u32[]{:S(2)}) copy-start(bf16[128,1024]{1,0:T(8,128)(2,1)} %param.15) | copy-start | bytes 786436
  6.5 153.7 %all-reduce.5.cloned.1.call-start = ((), (), s32[]{:S(2)}) async-start(), calls=%async_computation | async-start | bytes 2097152 | tf_op jit(solution)/shard_map/psum | solution.py:70
  7.8 9.4 %collective-permute-start = (bf16[1,64,1,256]{3,1,2,0:T(8,128)(2,1)S(1)}, bf16[1,64,1,256]{3,1,2,0:T(8,128)(2,1)S(1)}, u32[]{:S(2)}, u32[]{:S(2)}) collective-permute-start(bf16[1,64,1,256]{3,1,2,0:T(8,128)(2,1)S(1)} %get-tuple-element.25), channel_id=1, source_target_pairs={{0,1},{1,2},{2,3},{3,4},{4,5},{5,6},{6,7},{7,8},{8,9},{9,10},{10,1... | collective-permute-start | bytes 98312 | tf_op jit(solution)/shard_map/ppermute | solution.py:14
  15.3 9.5 %collective-permute-start.1 = (bf16[1,64,1,256]{3,1,2,0:T(8,128)(2,1)S(1)}, bf16[1,64,1,256]{3,1,2,0:T(8,128)(2,1)S(1)}, u32[]{:S(2)}, u32[]{:S(2)}) collective-permute-start(bf16[1,64,1,256]{3,1,2,0:T(8,128)(2,1)S(1)} %get-tuple-element.26), channel_id=1, source_target_pairs={{1,0},{2,1},{3,2},{4,3},{5,4},{6,5},{7,6},{8,7},{9,8},{10,9},{11,1... | collective-permute-start | bytes 98312 | tf_op jit(solution)/shard_map/ppermute | solution.py:17
  25.2 0.9 copy-start.7
  26.6 0.7 copy-start.9
  27.9 1.5 copy-start.10
  27.9 151.7 %copy-start.6 = (f32[4,64]{1,0:T(4,128)S(1)}, f32[4,64]{1,0:T(4,128)}, u32[]{:S(2)}) copy-start(f32[4,64]{1,0:T(4,128)} %param.21) | copy-start | bytes 3076
  161.2 18.4 %collective-permute-start.2 = (bf16[16,5,256]{2,0,1:T(8,128)(2,1)S(1)}, bf16[16,5,256]{2,0,1:T(8,128)(2,1)S(1)}, u32[]{:S(2)}, u32[]{:S(2)}) collective-permute-start(bf16[16,5,256]{2,0,1:T(8,128)(2,1)S(1)} %get-tuple-element.222), channel_id=1, source_target_pairs={{0,1},{1,2},{2,3},{3,4},{4,5},{5,6},{6,7},{7,8},{8,9},{9,10},{10,1... | collective-permute-start | bytes 122888 | tf_op jit(solution)/shard_map/ppermute | solution.py:14
  177.4 9.5 %collective-permute-start.3 = (bf16[16,5,256]{2,0,1:T(8,128)(2,1)S(1)}, bf16[16,5,256]{2,0,1:T(8,128)(2,1)S(1)}, u32[]{:S(2)}, u32[]{:S(2)}) collective-permute-start(bf16[16,5,256]{2,0,1:T(8,128)(2,1)S(1)} %get-tuple-element.223), channel_id=1, source_target_pairs={{1,0},{2,1},{3,2},{4,3},{5,4},{6,5},{7,6},{8,7},{9,8},{10,9},{11,1... | collective-permute-start | bytes 122888 | tf_op jit(solution)/shard_map/ppermute | solution.py:17
  189.4 0.9 copy-start.4
  192.2 0.9 copy-start.3
  201.6 1.0 copy-start.2
  206.7 0.8 copy-start.5
  210.8 4.3 %collective-permute-start.4 = (bf16[1,64,1,256]{3,1,2,0:T(8,128)(2,1)S(1)}, bf16[1,64,1,256]{3,1,2,0:T(8,128)(2,1)S(1)}, u32[]{:S(2)}, u32[]{:S(2)}) collective-permute-start(bf16[1,64,1,256]{3,1,2,0:T(8,128)(2,1)S(1)} %get-tuple-element.19), channel_id=1, source_target_pairs={{0,1},{1,2},{2,3},{3,4},{4,5},{5,6},{6,7},{7,8},{8,9},{9,10},{10,1... | collective-permute-start | bytes 98312 | tf_op jit(solution)/shard_map/ppermute | solution.py:14
  212.7 9.5 %collective-permute-start.5 = (bf16[1,64,1,256]{3,1,2,0:T(8,128)(2,1)S(1)}, bf16[1,64,1,256]{3,1,2,0:T(8,128)(2,1)S(1)}, u32[]{:S(2)}, u32[]{:S(2)}) collective-permute-start(bf16[1,64,1,256]{3,1,2,0:T(8,128)(2,1)S(1)} %get-tuple-element.20), channel_id=1, source_target_pairs={{1,0},{2,1},{3,2},{4,3},{5,4},{6,5},{7,6},{8,7},{9,8},{10,9},{11,1... | collective-permute-start | bytes 98312 | tf_op jit(solution)/shard_map/ppermute | solution.py:17
  223.3 0.9 copy-start.8
  224.7 0.7 copy-start.11
  225.4 1.7 copy-start.1
Sparse Core Ops, SparseCore 0:
  29.5 130.6 all-reduce.4
where the time goes:
time: 234 us
  waiting for transfers between devices  153 us (65%)
  starting transfers between devices  32.1 us (14%)
  local copies, waits for them, and re-layouts  16.6 us (7%)
  matrix products  15.5 us (7%)
  between operations  14.2 us (6%)
  other arithmetic  2.75 us (1%)
    psum x1, waiting for transfers between devices, per_device(): lax.psum(partial_mix.astype(jnp.bfloat16), 'frame').astype(jnp.float32)  131 us
    ppermute x3, starting transfers between devices, padded_2(): lax.ppermute(lax.slice_in_dim(block, block.shape[dim] - width, None, axis...  25.6 us
    ppermute x3, waiting for transfers between devices, padded_2(): lax.ppermute(lax.slice_in_dim(block, 0, width, axis=dim), axis, backward)  21.9 us
    dot_general x32, matrix products, sweep(): jnp.einsum('dgoi,gidrw->gorw', weight[row_tap], window, preferred_element...  14.1 us
    unnamed x73, local copies, waits for them, and re-layouts  13.2 us
    ppermute x3, starting transfers between devices, padded_2(): lax.ppermute(lax.slice_in_dim(block, 0, width, axis=dim), axis, backward)  6.43 us
  transfers between devices with their start and end apart: 7, of which 4 were waited for; matrix products, arithmetic and copies ran while one was open for 0% of the time, Pallas kernels for 0%

commit v1 on v0

--- a/solution.py
+++ b/solution.py
@@ -17,6 +17,31 @@
         high = lax.ppermute(lax.slice_in_dim(block, 0, width, axis=dim), axis, backward)
         block = jnp.concatenate([low, block, high], axis=dim)
     return block
+
+
+def halving_sum(partial, frame_index, frames, group_width):
+    share = frames // GROUPS
+    bits = GROUPS.bit_length() - 1
+    group_index = frame_index // share
+    blocks = partial.reshape((2,) * bits + (group_width,) + partial.shape[1:])
+    order = [bits - 1] + list(range(bits - 1))
+    axis_of = {bit: bits - 1 - bit for bit in range(bits)}
+    for position, bit in enumerate(order):
+        axis = axis_of[bit] - sum(1 for done in order[:position] if axis_of[done] < axis_of[bit])
+        mine = (group_index >> bit) & 1
+        keep = lax.dynamic_index_in_dim(blocks, mine, axis, keepdims=False)
+        send = lax.dynamic_index_in_dim(blocks, 1 - mine, axis, keepdims=False)
+        step = share << bit
+        pairs = [(i, i ^ step) for i in range(frames)]
+        got = lax.ppermute(send.astype(jnp.bfloat16), "frame", pairs)
+        blocks = keep + got.astype(jnp.float32)
+    step = 1
+    while step < share:
+        pairs = [(i, i ^ step) for i in range(frames)]
+        got = lax.ppermute(blocks.astype(jnp.bfloat16), "frame", pairs)
+        blocks = blocks.astype(jnp.bfloat16).astype(jnp.float32) + got.astype(jnp.float32)
+        step *= 2
+    return blocks
 
 
 def sweep(padded, weight, kernel_size, start, row_count, col_count):
@@ -66,17 +91,15 @@
     partial_mix = jnp.einsum(
         "ji,irw->jrw", frame_weight, encoded[0], preferred_element_type=jnp.float32
     )
-    mixed_hidden = (
-        lax.psum(partial_mix.astype(jnp.bfloat16), "frame").astype(jnp.float32)
-        + mix_b[:, None, None]
-    ).astype(jnp.bfloat16)
     per_group = frames * channels // GROUPS
     group_width = hidden_count // GROUPS
     local_groups = max(1, channels // per_group)
-    first_group = frame_index * channels // per_group
-    own_groups = lax.dynamic_slice_in_dim(
-        mixed_hidden, first_group * group_width, local_groups * group_width, 0
-    )
+    own_groups = (
+        halving_sum(partial_mix, frame_index, frames, group_width)
+        + lax.dynamic_slice_in_dim(
+            mix_b, (frame_index * channels // per_group) * group_width, group_width
+        )[:, None, None]
+    ).astype(jnp.bfloat16)
     margin = padded_2(own_groups, (("space", 1),), 5)
     margin = jnp.pad(margin, ((0, 0), (0, 0), (5, 5)))
     group_block = margin.reshape(local_groups, group_width, row_count + 10, col_count + 10)

time: 234 us -> 123 us (0.53)
  waiting for transfers between devices: 153 us -> 45.5 us
  between operations: 14.2 us -> 0.96 us
  starting transfers between devices: 32.1 us -> 40.7 us
    psum x1 -> x0, waiting for transfers between devices: 131 us -> none  [per_device(): lax.psum(partial_mix.astype(jnp.bfloat16), 'frame').astype(jnp.float32)]
    ppermute x0 -> x4, waiting for transfers between devices: none -> 23.6 us  [the longest x3 19.9 us: halving_sum(): got = lax.ppermute(send.astype(jnp.bfloat16), 'frame', pairs)]
    ppermute x0 -> x4, starting transfers between devices: none -> 16.7 us  [the longest x3 14.8 us: halving_sum(): got = lax.ppermute(send.astype(jnp.bfloat16), 'frame', pairs)]
    ppermute x3, starting transfers between devices: 25.6 us -> 17.5 us  [padded_2(): lax.ppermute(lax.slice_in_dim(block, block.shape[dim] - width, None, axis...]
    unnamed x73 -> x77, local copies, waits for them, and re-layouts: 13.2 us -> 13.9 us
  transfers between devices with their start and end apart: 7 -> 10, of which waited for: 4 -> 7; matrix products, arithmetic and copies ran while one was open for 0% -> 0% of each run, Pallas kernels for 0% -> 0%
where the time goes in v1:
time: 123 us; the launch traced here: 122 us
  waiting for transfers between devices  45.5 us (37%)
  starting transfers between devices  40.7 us (33%)
  local copies, waits for them, and re-layouts  17.5 us (14%)
  matrix products  14.5 us (12%)
  other arithmetic  3.17 us (3%)
    ppermute x3, waiting for transfers between devices, padded_2(): lax.ppermute(lax.slice_in_dim(block, 0, width, axis=dim), axis, backward)  21.8 us
    ppermute x3, waiting for transfers between devices, halving_sum(): got = lax.ppermute(send.astype(jnp.bfloat16), 'frame', pairs)  19.9 us
    ppermute x3, starting transfers between devices, padded_2(): lax.ppermute(lax.slice_in_dim(block, block.shape[dim] - width, None, axis...  17.5 us
    ppermute x3, starting transfers between devices, halving_sum(): got = lax.ppermute(send.astype(jnp.bfloat16), 'frame', pairs)  14.8 us
    dot_general x32, matrix products, sweep(): jnp.einsum('dgoi,gidrw->gorw', weight[row_tap], window, preferred_element...  14.1 us
    unnamed x77, local copies, waits for them, and re-layouts  13.9 us
    ppermute x3, starting transfers between devices, padded_2(): lax.ppermute(lax.slice_in_dim(block, 0, width, axis=dim), axis, backward)  6.43 us
    ppermute x1, waiting for transfers between devices, halving_sum(): got = lax.ppermute(blocks.astype(jnp.bfloat16), 'frame', pairs)  3.68 us
  transfers between devices with their start and end apart: 10, of which 7 were waited for; matrix products, arithmetic and copies ran while one was open for 0% of the time, Pallas kernels for 0%

profile of v1, /device:TPU:135, one launch (start us, length us, event | category | flops | bytes accessed | tf_op | source)
XLA Modules:
  0.0 122.3 jit_solution(567929518873320121)
XLA Ops:
  0.0 1.2 %copy.119 = bf16[1,64,16,256]{3,1,2,0:T(8,128)(2,1)S(1)} copy(bf16[1,64,16,256]{3,2,1,0:T(8,128)(2,1)} %param.12) | data formatting | bytes 1048576 | tf_op args[0]
  1.3 7.5 %collective-permute-start = (bf16[1,64,1,256]{3,1,2,0:T(8,128)(2,1)S(1)}, bf16[1,64,1,256]{3,1,2,0:T(8,128)(2,1)S(1)}, u32[]{:S(2)}, u32[]{:S(2)}) collective-permute-start(bf16[1,64,1,256]{3,1,2,0:T(8,128)(2,1)S(1)} %get-tuple-element.25), channel_id=1, source_target_pairs={{0,1},{1,2},{2,3},{3,4},{4,5},{5,6},{6,7},{7,8},{8,9},{9,10},{10,1... | collective-permute-start | bytes 98312 | tf_op jit(solution)/shard_map/ppermute | solution.py:14
  8.8 1.9 %collective-permute-start.1 = (bf16[1,64,1,256]{3,1,2,0:T(8,128)(2,1)S(1)}, bf16[1,64,1,256]{3,1,2,0:T(8,128)(2,1)S(1)}, u32[]{:S(2)}, u32[]{:S(2)}) collective-permute-start(bf16[1,64,1,256]{3,1,2,0:T(8,128)(2,1)S(1)} %get-tuple-element.26), channel_id=1, source_target_pairs={{1,0},{2,1},{3,2},{4,3},{5,4},{6,5},{7,6},{8,7},{9,8},{10,9},{11,1... | collective-permute-start | bytes 98312 | tf_op jit(solution)/shard_map/ppermute | solution.py:17
  10.8 7.4 %collective-permute-done.1 = bf16[1,64,1,256]{3,1,2,0:T(8,128)(2,1)S(1)} collective-permute-done((bf16[1,64,1,256]{3,1,2,0:T(8,128)(2,1)S(1)}, bf16[1,64,1,256]{3,1,2,0:T(8,128)(2,1)S(1)}, u32[]{:S(2)}, u32[]{:S(2)}) %collective-permute-start.1) | collective-permute-done | bytes 32800 | tf_op jit(solution)/shard_map/ppermute | solution.py:17
  18.2 0.5 fusion.172
  18.7 0.6 fusion.184
  19.6 0.4 fusion.57
  20.1 0.5 fusion.56
  20.7 0.6 multiply_convert_fusion.1
  21.3 0.4 fusion.185
  22.1 3.1 %collective-permute-start.2 = (bf16[2,2,16,16,256]{4,2,3,1,0:T(8,128)(2,1)S(1)}, bf16[2,2,16,16,256]{4,2,3,1,0:T(8,128)(2,1)}, u32[]{:S(2)}, u32[]{:S(2)}) collective-permute-start(bf16[2,2,16,16,256]{4,2,3,1,0:T(8,128)(2,1)S(1)} %fusion.180), channel_id=1, source_target_pairs={{0,256},{32,288},{64,320},{96,352},{128,384},{160,416},{192,448},{... | collective-permute-start | bytes 1572872 | tf_op jit(solution)/shard_map/ppermute | solution.py:36
  25.3 6.9 %collective-permute-done.2 = bf16[2,2,16,16,256]{4,2,3,1,0:T(8,128)(2,1)} collective-permute-done((bf16[2,2,16,16,256]{4,2,3,1,0:T(8,128)(2,1)S(1)}, bf16[2,2,16,16,256]{4,2,3,1,0:T(8,128)(2,1)}, u32[]{:S(2)}, u32[]{:S(2)}) %collective-permute-start.2) | collective-permute-done | bytes 524320 | tf_op jit(solution)/shard_map/ppermute | solution.py:36
  32.1 1.2 bitcast_add_fusion
  33.4 4.2 %collective-permute-start.3 = (bf16[2,16,16,256]{3,1,2,0:T(8,128)(2,1)S(1)}, bf16[2,16,16,256]{3,1,2,0:T(8,128)(2,1)S(1)}, u32[]{:S(2)}, u32[]{:S(2)}) collective-permute-start(bf16[2,16,16,256]{3,1,2,0:T(8,128)(2,1)S(1)} %fusion.205), channel_id=1, source_target_pairs={{0,64},{32,96},{64,0},{96,32},{128,192},{160,224},{192,128},{224,1... | collective-permute-start | bytes 786440 | tf_op jit(solution)/shard_map/ppermute | solution.py:36
  37.7 7.5 %collective-permute-done.3 = bf16[2,16,16,256]{3,1,2,0:T(8,128)(2,1)S(1)} collective-permute-done((bf16[2,16,16,256]{3,1,2,0:T(8,128)(2,1)S(1)}, bf16[2,16,16,256]{3,1,2,0:T(8,128)(2,1)S(1)}, u32[]{:S(2)}, u32[]{:S(2)}) %collective-permute-start.3) | collective-permute-done | bytes 262176 | tf_op jit(solution)/shard_map/ppermute | solution.py:36
  45.3 7.5 %collective-permute-start.4 = (bf16[16,16,256]{2,0,1:T(8,128)(2,1)S(1)}, bf16[16,16,256]{2,0,1:T(8,128)(2,1)S(1)}, u32[]{:S(2)}, u32[]{:S(2)}) collective-permute-start(bf16[16,16,256]{2,0,1:T(8,128)(2,1)S(1)} %fusion.207), channel_id=1, source_target_pairs={{0,128},{32,160},{64,192},{96,224},{128,0},{160,32},{192,64},{224,... | collective-permute-start | bytes 393224 | tf_op jit(solution)/shard_map/ppermute | solution.py:36
  52.7 5.6 %collective-permute-done.4 = bf16[16,16,256]{2,0,1:T(8,128)(2,1)S(1)} collective-permute-done((bf16[16,16,256]{2,0,1:T(8,128)(2,1)S(1)}, bf16[16,16,256]{2,0,1:T(8,128)(2,1)S(1)}, u32[]{:S(2)}, u32[]{:S(2)}) %collective-permute-start.4) | collective-permute-done | bytes 131104 | tf_op jit(solution)/shard_map/ppermute | solution.py:36
  58.4 1.9 %collective-permute-start.5 = (bf16[16,16,256]{2,0,1:T(8,128)(2,1)S(1)}, bf16[16,16,256]{2,0,1:T(8,128)(2,1)S(1)}, u32[]{:S(2)}, u32[]{:S(2)}) collective-permute-start(bf16[16,16,256]{2,0,1:T(8,128)(2,1)S(1)} %fusion.206), channel_id=1, source_target_pairs={{0,32},{32,0},{64,96},{96,64},{128,160},{160,128},{192,224},{224,1... | collective-permute-start | bytes 393224 | tf_op jit(solution)/shard_map/ppermute | solution.py:41
  60.4 3.7 %collective-permute-done.5 = bf16[16,16,256]{2,0,1:T(8,128)(2,1)S(1)} collective-permute-done((bf16[16,16,256]{2,0,1:T(8,128)(2,1)S(1)}, bf16[16,16,256]{2,0,1:T(8,128)(2,1)S(1)}, u32[]{:S(2)}, u32[]{:S(2)}) %collective-permute-start.5) | collective-permute-done | bytes 131104 | tf_op jit(solution)/shard_map/ppermute | solution.py:41
  64.2 8.1 %collective-permute-start.6 = (bf16[16,5,256]{2,0,1:T(8,128)(2,1)S(1)}, bf16[16,5,256]{2,0,1:T(8,128)(2,1)S(1)}, u32[]{:S(2)}, u32[]{:S(2)}) collective-permute-start(bf16[16,5,256]{2,0,1:T(8,128)(2,1)S(1)} %get-tuple-element.222), channel_id=1, source_target_pairs={{0,1},{1,2},{2,3},{3,4},{4,5},{5,6},{6,7},{7,8},{8,9},{9,10},{10,1... | collective-permute-start | bytes 122888 | tf_op jit(solution)/shard_map/ppermute | solution.py:14
  72.3 2.1 %collective-permute-start.7 = (bf16[16,5,256]{2,0,1:T(8,128)(2,1)S(1)}, bf16[16,5,256]{2,0,1:T(8,128)(2,1)S(1)}, u32[]{:S(2)}, u32[]{:S(2)}) collective-permute-start(bf16[16,5,256]{2,0,1:T(8,128)(2,1)S(1)} %get-tuple-element.223), channel_id=1, source_target_pairs={{1,0},{2,1},{3,2},{4,3},{5,4},{6,5},{7,6},{8,7},{9,8},{10,9},{11,1... | collective-permute-start | bytes 122888 | tf_op jit(solution)/shard_map/ppermute | solution.py:17
  74.4 7.4 %collective-permute-done.7 = bf16[16,5,256]{2,0,1:T(8,128)(2,1)S(1)} collective-permute-done((bf16[16,5,256]{2,0,1:T(8,128)(2,1)S(1)}, bf16[16,5,256]{2,0,1:T(8,128)(2,1)S(1)}, u32[]{:S(2)}, u32[]{:S(2)}) %collective-permute-start.7) | collective-permute-done | bytes 40992 | tf_op jit(solution)/shard_map/ppermute | solution.py:17
  82.0 0.4 slice_bitcast_fusion.132
  83.3 0.4 constant_dynamic-update-slice_fusion.9
  84.2 0.5 constant_dynamic-update-slice_fusion.5
  85.1 0.3 convolution_bitcast_fusion.13
  85.5 0.3 convolution_bitcast_fusion.10
  85.8 0.3 convolution_bitcast_fusion.11
  87.1 0.5 constant_dynamic-update-slice_fusion.4
  87.5 0.5 copy-done.5
  88.0 0.3 convolution_bitcast_fusion.6
  88.3 0.3 convolution_bitcast_fusion.7
  88.7 0.3 convolution_bitcast_fusion.8
  89.8 0.4 constant_dynamic-update-slice_fusion.3
  90.2 0.3 convolution_bitcast_fusion.3
  91.2 0.4 constant_dynamic-update-slice_fusion.2
  93.5 0.4 constant_dynamic-update-slice_fusion.1
  94.9 0.4 constant_dynamic-update-slice_fusion
  96.8 0.3 convolution_bitcast_fusion.12
  97.1 0.4 copy-done.4
  97.5 0.4 fusion.59
  98.0 0.6 fusion.157
  98.6 0.4 fusion.154
  99.0 0.4 fusion.151
  99.5 0.4 fusion.148
  99.9 0.4 fusion.145
  100.4 0.4 fusion.142
  100.8 0.4 fusion.139
  101.3 0.4 fusion.136
  101.7 0.4 fusion.133
  103.2 0.4 compare_select_fusion
  103.6 0.5 compare_select_fusion.2
  104.2 0.7 compare_select_fusion.1
  105.2 0.7 fusion.160
  106.0 1.9 %collective-permute-start.8 = (bf16[1,64,1,256]{3,1,2,0:T(8,128)(2,1)S(1)}, bf16[1,64,1,256]{3,1,2,0:T(8,128)(2,1)S(1)}, u32[]{:S(2)}, u32[]{:S(2)}) collective-permute-start(bf16[1,64,1,256]{3,1,2,0:T(8,128)(2,1)S(1)} %get-tuple-element.19), channel_id=1, source_target_pairs={{0,1},{1,2},{2,3},{3,4},{4,5},{5,6},{6,7},{7,8},{8,9},{9,10},{10,1... | collective-permute-start | bytes 98312 | tf_op jit(solution)/shard_map/ppermute | solution.py:14
  107.9 2.4 %collective-permute-start.9 = (bf16[1,64,1,256]{3,1,2,0:T(8,128)(2,1)S(1)}, bf16[1,64,1,256]{3,1,2,0:T(8,128)(2,1)S(1)}, u32[]{:S(2)}, u32[]{:S(2)}) collective-permute-start(bf16[1,64,1,256]{3,1,2,0:T(8,128)(2,1)S(1)} %get-tuple-element.20), channel_id=1, source_target_pairs={{1,0},{2,1},{3,2},{4,3},{5,4},{6,5},{7,6},{8,7},{9,8},{10,9},{11,1... | collective-permute-start | bytes 98312 | tf_op jit(solution)/shard_map/ppermute | solution.py:17
  110.3 7.0 %collective-permute-done.9 = bf16[1,64,1,256]{3,1,2,0:T(8,128)(2,1)S(1)} collective-permute-done((bf16[1,64,1,256]{3,1,2,0:T(8,128)(2,1)S(1)}, bf16[1,64,1,256]{3,1,2,0:T(8,128)(2,1)S(1)}, u32[]{:S(2)}, u32[]{:S(2)}) %collective-permute-start.9) | collective-permute-done | bytes 32800 | tf_op jit(solution)/shard_map/ppermute | solution.py:17
  117.4 0.5 select_maximum_fusion
  117.8 0.7 slice_bitcast_fusion.5
  118.6 0.8 copy-done.10
  119.5 0.5 fusion.53
  119.9 0.5 fusion.54
  120.6 0.6 fusion.173
  121.2 1.1 copy.51
  (90 shorter events, 11.3 us)
Async XLA Ops:
  0.0 10.7 %copy-start = (bf16[128,1024]{1,0:T(8,128)(2,1)S(1)}, bf16[128,1024]{1,0:T(8,128)(2,1)}, u32[]{:S(2)}) copy-start(bf16[128,1024]{1,0:T(8,128)(2,1)} %param.15) | copy-start | bytes 786436
  1.3 9.5 %collective-permute-start = (bf16[1,64,1,256]{3,1,2,0:T(8,128)(2,1)S(1)}, bf16[1,64,1,256]{3,1,2,0:T(8,128)(2,1)S(1)}, u32[]{:S(2)}, u32[]{:S(2)}) collective-permute-start(bf16[1,64,1,256]{3,1,2,0:T(8,128)(2,1)S(1)} %get-tuple-element.25), channel_id=1, source_target_pairs={{0,1},{1,2},{2,3},{3,4},{4,5},{5,6},{6,7},{7,8},{8,9},{9,10},{10,1... | collective-permute-start | bytes 98312 | tf_op jit(solution)/shard_map/ppermute | solution.py:14
  8.8 9.5 %collective-permute-start.1 = (bf16[1,64,1,256]{3,1,2,0:T(8,128)(2,1)S(1)}, bf16[1,64,1,256]{3,1,2,0:T(8,128)(2,1)S(1)}, u32[]{:S(2)}, u32[]{:S(2)}) collective-permute-start(bf16[1,64,1,256]{3,1,2,0:T(8,128)(2,1)S(1)} %get-tuple-element.26), channel_id=1, source_target_pairs={{1,0},{2,1},{3,2},{4,3},{5,4},{6,5},{7,6},{8,7},{9,8},{10,9},{11,1... | collective-permute-start | bytes 98312 | tf_op jit(solution)/shard_map/ppermute | solution.py:17
  18.7 0.9 copy-start.9
  20.0 0.7 copy-start.11
  21.3 0.8 copy-start.2
  22.1 10.0 %collective-permute-start.2 = (bf16[2,2,16,16,256]{4,2,3,1,0:T(8,128)(2,1)S(1)}, bf16[2,2,16,16,256]{4,2,3,1,0:T(8,128)(2,1)}, u32[]{:S(2)}, u32[]{:S(2)}) collective-permute-start(bf16[2,2,16,16,256]{4,2,3,1,0:T(8,128)(2,1)S(1)} %fusion.180), channel_id=1, source_target_pairs={{0,256},{32,288},{64,320},{96,352},{128,384},{160,416},{192,448},{... | collective-permute-start | bytes 1572872 | tf_op jit(solution)/shard_map/ppermute | solution.py:36
  33.4 26.9 %copy-start.12 = (f32[128]{0:T(128)S(1)}, f32[128]{0:T(128)}, u32[]{:S(2)}) copy-start(f32[128]{0:T(128)} %param.16) | copy-start | bytes 1540
  33.4 41.0 %copy-start.8 = (f32[4,64]{1,0:T(4,128)S(1)}, f32[4,64]{1,0:T(4,128)}, u32[]{:S(2)}) copy-start(f32[4,64]{1,0:T(4,128)} %param.21) | copy-start | bytes 3076
  33.4 11.7 %collective-permute-start.3 = (bf16[2,16,16,256]{3,1,2,0:T(8,128)(2,1)S(1)}, bf16[2,16,16,256]{3,1,2,0:T(8,128)(2,1)S(1)}, u32[]{:S(2)}, u32[]{:S(2)}) collective-permute-start(bf16[2,16,16,256]{3,1,2,0:T(8,128)(2,1)S(1)} %fusion.205), channel_id=1, source_target_pairs={{0,64},{32,96},{64,0},{96,32},{128,192},{160,224},{192,128},{224,1... | collective-permute-start | bytes 786440 | tf_op jit(solution)/shard_map/ppermute | solution.py:36
  45.3 13.1 %collective-permute-start.4 = (bf16[16,16,256]{2,0,1:T(8,128)(2,1)S(1)}, bf16[16,16,256]{2,0,1:T(8,128)(2,1)S(1)}, u32[]{:S(2)}, u32[]{:S(2)}) collective-permute-start(bf16[16,16,256]{2,0,1:T(8,128)(2,1)S(1)} %fusion.207), channel_id=1, source_target_pairs={{0,128},{32,160},{64,192},{96,224},{128,0},{160,32},{192,64},{224,... | collective-permute-start | bytes 393224 | tf_op jit(solution)/shard_map/ppermute | solution.py:36
  58.4 5.7 %collective-permute-start.5 = (bf16[16,16,256]{2,0,1:T(8,128)(2,1)S(1)}, bf16[16,16,256]{2,0,1:T(8,128)(2,1)S(1)}, u32[]{:S(2)}, u32[]{:S(2)}) collective-permute-start(bf16[16,16,256]{2,0,1:T(8,128)(2,1)S(1)} %fusion.206), channel_id=1, source_target_pairs={{0,32},{32,0},{64,96},{96,64},{128,160},{160,128},{192,224},{224,1... | collective-permute-start | bytes 393224 | tf_op jit(solution)/shard_map/ppermute | solution.py:41
  64.2 10.3 %collective-permute-start.6 = (bf16[16,5,256]{2,0,1:T(8,128)(2,1)S(1)}, bf16[16,5,256]{2,0,1:T(8,128)(2,1)S(1)}, u32[]{:S(2)}, u32[]{:S(2)}) collective-permute-start(bf16[16,5,256]{2,0,1:T(8,128)(2,1)S(1)} %get-tuple-element.222), channel_id=1, source_target_pairs={{0,1},{1,2},{2,3},{3,4},{4,5},{5,6},{6,7},{7,8},{8,9},{9,10},{10,1... | collective-permute-start | bytes 122888 | tf_op jit(solution)/shard_map/ppermute | solution.py:14
  72.3 9.5 %collective-permute-start.7 = (bf16[16,5,256]{2,0,1:T(8,128)(2,1)S(1)}, bf16[16,5,256]{2,0,1:T(8,128)(2,1)S(1)}, u32[]{:S(2)}, u32[]{:S(2)}) collective-permute-start(bf16[16,5,256]{2,0,1:T(8,128)(2,1)S(1)} %get-tuple-element.223), channel_id=1, source_target_pairs={{1,0},{2,1},{3,2},{4,3},{5,4},{6,5},{7,6},{8,7},{9,8},{10,9},{11,1... | collective-permute-start | bytes 122888 | tf_op jit(solution)/shard_map/ppermute | solution.py:17
  84.2 0.9 copy-start.6
  87.1 0.9 copy-start.5
  96.5 1.0 copy-start.4
  101.7 0.8 copy-start.7
  104.2 1.0 copy-start.3
  106.0 4.3 %collective-permute-start.8 = (bf16[1,64,1,256]{3,1,2,0:T(8,128)(2,1)S(1)}, bf16[1,64,1,256]{3,1,2,0:T(8,128)(2,1)S(1)}, u32[]{:S(2)}, u32[]{:S(2)}) collective-permute-start(bf16[1,64,1,256]{3,1,2,0:T(8,128)(2,1)S(1)} %get-tuple-element.19), channel_id=1, source_target_pairs={{0,1},{1,2},{2,3},{3,4},{4,5},{5,6},{6,7},{7,8},{8,9},{9,10},{10,1... | collective-permute-start | bytes 98312 | tf_op jit(solution)/shard_map/ppermute | solution.py:14
  107.9 9.5 %collective-permute-start.9 = (bf16[1,64,1,256]{3,1,2,0:T(8,128)(2,1)S(1)}, bf16[1,64,1,256]{3,1,2,0:T(8,128)(2,1)S(1)}, u32[]{:S(2)}, u32[]{:S(2)}) collective-permute-start(bf16[1,64,1,256]{3,1,2,0:T(8,128)(2,1)S(1)} %get-tuple-element.20), channel_id=1, source_target_pairs={{1,0},{2,1},{3,2},{4,3},{5,4},{6,5},{7,6},{8,7},{9,8},{10,9},{11,1... | collective-permute-start | bytes 98312 | tf_op jit(solution)/shard_map/ppermute | solution.py:17
  118.6 0.9 copy-start.10
  119.9 0.7 copy-start.13
  120.6 1.7 %copy-start.1 = (bf16[128,1024]{1,0:T(8,128)(2,1)S(1)}, bf16[128,1024]{1,0:T(8,128)(2,1)}, u32[]{:S(2)}) copy-start(bf16[128,1024]{1,0:T(8,128)(2,1)} %param.15) | copy-start | bytes 786436

commit v2 on v0

--- a/solution.py
+++ b/solution.py
@@ -17,6 +17,22 @@
         high = lax.ppermute(lax.slice_in_dim(block, 0, width, axis=dim), axis, backward)
         block = jnp.concatenate([low, block, high], axis=dim)
     return block
+
+
+def project(encoded, mix_w, mix_b, frames, group_width):
+    channels, row_count, col_count = encoded.shape
+    rows = row_count // frames
+    blocks = encoded.reshape(channels, frames, rows, col_count).transpose(1, 0, 2, 3)
+    stacked = lax.all_to_all(blocks, "frame", 0, 0, tiled=False)
+    stacked = stacked.reshape(frames * channels, rows, col_count)
+    hidden = (
+        jnp.einsum("ji,irw->jrw", mix_w, stacked, preferred_element_type=jnp.float32)
+        + mix_b[:, None, None]
+    ).astype(jnp.bfloat16)
+    hidden = hidden.reshape(GROUPS, group_width, rows, col_count)
+    hidden = jnp.repeat(hidden, frames // GROUPS, axis=0)
+    own = lax.all_to_all(hidden, "frame", 0, 0, tiled=False)
+    return own.transpose(1, 0, 2, 3).reshape(group_width, row_count, col_count)
 
 
 def sweep(padded, weight, kernel_size, start, row_count, col_count):
@@ -62,21 +78,10 @@
     padded = padded_2(features, (("space", 2),), 1)
     encoded = finish(padded, enc_w, enc_b, row_count, col_count)
     hidden_count = mix_w.shape[0]
-    frame_weight = lax.dynamic_slice_in_dim(mix_w, frame_index * channels, channels, 1)
-    partial_mix = jnp.einsum(
-        "ji,irw->jrw", frame_weight, encoded[0], preferred_element_type=jnp.float32
-    )
-    mixed_hidden = (
-        lax.psum(partial_mix.astype(jnp.bfloat16), "frame").astype(jnp.float32)
-        + mix_b[:, None, None]
-    ).astype(jnp.bfloat16)
     per_group = frames * channels // GROUPS
     group_width = hidden_count // GROUPS
     local_groups = max(1, channels // per_group)
-    first_group = frame_index * channels // per_group
-    own_groups = lax.dynamic_slice_in_dim(
-        mixed_hidden, first_group * group_width, local_groups * group_width, 0
-    )
+    own_groups = project(encoded[0], mix_w, mix_b, frames, group_width)
     margin = padded_2(own_groups, (("space", 1),), 5)
     margin = jnp.pad(margin, ((0, 0), (0, 0), (5, 5)))
     group_block = margin.reshape(local_groups, group_width, row_count + 10, col_count + 10)

time: 234 us -> 104 us (0.44)
  the two profiles are of different devices: /device:TPU:135 before, /device:TPU:256 now
where the time goes in v2:
time: 104 us
  blocking collectives  34.4 us (33%)
  starting transfers between devices  19.2 us (18%)
  local copies, waits for them, and re-layouts  17 us (16%)
  waiting for transfers between devices  16 us (15%)
  matrix products  14.3 us (14%)
  other arithmetic  1.75 us (2%)
    all_to_all x1, blocking collectives, project(): stacked = lax.all_to_all(blocks, 'frame', 0, 0, tiled=False)  21.3 us
    ppermute x3, waiting for transfers between devices, padded_2(): lax.ppermute(lax.slice_in_dim(block, block.shape[dim] - width, None, axis...  14.4 us
    dot_general x32, matrix products, sweep(): jnp.einsum('dgoi,gidrw->gorw', weight[row_tap], window, preferred_element...  14.1 us
    unnamed x81, local copies, waits for them, and re-layouts  13.6 us
    all_to_all x1, blocking collectives, project(): own = lax.all_to_all(hidden, 'frame', 0, 0, tiled=False)  13.1 us
    ppermute x3, starting transfers between devices, padded_2(): lax.ppermute(lax.slice_in_dim(block, 0, width, axis=dim), axis, backward)  12.8 us
    ppermute x3, starting transfers between devices, padded_2(): lax.ppermute(lax.slice_in_dim(block, block.shape[dim] - width, None, axis...  6.43 us
    another operation x7, local copies, waits for them, and re-layouts, sweep(): jnp.stack([lax.slice_in_dim(band, start + col_tap, start + col_tap + col_...  2.28 us
  transfers between devices with their start and end apart: 6, of which 3 were waited for; matrix products, arithmetic and copies ran while one was open for 0% of the time, Pallas kernels for 0%

profile of v2, /device:TPU:256, one launch (start us, length us, event | category | flops | bytes accessed | tf_op | source)
XLA Modules:
  0.0 103.5 jit_solution(16191054660468351811)
XLA Ops:
  0.0 1.2 %copy.178 = bf16[1,64,16,256]{3,1,2,0:T(8,128)(2,1)S(1)} copy(bf16[1,64,16,256]{3,2,1,0:T(8,128)(2,1)} %param.12) | data formatting | bytes 1048576 | tf_op args[0]
  1.3 1.9 %collective-permute-start = (bf16[1,64,1,256]{3,1,2,0:T(8,128)(2,1)S(1)}, bf16[1,64,1,256]{3,1,2,0:T(8,128)(2,1)S(1)}, u32[]{:S(2)}, u32[]{:S(2)}) collective-permute-start(bf16[1,64,1,256]{3,1,2,0:T(8,128)(2,1)S(1)} %get-tuple-element.25), channel_id=1, source_target_pairs={{0,1},{1,2},{2,3},{3,4},{4,5},{5,6},{6,7},{7,8},{8,9},{9,10},{10,1... | collective-permute-start | bytes 98312 | tf_op jit(solution)/shard_map/ppermute | solution.py:14
  3.2 7.9 %collective-permute-start.1 = (bf16[1,64,1,256]{3,1,2,0:T(8,128)(2,1)S(1)}, bf16[1,64,1,256]{3,1,2,0:T(8,128)(2,1)S(1)}, u32[]{:S(2)}, u32[]{:S(2)}) collective-permute-start(bf16[1,64,1,256]{3,1,2,0:T(8,128)(2,1)S(1)} %get-tuple-element.26), channel_id=1, source_target_pairs={{1,0},{2,1},{3,2},{4,3},{5,4},{6,5},{7,6},{8,7},{9,8},{10,9},{11,1... | collective-permute-start | bytes 98312 | tf_op jit(solution)/shard_map/ppermute | solution.py:17
  11.1 1.6 %collective-permute-done.1 = bf16[1,64,1,256]{3,1,2,0:T(8,128)(2,1)S(1)} collective-permute-done((bf16[1,64,1,256]{3,1,2,0:T(8,128)(2,1)S(1)}, bf16[1,64,1,256]{3,1,2,0:T(8,128)(2,1)S(1)}, u32[]{:S(2)}, u32[]{:S(2)}) %collective-permute-start.1) | collective-permute-done | bytes 32800 | tf_op jit(solution)/shard_map/ppermute | solution.py:17
  12.6 0.5 fusion.173
  13.1 0.6 fusion.184
  13.7 0.3 copy-done.8
  14.0 0.5 fusion.56
  14.5 0.5 fusion.57
  15.1 0.6 multiply_convert_fusion.1
  15.7 21.3 %all_to_all.10 = bf16[16,64,1,256]{3,1,2,0:T(8,128)(2,1)S(1)} all-to-all(bf16[16,64,1,256]{3,1,2,0:T(8,128)(2,1)S(1)} %bitcast.1275), channel_id=1, replica_groups=mesh['frame'=16,'space'=32] {'frame'}, dimensions={0} | all-to-all | bytes 1048576 | tf_op jit(solution)/shard_map/all_to_all | solution.py:26
  37.0 0.2 fusion.161
  37.3 13.1 %all_to_all.11 = bf16[16,16,1,256]{3,1,2,0:T(8,128)(2,1)S(1)} all-to-all(bf16[16,16,1,256]{3,1,2,0:T(8,128)(2,1)S(1)} %bitcast.1279), channel_id=1, replica_groups=mesh['frame'=16,'space'=32] {'frame'}, dimensions={0} | all-to-all | bytes 262144 | tf_op jit(solution)/shard_map/all_to_all | solution.py:34
  50.4 3.0 %collective-permute-start.3 = (bf16[16,5,256]{2,0,1:T(8,128)(2,1)S(1)}, bf16[16,5,256]{2,0,1:T(8,128)(2,1)S(1)}, u32[]{:S(2)}, u32[]{:S(2)}) collective-permute-start(bf16[16,5,256]{2,0,1:T(8,128)(2,1)S(1)} %get-tuple-element.211), channel_id=1, source_target_pairs={{1,0},{2,1},{3,2},{4,3},{5,4},{6,5},{7,6},{8,7},{9,8},{10,9},{11,1... | collective-permute-start | bytes 122888 | tf_op jit(solution)/shard_map/ppermute | solution.py:17
  53.4 2.1 %collective-permute-start.2 = (bf16[16,5,256]{2,0,1:T(8,128)(2,1)S(1)}, bf16[16,5,256]{2,0,1:T(8,128)(2,1)S(1)}, u32[]{:S(2)}, u32[]{:S(2)}) collective-permute-start(bf16[16,5,256]{2,0,1:T(8,128)(2,1)S(1)} %get-tuple-element.210), channel_id=1, source_target_pairs={{0,1},{1,2},{2,3},{3,4},{4,5},{5,6},{6,7},{7,8},{8,9},{9,10},{10,1... | collective-permute-start | bytes 122888 | tf_op jit(solution)/shard_map/ppermute | solution.py:14
  55.5 7.4 %collective-permute-done.2 = bf16[16,5,256]{2,0,1:T(8,128)(2,1)S(1)} collective-permute-done((bf16[16,5,256]{2,0,1:T(8,128)(2,1)S(1)}, bf16[16,5,256]{2,0,1:T(8,128)(2,1)S(1)}, u32[]{:S(2)}, u32[]{:S(2)}) %collective-permute-start.2) | collective-permute-done | bytes 40992 | tf_op jit(solution)/shard_map/ppermute | solution.py:14
  63.2 0.3 slice_bitcast_fusion.126
  64.3 0.3 constant_dynamic-update-slice_fusion.9
  65.1 0.4 constant_dynamic-update-slice_fusion.5
  66.4 0.5 constant_dynamic-update-slice_fusion.4
  67.9 0.4 constant_dynamic-update-slice_fusion.3
  68.3 0.4 constant_dynamic-update-slice_fusion.2
  70.6 0.4 constant_dynamic-update-slice_fusion.1
  71.0 0.4 constant_dynamic-update-slice_fusion
  74.5 0.3 copy-done.3
  74.8 0.3 convolution_bitcast_fusion.3
  75.2 0.3 convolution_bitcast_fusion.4
  75.5 0.3 convolution_bitcast_fusion.5
  75.9 0.3 convolution_bitcast_fusion.6
  76.2 0.3 convolution_bitcast_fusion.7
  76.6 0.3 convolution_bitcast_fusion.8
  76.9 0.5 copy-done.4
  77.5 0.3 convolution_bitcast_fusion.10
  77.8 0.3 convolution_bitcast_fusion.11
  78.2 0.3 convolution_bitcast_fusion.12
  78.5 0.3 convolution_bitcast_fusion.13
  78.9 0.3 copy-done.2
  79.2 0.6 fusion.59
  79.8 0.4 fusion.157
  80.3 0.4 fusion.154
  80.7 0.4 fusion.151
  81.2 0.4 fusion.148
  81.6 0.4 fusion.145
  82.1 0.4 fusion.142
  82.5 0.4 fusion.139
  83.0 0.4 fusion.136
  83.4 0.4 fusion.133
  83.9 0.5 compare_select_fusion
  84.3 0.3 copy-done.5
  84.6 0.3 convolution_bitcast_fusion
  85.0 0.3 convolution_bitcast_fusion.1
  85.3 0.5 compare_select_fusion.2
  85.8 0.7 compare_select_fusion.1
  86.5 0.7 fusion.160
  87.2 1.9 %collective-permute-start.5 = (bf16[1,64,1,256]{3,1,2,0:T(8,128)(2,1)S(1)}, bf16[1,64,1,256]{3,1,2,0:T(8,128)(2,1)S(1)}, u32[]{:S(2)}, u32[]{:S(2)}) collective-permute-start(bf16[1,64,1,256]{3,1,2,0:T(8,128)(2,1)S(1)} %get-tuple-element.20), channel_id=1, source_target_pairs={{1,0},{2,1},{3,2},{4,3},{5,4},{6,5},{7,6},{8,7},{9,8},{10,9},{11,1... | collective-permute-start | bytes 98312 | tf_op jit(solution)/shard_map/ppermute | solution.py:17
  89.2 2.4 %collective-permute-start.4 = (bf16[1,64,1,256]{3,1,2,0:T(8,128)(2,1)S(1)}, bf16[1,64,1,256]{3,1,2,0:T(8,128)(2,1)S(1)}, u32[]{:S(2)}, u32[]{:S(2)}) collective-permute-start(bf16[1,64,1,256]{3,1,2,0:T(8,128)(2,1)S(1)} %get-tuple-element.19), channel_id=1, source_target_pairs={{0,1},{1,2},{2,3},{3,4},{4,5},{5,6},{6,7},{7,8},{8,9},{9,10},{10,1... | collective-permute-start | bytes 98312 | tf_op jit(solution)/shard_map/ppermute | solution.py:14
  91.6 7.0 %collective-permute-done.4 = bf16[1,64,1,256]{3,1,2,0:T(8,128)(2,1)S(1)} collective-permute-done((bf16[1,64,1,256]{3,1,2,0:T(8,128)(2,1)S(1)}, bf16[1,64,1,256]{3,1,2,0:T(8,128)(2,1)S(1)}, u32[]{:S(2)}, u32[]{:S(2)}) %collective-permute-start.4) | collective-permute-done | bytes 32800 | tf_op jit(solution)/shard_map/ppermute | solution.py:14
  98.6 0.5 select_maximum_fusion
  99.1 0.7 slice_bitcast_fusion.5
  99.9 0.8 copy-done.9
  100.7 0.5 fusion.53
  101.2 0.5 fusion.54
  101.8 0.6 fusion.174
  102.4 1.1 %copy.114 = bf16[1,64,16,256]{3,2,1,0:T(8,128)(2,1)} copy(bf16[1,64,16,256]{3,1,2,0:T(8,128)(2,1)S(1)} %fusion.174) | data formatting | bytes 1048576 | tf_op jit(solution)/shard_map/convert_element_type | solution.py:58
  (82 shorter events, 8.6 us)
Async XLA Ops:
  0.0 37.0 %copy-start = (bf16[128,1024]{1,0:T(8,128)(2,1)S(1)}, bf16[128,1024]{1,0:T(8,128)(2,1)}, u32[]{:S(2)}) copy-start(bf16[128,1024]{1,0:T(8,128)(2,1)} %param.15) | copy-start | bytes 786436
  1.3 9.8 %collective-permute-start = (bf16[1,64,1,256]{3,1,2,0:T(8,128)(2,1)S(1)}, bf16[1,64,1,256]{3,1,2,0:T(8,128)(2,1)S(1)}, u32[]{:S(2)}, u32[]{:S(2)}) collective-permute-start(bf16[1,64,1,256]{3,1,2,0:T(8,128)(2,1)S(1)} %get-tuple-element.25), channel_id=1, source_target_pairs={{0,1},{1,2},{2,3},{3,4},{4,5},{5,6},{6,7},{7,8},{8,9},{9,10},{10,1... | collective-permute-start | bytes 98312 | tf_op jit(solution)/shard_map/ppermute | solution.py:14
  3.2 9.4 %collective-permute-start.1 = (bf16[1,64,1,256]{3,1,2,0:T(8,128)(2,1)S(1)}, bf16[1,64,1,256]{3,1,2,0:T(8,128)(2,1)S(1)}, u32[]{:S(2)}, u32[]{:S(2)}) collective-permute-start(bf16[1,64,1,256]{3,1,2,0:T(8,128)(2,1)S(1)} %get-tuple-element.26), channel_id=1, source_target_pairs={{1,0},{2,1},{3,2},{4,3},{5,4},{6,5},{7,6},{8,7},{9,8},{10,9},{11,1... | collective-permute-start | bytes 98312 | tf_op jit(solution)/shard_map/ppermute | solution.py:17
  13.1 0.9 copy-start.8
  14.5 0.7 copy-start.10
  15.1 21.9 %copy-start.7 = (f32[128]{0:T(128)S(1)}, f32[128]{0:T(128)}, u32[]{:S(2)}) copy-start(f32[128]{0:T(128)} %param.16) | copy-start | bytes 1540
  15.7 39.8 %copy-start.6 = (f32[4,64]{1,0:T(4,128)S(1)}, f32[4,64]{1,0:T(4,128)}, u32[]{:S(2)}) copy-start(f32[4,64]{1,0:T(4,128)} %param.21) | copy-start | bytes 3076
  50.4 5.1 %collective-permute-start.3 = (bf16[16,5,256]{2,0,1:T(8,128)(2,1)S(1)}, bf16[16,5,256]{2,0,1:T(8,128)(2,1)S(1)}, u32[]{:S(2)}, u32[]{:S(2)}) collective-permute-start(bf16[16,5,256]{2,0,1:T(8,128)(2,1)S(1)} %get-tuple-element.211), channel_id=1, source_target_pairs={{1,0},{2,1},{3,2},{4,3},{5,4},{6,5},{7,6},{8,7},{9,8},{10,9},{11,1... | collective-permute-start | bytes 122888 | tf_op jit(solution)/shard_map/ppermute | solution.py:17
  53.4 9.5 %collective-permute-start.2 = (bf16[16,5,256]{2,0,1:T(8,128)(2,1)S(1)}, bf16[16,5,256]{2,0,1:T(8,128)(2,1)S(1)}, u32[]{:S(2)}, u32[]{:S(2)}) collective-permute-start(bf16[16,5,256]{2,0,1:T(8,128)(2,1)S(1)} %get-tuple-element.210), channel_id=1, source_target_pairs={{0,1},{1,2},{2,3},{3,4},{4,5},{5,6},{6,7},{7,8},{8,9},{9,10},{10,1... | collective-permute-start | bytes 122888 | tf_op jit(solution)/shard_map/ppermute | solution.py:14
  73.9 0.9 copy-start.3
  76.6 0.9 copy-start.4
  78.2 1.0 copy-start.2
  83.8 0.8 copy-start.5
  87.2 4.3 %collective-permute-start.5 = (bf16[1,64,1,256]{3,1,2,0:T(8,128)(2,1)S(1)}, bf16[1,64,1,256]{3,1,2,0:T(8,128)(2,1)S(1)}, u32[]{:S(2)}, u32[]{:S(2)}) collective-permute-start(bf16[1,64,1,256]{3,1,2,0:T(8,128)(2,1)S(1)} %get-tuple-element.20), channel_id=1, source_target_pairs={{1,0},{2,1},{3,2},{4,3},{5,4},{6,5},{7,6},{8,7},{9,8},{10,9},{11,1... | collective-permute-start | bytes 98312 | tf_op jit(solution)/shard_map/ppermute | solution.py:17
  89.2 9.5 %collective-permute-start.4 = (bf16[1,64,1,256]{3,1,2,0:T(8,128)(2,1)S(1)}, bf16[1,64,1,256]{3,1,2,0:T(8,128)(2,1)S(1)}, u32[]{:S(2)}, u32[]{:S(2)}) collective-permute-start(bf16[1,64,1,256]{3,1,2,0:T(8,128)(2,1)S(1)} %get-tuple-element.19), channel_id=1, source_target_pairs={{0,1},{1,2},{2,3},{3,4},{4,5},{5,6},{6,7},{7,8},{8,9},{9,10},{10,1... | collective-permute-start | bytes 98312 | tf_op jit(solution)/shard_map/ppermute | solution.py:14
  99.8 0.9 copy-start.9
  101.2 0.7 copy-start.11
  101.8 1.7 %copy-start.1 = (bf16[128,1024]{1,0:T(8,128)(2,1)S(1)}, bf16[128,1024]{1,0:T(8,128)(2,1)}, u32[]{:S(2)}) copy-start(bf16[128,1024]{1,0:T(8,128)(2,1)} %param.15) | copy-start | bytes 786436

commit v3 on v2

--- a/solution.py
+++ b/solution.py
@@ -1,5 +1,8 @@
+import functools
+
 import jax
 import jax.numpy as jnp
+from jax.experimental import pallas as pl
 from jax import lax
 from jax.sharding import PartitionSpec as P
 
@@ -33,6 +36,56 @@
     hidden = jnp.repeat(hidden, frames // GROUPS, axis=0)
     own = lax.all_to_all(hidden, "frame", 0, 0, tiled=False)
     return own.transpose(1, 0, 2, 3).reshape(group_width, row_count, col_count)
+
+
+def branch_kernel(window_ref, weight_ref, bias_ref, out_ref, *, row_count, row_pitch, taps, width):
+    def row(y, carry):
+        acc = jnp.zeros((row_pitch, weight_ref.shape[2]), jnp.float32)
+        for tap in range(taps):
+            start = pl.multiple_of((y + tap) * row_pitch, 16)
+            acc = acc + jnp.dot(
+                window_ref[pl.ds(start, row_pitch), :],
+                weight_ref[tap],
+                preferred_element_type=jnp.float32,
+            )
+        acc = acc + bias_ref[...]
+        acc = jnp.where(acc > 0, acc, 0.2 * acc)
+        total = acc[:, 0:width]
+        for part in range(1, weight_ref.shape[2] // width):
+            total = total + acc[:, part * width : (part + 1) * width]
+        out_ref[pl.ds(pl.multiple_of(y * row_pitch, 16), row_pitch), :] = total
+        return carry
+
+    lax.fori_loop(0, row_count, row, 0)
+
+
+def branches(margin, weights, biases, row_count, col_count):
+    inner = margin.shape[0]
+    taps = max(w.shape[0] for w in weights)
+    half = taps // 2
+    out_width = weights[0].shape[2]
+    row_pitch = -(-(col_count + 2 * half) // 16) * 16
+    padded = jnp.pad(margin, ((0, 0), (0, 0), (half, row_pitch - col_count - half)))
+    flat = padded.transpose(1, 2, 0).reshape(-1, inner)
+    length = flat.shape[0]
+    flat = jnp.pad(flat, ((0, 16), (0, 0)))
+    window = jnp.concatenate([flat[shift : shift + length] for shift in range(taps)], axis=1)
+    stacked = []
+    for w in weights:
+        k = w.shape[0]
+        low = half - k // 2
+        w = jnp.pad(w, ((low, taps - k - low), (low, taps - k - low), (0, 0), (0, 0)))
+        stacked.append(w.transpose(0, 1, 3, 2).reshape(taps, taps * inner, out_width))
+    weight = jnp.concatenate(stacked, axis=2)
+    bias = biases.reshape(1, -1)
+    out = pl.pallas_call(
+        functools.partial(
+            branch_kernel, row_count=row_count, row_pitch=row_pitch, taps=taps, width=out_width
+        ),
+        out_shape=jax.ShapeDtypeStruct((row_count * row_pitch, out_width), jnp.float32),
+    )(window, weight, bias)
+    out = out.reshape(row_count, row_pitch, out_width)[:, :col_count]
+    return out.transpose(2, 0, 1)
 
 
 def sweep(padded, weight, kernel_size, start, row_count, col_count):
@@ -83,19 +136,7 @@
     local_groups = max(1, channels // per_group)
     own_groups = project(encoded[0], mix_w, mix_b, frames, group_width)
     margin = padded_2(own_groups, (("space", 1),), 5)
-    margin = jnp.pad(margin, ((0, 0), (0, 0), (5, 5)))
-    group_block = margin.reshape(local_groups, group_width, row_count + 10, col_count + 10)
-    summed = jnp.zeros((channels, row_count, col_count), jnp.float32)
-    for branch_index, weight in enumerate((branch3, branch5, branch7, branch11)):
-        kernel_size = weight.shape[0]
-        shaped = weight.reshape(
-            kernel_size, kernel_size, local_groups, channels // local_groups, group_width
-        )
-        branch = sweep(group_block, shaped, kernel_size, 5 - kernel_size // 2, row_count, col_count)
-        branch = (
-            branch.reshape(channels, row_count, col_count) + branch_b[branch_index][:, None, None]
-        )
-        summed = summed + jnp.where(branch > 0, branch, 0.2 * branch)
+    summed = branches(margin, (branch3, branch5, branch7, branch11), branch_b, row_count, col_count)
     joined = (summed + encoded[0].astype(jnp.float32)).astype(jnp.bfloat16)[None]
     padded_dec = padded_2(joined, (("space", 2),), 1)
     return finish(padded_dec, dec_w, dec_b, row_count, col_count)

time: 104 us -> 133 us (1.28)
  the two profiles are of different devices: /device:TPU:256 before, /device:TPU:135 now
where the time goes in v3:
time: 133 us; the launch traced here: 132 us
  local copies, waits for them, and re-layouts  37.4 us (28%)
  waiting for transfers between devices  27.5 us (21%)
  starting transfers between devices  26.4 us (20%)
  blocking collectives  18.5 us (14%)
  Pallas kernels  13.8 us (10%)
  other arithmetic  4.64 us (3%)
  matrix products  3.24 us (2%)
    ppermute x3, waiting for transfers between devices, padded_2(): lax.ppermute(lax.slice_in_dim(block, 0, width, axis=dim), axis, backward)  20.3 us
    concatenate x1, local copies, waits for them, and re-layouts, branches(): jnp.concatenate([flat[shift:shift + length] for shift in range(taps)], ax...  19 us
    all_to_all x1, blocking collectives, project(): stacked = lax.all_to_all(blocks, 'frame', 0, 0, tiled=False)  18.5 us
    ppermute x3, starting transfers between devices, padded_2(): lax.ppermute(lax.slice_in_dim(block, block.shape[dim] - width, None, axis...  16.8 us
    pallas_call x1, Pallas kernels, branches(): pl.pallas_call(functools.partial(branch_kernel, row_count=row_count, row_...  13.8 us
    slice x2, local copies, waits for them, and re-layouts, branches(): flat[shift:shift + length]  8.9 us
    all_to_all x1, waiting for transfers between devices, project(): own = lax.all_to_all(hidden, 'frame', 0, 0, tiled=False)  7.15 us
    ppermute x3, starting transfers between devices, padded_2(): lax.ppermute(lax.slice_in_dim(block, 0, width, axis=dim), axis, backward)  5.76 us
  transfers between devices with their start and end apart: 7, of which 4 were waited for; matrix products, arithmetic and copies ran while one was open for 2% of the time, Pallas kernels for 0%

profile of v3, /device:TPU:135, one launch (start us, length us, event | category | flops | bytes accessed | tf_op | source)
XLA Modules:
  0.0 131.7 jit_solution(9345786406792742904)
XLA Ops:
  0.0 0.0 copy-start
  0.0 1.2 copy.58
  1.3 7.5 %collective-permute-start = (bf16[1,64,1,256]{3,1,2,0:T(8,128)(2,1)S(1)}, bf16[1,64,1,256]{3,1,2,0:T(8,128)(2,1)S(1)}, u32[]{:S(2)}, u32[]{:S(2)}) collective-permute-start(bf16[1,64,1,256]{3,1,2,0:T(8,128)(2,1)S(1)} %get-tuple-element.36), channel_id=1, source_target_pairs={{0,1},{1,2},{2,3},{3,4},{4,5},{5,6},{6,7},{7,8},{8,9},{9,10},{10,1... | collective-permute-start | bytes 98312 | tf_op jit(solution)/shard_map/ppermute | solution.py:17
  8.8 1.9 %collective-permute-start.1 = (bf16[1,64,1,256]{3,1,2,0:T(8,128)(2,1)S(1)}, bf16[1,64,1,256]{3,1,2,0:T(8,128)(2,1)S(1)}, u32[]{:S(2)}, u32[]{:S(2)}) collective-permute-start(bf16[1,64,1,256]{3,1,2,0:T(8,128)(2,1)S(1)} %get-tuple-element.37), channel_id=1, source_target_pairs={{1,0},{2,1},{3,2},{4,3},{5,4},{6,5},{7,6},{8,7},{9,8},{10,9},{11,1... | collective-permute-start | bytes 98312 | tf_op jit(solution)/shard_map/ppermute | solution.py:20
  10.7 0.0 collective-permute-done
  10.7 7.5 %collective-permute-done.1 = bf16[1,64,1,256]{3,1,2,0:T(8,128)(2,1)S(1)} collective-permute-done((bf16[1,64,1,256]{3,1,2,0:T(8,128)(2,1)S(1)}, bf16[1,64,1,256]{3,1,2,0:T(8,128)(2,1)S(1)}, u32[]{:S(2)}, u32[]{:S(2)}) %collective-permute-start.1) | collective-permute-done | bytes 32800 | tf_op jit(solution)/shard_map/ppermute | solution.py:20
  18.2 0.5 fusion.51
  18.7 0.0 copy-start.8
  18.7 0.6 fusion.57
  19.3 0.3 copy-done.8
  19.6 0.4 fusion.34
  20.1 0.0 copy-start.10
  20.1 0.4 fusion.35
  20.5 0.2 copy-done.10
  20.7 0.6 multiply_convert_fusion.1
  21.3 0.0 copy-start.1
  21.3 0.0 copy-start.5
  21.3 0.0 copy-start.4
  21.3 0.0 copy-start.3
  21.4 0.7 copy-done.1
  22.1 18.5 %all_to_all.10 = bf16[16,64,1,256]{3,1,2,0:T(8,128)(2,1)S(1)} all-to-all(bf16[16,64,1,256]{3,1,2,0:T(8,128)(2,1)S(1)} %bitcast.218), channel_id=1, replica_groups=mesh['frame'=16,'space'=32] {'frame'}, dimensions={0} | all-to-all | bytes 1048576 | tf_op jit(solution)/shard_map/all_to_all | solution.py:29
  40.6 0.0 copy-done
  40.6 0.0 copy-done.7
  40.6 0.2 fusion.45
  40.9 0.7 broadcast_in_dim.6
  41.5 3.8 %all-to-all-start.1 = ((bf16[16,16,1,256]{3,1,2,0:T(8,128)(2,1)}), bf16[16,16,1,256]{3,1,2,0:T(8,128)(2,1)S(1)}, u32[]{:S(2)}, u32[]{:S(2)}) async-start(bf16[16,16,1,256]{3,1,2,0:T(8,128)(2,1)} %bitcast.32), calls=%async_computation.1 | async-start | bytes 262144 | tf_op jit(solution)/shard_map/all_to_all | solution.py:37
  45.3 0.0 copy-done.5
  45.3 0.1 pad.30
  45.4 0.0 copy-done.4
  45.4 0.1 pad.31
  45.5 0.0 copy-done.3
  45.5 0.0 copy-start.6
  45.5 0.1 pad.32
  45.6 7.2 %all-to-all-done.1 = bf16[16,16,1,256]{3,1,2,0:T(8,128)(2,1)S(1)} async-done(((bf16[16,16,1,256]{3,1,2,0:T(8,128)(2,1)}), bf16[16,16,1,256]{3,1,2,0:T(8,128)(2,1)S(1)}, u32[]{:S(2)}, u32[]{:S(2)}) %all-to-all-start.1) | async-done | bytes 131104 | tf_op jit(solution)/shard_map/all_to_all | solution.py:37
  52.8 6.8 %collective-permute-start.2 = (bf16[16,5,256]{2,0,1:T(8,128)(2,1)S(1)}, bf16[16,5,256]{2,0,1:T(8,128)(2,1)S(1)}, u32[]{:S(2)}, u32[]{:S(2)}) collective-permute-start(bf16[16,5,256]{2,0,1:T(8,128)(2,1)S(1)} %get-tuple-element.38), channel_id=1, source_target_pairs={{0,1},{1,2},{2,3},{3,4},{4,5},{5,6},{6,7},{7,8},{8,9},{9,10},{10,1... | collective-permute-start | bytes 122888 | tf_op jit(solution)/shard_map/ppermute | solution.py:17
  59.5 1.9 %collective-permute-start.3 = (bf16[16,5,256]{2,0,1:T(8,128)(2,1)S(1)}, bf16[16,5,256]{2,0,1:T(8,128)(2,1)S(1)}, u32[]{:S(2)}, u32[]{:S(2)}) collective-permute-start(bf16[16,5,256]{2,0,1:T(8,128)(2,1)S(1)} %get-tuple-element.39), channel_id=1, source_target_pairs={{1,0},{2,1},{3,2},{4,3},{5,4},{6,5},{7,6},{8,7},{9,8},{10,9},{11,1... | collective-permute-start | bytes 122888 | tf_op jit(solution)/shard_map/ppermute | solution.py:20
  61.5 1.6 %pad_maximum_fusion.weight_ref = bf16[11,176,256]{2,1,0:T(8,128)(2,1)} fusion(bf16[11,176,64]{2,1,0:T(8,128)(2,1)S(1)} %bitcast.225, bf16[11,176,64]{2,1,0:T(8,128)(2,1)S(1)} %bitcast.222, bf16[11,176,64]{2,1,0:T(8,128)(2,1)S(1)} %bitcast.221, bf16[11,176,64]{2,1,0:T(8,128)(2,1)S(1)} %bitcast.220), kind=kLoop, calls=%fused_computation.59 | loop fusion | flops 3964928 | bytes 1982464 | tf_op jit(solution)/shard_map/concatenate | solution.py:79
  63.1 0.6 reshape.146.bias_ref
  63.7 0.0 collective-permute-done.2
  63.7 5.3 %collective-permute-done.3 = bf16[16,5,256]{2,0,1:T(8,128)(2,1)S(1)} collective-permute-done((bf16[16,5,256]{2,0,1:T(8,128)(2,1)S(1)}, bf16[16,5,256]{2,0,1:T(8,128)(2,1)S(1)}, u32[]{:S(2)}, u32[]{:S(2)}) %collective-permute-start.3) | collective-permute-done | bytes 40992 | tf_op jit(solution)/shard_map/ppermute | solution.py:20
  69.1 0.2 fusion.63
  69.2 0.9 copy.38
  70.1 7.1 %pad_slice_fusion = (bf16[7072,16]{1,0:T(8,128)(2,1)}, bf16[7072,16]{1,0:T(8,128)(2,1)}, bf16[7072,16]{1,0:T(8,128)(2,1)}, bf16[7072,16]{1,0:T(8,128)(2,1)}, bf1...) fusion(bf16[7072,16]{1,0:T(8,128)(2,1)S(1)} %bitcast.213), kind=kLoop, calls=%fused_computation.118 | loop fusion | bytes 2263040 | tf_op jit(solution)/shard_map/slice | solution.py:72
  77.2 1.8 %pad_slice_fusion.9 = bf16[7072,16]{1,0:T(8,128)(2,1)} fusion(bf16[7072,16]{1,0:T(8,128)(2,1)S(1)} %bitcast.214), kind=kLoop, calls=%fused_computation.127 | loop fusion | bytes 452608 | tf_op jit(solution)/shard_map/slice | solution.py:72
  79.1 19.0 %concatenate.31.window_ref = bf16[7072,176]{1,0:T(8,128)(2,1)} concatenate(bf16[7072,16]{1,0:T(8,128)(2,1)S(1)} %bitcast.215, bf16[7072,16]{1,0:T(8,128)(2,1)} %pad_slice_fusion.9, bf16[7072,16]{1,0:T(8,128)(2,1)} %get-tuple-element.6, bf16[7072,16]{1,0:T(8,128)(2,1)} %get-tuple-element.7, bf16[7072,16]{1,0:T(8,128)(2,1)} %get-tuple-element.8, ...), dimensions={1} | concatenate | bytes 4978688 | tf_op jit(solution)/shard_map/concatenate | solution.py:72
  98.1 13.8 %shard_map.118 = f32[4352,64]{1,0:T(8,128)} custom-call(bf16[7072,176]{1,0:T(8,128)(2,1)} %concatenate.31.window_ref, bf16[11,176,256]{2,1,0:T(8,128)(2,1)} %pad_maximum_fusion.weight_ref, f32[1,256]{1,0:T(1,128)} %reshape.146.bias_ref), custom_call_target="tpu_custom_call" | custom-call | tf_op jit(solution)/shard_map/pallas_call | solution.py:81
  111.9 1.7 %slice.209 = f32[16,256,64]{2,1,0:T(8,128)S(1)} slice(f32[16,272,64]{2,1,0:T(8,128)} %bitcast.216), slice={[0:16], [0:256], [0:64]} | slice | bytes 2097152 | tf_op jit(solution)/shard_map/slice | solution.py:87
  113.6 0.6 copy.55
  114.2 1.2 fusion.82
  115.5 2.5 %collective-permute-start.4 = (bf16[1,64,1,256]{3,1,2,0:T(8,128)(2,1)S(1)}, bf16[1,64,1,256]{3,1,2,0:T(8,128)(2,1)S(1)}, u32[]{:S(2)}, u32[]{:S(2)}) collective-permute-start(bf16[1,64,1,256]{3,1,2,0:T(8,128)(2,1)S(1)} %get-tuple-element.30), channel_id=1, source_target_pairs={{0,1},{1,2},{2,3},{3,4},{4,5},{5,6},{6,7},{7,8},{8,9},{9,10},{10,1... | collective-permute-start | bytes 98312 | tf_op jit(solution)/shard_map/ppermute | solution.py:17
  118.0 1.9 %collective-permute-start.5 = (bf16[1,64,1,256]{3,1,2,0:T(8,128)(2,1)S(1)}, bf16[1,64,1,256]{3,1,2,0:T(8,128)(2,1)S(1)}, u32[]{:S(2)}, u32[]{:S(2)}) collective-permute-start(bf16[1,64,1,256]{3,1,2,0:T(8,128)(2,1)S(1)} %get-tuple-element.31), channel_id=1, source_target_pairs={{1,0},{2,1},{3,2},{4,3},{5,4},{6,5},{7,6},{8,7},{9,8},{10,9},{11,1... | collective-permute-start | bytes 98312 | tf_op jit(solution)/shard_map/ppermute | solution.py:20
  119.9 0.0 collective-permute-done.4
  120.0 7.5 %collective-permute-done.5 = bf16[1,64,1,256]{3,1,2,0:T(8,128)(2,1)S(1)} collective-permute-done((bf16[1,64,1,256]{3,1,2,0:T(8,128)(2,1)S(1)}, bf16[1,64,1,256]{3,1,2,0:T(8,128)(2,1)S(1)}, u32[]{:S(2)}, u32[]{:S(2)}) %collective-permute-start.5) | collective-permute-done | bytes 32800 | tf_op jit(solution)/shard_map/ppermute | solution.py:20
  127.5 0.5 select_maximum_fusion
  127.9 0.0 copy-start.9
  128.0 0.7 slice_bitcast_fusion.5
  128.7 0.2 copy-done.9
  128.9 0.5 fusion.32
  129.3 0.1 fusion.55
  129.4 0.0 copy-start.11
  129.4 0.5 fusion.31
  129.9 0.2 copy-done.11
  130.0 0.6 fusion.52
  130.7 1.1 copy.43
  (7 shorter events, 0.0 us)
Async XLA Ops:
  0.0 40.6 %copy-start = (bf16[128,1024]{1,0:T(8,128)(2,1)S(1)}, bf16[128,1024]{1,0:T(8,128)(2,1)}, u32[]{:S(2)}) copy-start(bf16[128,1024]{1,0:T(8,128)(2,1)} %param.15) | copy-start | bytes 786436
  1.3 9.4 %collective-permute-start = (bf16[1,64,1,256]{3,1,2,0:T(8,128)(2,1)S(1)}, bf16[1,64,1,256]{3,1,2,0:T(8,128)(2,1)S(1)}, u32[]{:S(2)}, u32[]{:S(2)}) collective-permute-start(bf16[1,64,1,256]{3,1,2,0:T(8,128)(2,1)S(1)} %get-tuple-element.36), channel_id=1, source_target_pairs={{0,1},{1,2},{2,3},{3,4},{4,5},{5,6},{6,7},{7,8},{8,9},{9,10},{10,1... | collective-permute-start | bytes 98312 | tf_op jit(solution)/shard_map/ppermute | solution.py:17
  8.8 9.5 %collective-permute-start.1 = (bf16[1,64,1,256]{3,1,2,0:T(8,128)(2,1)S(1)}, bf16[1,64,1,256]{3,1,2,0:T(8,128)(2,1)S(1)}, u32[]{:S(2)}, u32[]{:S(2)}) collective-permute-start(bf16[1,64,1,256]{3,1,2,0:T(8,128)(2,1)S(1)} %get-tuple-element.37), channel_id=1, source_target_pairs={{1,0},{2,1},{3,2},{4,3},{5,4},{6,5},{7,6},{8,7},{9,8},{10,9},{11,1... | collective-permute-start | bytes 98312 | tf_op jit(solution)/shard_map/ppermute | solution.py:20
  18.7 0.9 copy-start.8
  20.1 0.7 copy-start.10
  20.7 19.9 %copy-start.7 = (f32[128]{0:T(128)S(1)}, f32[128]{0:T(128)}, u32[]{:S(2)}) copy-start(f32[128]{0:T(128)} %param.16) | copy-start | bytes 1540
  21.3 0.8 copy-start.1
  21.3 24.0 %copy-start.5 = (bf16[3,3,64,16]{2,3,1,0:T(8,128)(2,1)S(1)}, bf16[3,3,64,16]{2,3,1,0:T(8,128)(2,1)}, u32[]{:S(2)}) copy-start(bf16[3,3,64,16]{2,3,1,0:T(8,128)(2,1)} %param.17) | copy-start | bytes 55300
  21.3 24.1 %copy-start.4 = (bf16[5,5,64,16]{2,3,1,0:T(8,128)(2,1)S(1)}, bf16[5,5,64,16]{2,3,1,0:T(8,128)(2,1)}, u32[]{:S(2)}) copy-start(bf16[5,5,64,16]{2,3,1,0:T(8,128)(2,1)} %param.18) | copy-start | bytes 153604
  21.3 24.1 %copy-start.3 = (bf16[7,7,64,16]{2,3,1,0:T(8,128)(2,1)S(1)}, bf16[7,7,64,16]{2,3,1,0:T(8,128)(2,1)}, u32[]{:S(2)}) copy-start(bf16[7,7,64,16]{2,3,1,0:T(8,128)(2,1)} %param.19) | copy-start | bytes 301060
  40.6 20.9 %copy-start.2 = (bf16[11,11,64,16]{2,3,1,0:T(8,128)(2,1)S(1)}, bf16[11,11,64,16]{2,3,1,0:T(8,128)(2,1)}, u32[]{:S(2)}) copy-start(bf16[11,11,64,16]{2,3,1,0:T(8,128)(2,1)} %param.20) | copy-start | bytes 743428
  41.5 11.2 %all-to-all-start.1 = ((bf16[16,16,1,256]{3,1,2,0:T(8,128)(2,1)}), bf16[16,16,1,256]{3,1,2,0:T(8,128)(2,1)S(1)}, u32[]{:S(2)}, u32[]{:S(2)}) async-start(bf16[16,16,1,256]{3,1,2,0:T(8,128)(2,1)} %bitcast.32), calls=%async_computation.1 | async-start | bytes 262144 | tf_op jit(solution)/shard_map/all_to_all | solution.py:37
  45.5 17.6 %copy-start.6 = (f32[4,64]{1,0:T(4,128)S(1)}, f32[4,64]{1,0:T(4,128)}, u32[]{:S(2)}) copy-start(f32[4,64]{1,0:T(4,128)} %param.21) | copy-start | bytes 3076
  52.8 11.0 %collective-permute-start.2 = (bf16[16,5,256]{2,0,1:T(8,128)(2,1)S(1)}, bf16[16,5,256]{2,0,1:T(8,128)(2,1)S(1)}, u32[]{:S(2)}, u32[]{:S(2)}) collective-permute-start(bf16[16,5,256]{2,0,1:T(8,128)(2,1)S(1)} %get-tuple-element.38), channel_id=1, source_target_pairs={{0,1},{1,2},{2,3},{3,4},{4,5},{5,6},{6,7},{7,8},{8,9},{9,10},{10,1... | collective-permute-start | bytes 122888 | tf_op jit(solution)/shard_map/ppermute | solution.py:17
  59.5 9.6 %collective-permute-start.3 = (bf16[16,5,256]{2,0,1:T(8,128)(2,1)S(1)}, bf16[16,5,256]{2,0,1:T(8,128)(2,1)S(1)}, u32[]{:S(2)}, u32[]{:S(2)}) collective-permute-start(bf16[16,5,256]{2,0,1:T(8,128)(2,1)S(1)} %get-tuple-element.39), channel_id=1, source_target_pairs={{1,0},{2,1},{3,2},{4,3},{5,4},{6,5},{7,6},{8,7},{9,8},{10,9},{11,1... | collective-permute-start | bytes 122888 | tf_op jit(solution)/shard_map/ppermute | solution.py:20
  115.5 4.5 %collective-permute-start.4 = (bf16[1,64,1,256]{3,1,2,0:T(8,128)(2,1)S(1)}, bf16[1,64,1,256]{3,1,2,0:T(8,128)(2,1)S(1)}, u32[]{:S(2)}, u32[]{:S(2)}) collective-permute-start(bf16[1,64,1,256]{3,1,2,0:T(8,128)(2,1)S(1)} %get-tuple-element.30), channel_id=1, source_target_pairs={{0,1},{1,2},{2,3},{3,4},{4,5},{5,6},{6,7},{7,8},{8,9},{9,10},{10,1... | collective-permute-start | bytes 98312 | tf_op jit(solution)/shard_map/ppermute | solution.py:17
  118.0 9.5 %collective-permute-start.5 = (bf16[1,64,1,256]{3,1,2,0:T(8,128)(2,1)S(1)}, bf16[1,64,1,256]{3,1,2,0:T(8,128)(2,1)S(1)}, u32[]{:S(2)}, u32[]{:S(2)}) collective-permute-start(bf16[1,64,1,256]{3,1,2,0:T(8,128)(2,1)S(1)} %get-tuple-element.31), channel_id=1, source_target_pairs={{1,0},{2,1},{3,2},{4,3},{5,4},{6,5},{7,6},{8,7},{9,8},{10,9},{11,1... | collective-permute-start | bytes 98312 | tf_op jit(solution)/shard_map/ppermute | solution.py:20
  127.9 0.9 copy-start.9
  129.4 0.7 copy-start.11

commit v4 on v2

--- a/solution.py
+++ b/solution.py
@@ -33,6 +33,27 @@
     hidden = jnp.repeat(hidden, frames // GROUPS, axis=0)
     own = lax.all_to_all(hidden, "frame", 0, 0, tiled=False)
     return own.transpose(1, 0, 2, 3).reshape(group_width, row_count, col_count)
+
+
+def branches(margin, weights, biases, row_count, col_count):
+    half = max(w.shape[0] for w in weights) // 2
+    shifted = jnp.stack(
+        [lax.slice_in_dim(margin, b, b + col_count, axis=2) for b in range(2 * half + 1)]
+    )
+    summed = jnp.zeros((weights[0].shape[2], row_count, col_count), jnp.float32)
+    for index, weight in enumerate(weights):
+        k = weight.shape[0]
+        low = half - k // 2
+        acc = jnp.zeros_like(summed)
+        for a in range(k):
+            window = lax.slice_in_dim(shifted, low, low + k, axis=0)
+            window = lax.slice_in_dim(window, low + a, low + a + row_count, axis=2)
+            acc = acc + jnp.einsum(
+                "doi,dirw->orw", weight[a], window, preferred_element_type=jnp.float32
+            )
+        acc = acc + biases[index][:, None, None]
+        summed = summed + jnp.where(acc > 0, acc, 0.2 * acc)
+    return summed
 
 
 def sweep(padded, weight, kernel_size, start, row_count, col_count):
@@ -84,18 +105,7 @@
     own_groups = project(encoded[0], mix_w, mix_b, frames, group_width)
     margin = padded_2(own_groups, (("space", 1),), 5)
     margin = jnp.pad(margin, ((0, 0), (0, 0), (5, 5)))
-    group_block = margin.reshape(local_groups, group_width, row_count + 10, col_count + 10)
-    summed = jnp.zeros((channels, row_count, col_count), jnp.float32)
-    for branch_index, weight in enumerate((branch3, branch5, branch7, branch11)):
-        kernel_size = weight.shape[0]
-        shaped = weight.reshape(
-            kernel_size, kernel_size, local_groups, channels // local_groups, group_width
-        )
-        branch = sweep(group_block, shaped, kernel_size, 5 - kernel_size // 2, row_count, col_count)
-        branch = (
-            branch.reshape(channels, row_count, col_count) + branch_b[branch_index][:, None, None]
-        )
-        summed = summed + jnp.where(branch > 0, branch, 0.2 * branch)
+    summed = branches(margin, (branch3, branch5, branch7, branch11), branch_b, row_count, col_count)
     joined = (summed + encoded[0].astype(jnp.float32)).astype(jnp.bfloat16)[None]
     padded_dec = padded_2(joined, (("space", 2),), 1)
     return finish(padded_dec, dec_w, dec_b, row_count, col_count)

time: 104 us -> 94.9 us (0.913)
  local copies, waits for them, and re-layouts: 17 us -> 7.84 us
    dot_general x0 -> x26, matrix products: none -> 11.5 us  [branches(): jnp.einsum('doi,dirw->orw', weight[a], window, preferred_element_type=jnp...]
    dot_general x32 -> x6, matrix products: 14.1 us -> 2.98 us  [sweep(): jnp.einsum('dgoi,gidrw->gorw', weight[row_tap], window, preferred_element...]
    unnamed x81 -> x37, local copies, waits for them, and re-layouts: 13.6 us -> 5.38 us
    another operation x7 -> x1, local copies, waits for them, and re-layouts: 2.28 us -> 0.72 us  [sweep(): jnp.stack([lax.slice_in_dim(band, start + col_tap, start + col_tap + col_...]
where the time goes in v4:
time: 94.9 us; the launch traced here: 94.3 us
  blocking collectives  34.4 us (36%)
  starting transfers between devices  19.4 us (20%)
  waiting for transfers between devices  15.8 us (17%)
  matrix products  14.7 us (15%)
  local copies, waits for them, and re-layouts  7.84 us (8%)
  other arithmetic  1.68 us (2%)
    all_to_all x1, blocking collectives, project(): stacked = lax.all_to_all(blocks, 'frame', 0, 0, tiled=False)  21.3 us
    ppermute x3, waiting for transfers between devices, padded_2(): lax.ppermute(lax.slice_in_dim(block, block.shape[dim] - width, None, axis...  14.2 us
    all_to_all x1, blocking collectives, project(): own = lax.all_to_all(hidden, 'frame', 0, 0, tiled=False)  13.1 us
    ppermute x3, starting transfers between devices, padded_2(): lax.ppermute(lax.slice_in_dim(block, 0, width, axis=dim), axis, backward)  12.8 us
    dot_general x26, matrix products, branches(): jnp.einsum('doi,dirw->orw', weight[a], window, preferred_element_type=jnp...  11.5 us
    ppermute x3, starting transfers between devices, padded_2(): lax.ppermute(lax.slice_in_dim(block, block.shape[dim] - width, None, axis...  6.65 us
    unnamed x37, local copies, waits for them, and re-layouts  5.38 us
    dot_general x6, matrix products, sweep(): jnp.einsum('dgoi,gidrw->gorw', weight[row_tap], window, preferred_element...  2.98 us
  transfers between devices with their start and end apart: 6, of which 3 were waited for; matrix products, arithmetic and copies ran while one was open for 0% of the time, Pallas kernels for 0%

profile of v4, /device:TPU:256, one launch (start us, length us, event | category | flops | bytes accessed | tf_op | source)
XLA Modules:
  0.0 94.3 jit_solution(9797879038314955174)
XLA Ops:
  0.0 1.2 %copy.142 = bf16[1,64,16,256]{3,1,2,0:T(8,128)(2,1)S(1)} copy(bf16[1,64,16,256]{3,2,1,0:T(8,128)(2,1)} %param.12) | data formatting | bytes 1048576 | tf_op args[0]
  1.3 1.9 %collective-permute-start = (bf16[1,64,1,256]{3,1,2,0:T(8,128)(2,1)S(1)}, bf16[1,64,1,256]{3,1,2,0:T(8,128)(2,1)S(1)}, u32[]{:S(2)}, u32[]{:S(2)}) collective-permute-start(bf16[1,64,1,256]{3,1,2,0:T(8,128)(2,1)S(1)} %get-tuple-element.25), channel_id=1, source_target_pairs={{0,1},{1,2},{2,3},{3,4},{4,5},{5,6},{6,7},{7,8},{8,9},{9,10},{10,1... | collective-permute-start | bytes 98312 | tf_op jit(solution)/shard_map/ppermute | solution.py:14
  3.2 7.9 %collective-permute-start.1 = (bf16[1,64,1,256]{3,1,2,0:T(8,128)(2,1)S(1)}, bf16[1,64,1,256]{3,1,2,0:T(8,128)(2,1)S(1)}, u32[]{:S(2)}, u32[]{:S(2)}) collective-permute-start(bf16[1,64,1,256]{3,1,2,0:T(8,128)(2,1)S(1)} %get-tuple-element.26), channel_id=1, source_target_pairs={{1,0},{2,1},{3,2},{4,3},{5,4},{6,5},{7,6},{8,7},{9,8},{10,9},{11,1... | collective-permute-start | bytes 98312 | tf_op jit(solution)/shard_map/ppermute | solution.py:17
  11.1 1.6 %collective-permute-done.1 = bf16[1,64,1,256]{3,1,2,0:T(8,128)(2,1)S(1)} collective-permute-done((bf16[1,64,1,256]{3,1,2,0:T(8,128)(2,1)S(1)}, bf16[1,64,1,256]{3,1,2,0:T(8,128)(2,1)S(1)}, u32[]{:S(2)}, u32[]{:S(2)}) %collective-permute-start.1) | collective-permute-done | bytes 32800 | tf_op jit(solution)/shard_map/ppermute | solution.py:17
  12.6 0.5 fusion.85
  13.1 0.6 fusion.90
  13.7 0.3 copy-done.7
  14.0 0.5 fusion.34
  14.5 0.5 fusion.35
  14.9 0.2 copy-done.9
  15.1 0.6 multiply_convert_fusion.1
  15.7 21.3 %all_to_all.10 = bf16[16,64,1,256]{3,1,2,0:T(8,128)(2,1)S(1)} all-to-all(bf16[16,64,1,256]{3,1,2,0:T(8,128)(2,1)S(1)} %bitcast.598), channel_id=1, replica_groups=mesh['frame'=16,'space'=32] {'frame'}, dimensions={0} | all-to-all | bytes 1048576 | tf_op jit(solution)/shard_map/all_to_all | solution.py:26
  37.0 0.2 fusion.80
  37.3 13.1 %all_to_all.11 = bf16[16,16,1,256]{3,1,2,0:T(8,128)(2,1)S(1)} all-to-all(bf16[16,16,1,256]{3,1,2,0:T(8,128)(2,1)S(1)} %bitcast.600), channel_id=1, replica_groups=mesh['frame'=16,'space'=32] {'frame'}, dimensions={0} | all-to-all | bytes 262144 | tf_op jit(solution)/shard_map/all_to_all | solution.py:34
  50.4 3.0 %collective-permute-start.3 = (bf16[16,5,256]{2,0,1:T(8,128)(2,1)S(1)}, bf16[16,5,256]{2,0,1:T(8,128)(2,1)S(1)}, u32[]{:S(2)}, u32[]{:S(2)}) collective-permute-start(bf16[16,5,256]{2,0,1:T(8,128)(2,1)S(1)} %get-tuple-element.38), channel_id=1, source_target_pairs={{1,0},{2,1},{3,2},{4,3},{5,4},{6,5},{7,6},{8,7},{9,8},{10,9},{11,1... | collective-permute-start | bytes 122888 | tf_op jit(solution)/shard_map/ppermute | solution.py:17
  53.4 2.1 %collective-permute-start.2 = (bf16[16,5,256]{2,0,1:T(8,128)(2,1)S(1)}, bf16[16,5,256]{2,0,1:T(8,128)(2,1)S(1)}, u32[]{:S(2)}, u32[]{:S(2)}) collective-permute-start(bf16[16,5,256]{2,0,1:T(8,128)(2,1)S(1)} %get-tuple-element.37), channel_id=1, source_target_pairs={{0,1},{1,2},{2,3},{3,4},{4,5},{5,6},{6,7},{7,8},{8,9},{9,10},{10,1... | collective-permute-start | bytes 122888 | tf_op jit(solution)/shard_map/ppermute | solution.py:14
  55.5 7.4 %collective-permute-done.2 = bf16[16,5,256]{2,0,1:T(8,128)(2,1)S(1)} collective-permute-done((bf16[16,5,256]{2,0,1:T(8,128)(2,1)S(1)}, bf16[16,5,256]{2,0,1:T(8,128)(2,1)S(1)}, u32[]{:S(2)}, u32[]{:S(2)}) %collective-permute-start.2) | collective-permute-done | bytes 40992 | tf_op jit(solution)/shard_map/ppermute | solution.py:14
  63.1 0.1 fusion.94
  63.4 0.1 bitcast_dynamic-update-slice_fusion.2
  64.1 0.1 fusion.96
  64.3 0.2 copy-done.1
  64.5 0.4 convolution_bitcast_fusion.15
  65.0 0.4 convolution_bitcast_fusion.16
  65.4 0.4 convolution_bitcast_fusion.17
  65.8 0.4 convolution_bitcast_fusion.18
  66.2 0.4 convolution_bitcast_fusion.19
  66.7 0.4 convolution_bitcast_fusion.20
  67.1 0.4 convolution_bitcast_fusion.21
  67.5 0.4 convolution_bitcast_fusion.22
  67.9 0.4 convolution_bitcast_fusion.23
  68.4 0.4 convolution_bitcast_fusion.24
  68.9 0.2 bitcast_dynamic-update-slice_fusion.14
  69.2 0.2 bitcast_dynamic-update-slice_fusion.5
  69.6 0.2 bitcast_dynamic-update-slice_fusion.9
  70.1 0.3 convolution_bitcast_fusion.3
  70.4 0.3 convolution_bitcast_fusion.4
  70.8 0.3 convolution_bitcast_fusion.5
  71.1 0.3 convolution_bitcast_fusion.6
  71.5 0.3 convolution_bitcast_fusion.7
  71.8 0.3 convolution_bitcast_fusion.8
  72.2 0.2 copy-done.3
  72.4 0.3 convolution_bitcast_fusion.10
  72.7 0.3 convolution_bitcast_fusion.11
  73.1 0.3 convolution_bitcast_fusion.12
  73.4 0.3 convolution_bitcast_fusion.13
  73.8 0.2 fusion.99
  74.0 0.2 copy-done.4
  74.2 0.3 convolution_bitcast_fusion
  74.6 0.3 convolution_bitcast_fusion.1
  74.9 0.6 compare_select_fusion.2
  75.5 0.9 compare_select_fusion.1
  76.3 1.0 %compare_select_fusion = f32[64,16,256]{2,0,1:T(8,128)S(1)} fusion(f32[16,256,64]{1,2,0:T(8,128)S(1)} %convolution_bitcast_fusion.15, f32[16,256,64]{1,2,0:T(8,128)S(1)} %convolution_bitcast_fusion.16, f32[16,256,64]{1,2,0:T(8,128)S(1)} %convolution_bitcast_fusion.17, f32[16,256,64]{1,2,0:T(8,128)S(1)} %convolution_bitcast_fusion.18, ...), kind=kOutput, calls=%fused_computation | convolution fusion | flops 95944704 | bytes 13922816 | tf_op jit(solution)/shard_map/doi,dirw->orw/dot_general | solution.py:51
  77.4 0.7 fusion.79
  78.1 1.9 %collective-permute-start.5 = (bf16[1,64,1,256]{3,1,2,0:T(8,128)(2,1)S(1)}, bf16[1,64,1,256]{3,1,2,0:T(8,128)(2,1)S(1)}, u32[]{:S(2)}, u32[]{:S(2)}) collective-permute-start(bf16[1,64,1,256]{3,1,2,0:T(8,128)(2,1)S(1)} %get-tuple-element.20), channel_id=1, source_target_pairs={{1,0},{2,1},{3,2},{4,3},{5,4},{6,5},{7,6},{8,7},{9,8},{10,9},{11,1... | collective-permute-start | bytes 98312 | tf_op jit(solution)/shard_map/ppermute | solution.py:17
  80.0 2.6 %collective-permute-start.4 = (bf16[1,64,1,256]{3,1,2,0:T(8,128)(2,1)S(1)}, bf16[1,64,1,256]{3,1,2,0:T(8,128)(2,1)S(1)}, u32[]{:S(2)}, u32[]{:S(2)}) collective-permute-start(bf16[1,64,1,256]{3,1,2,0:T(8,128)(2,1)S(1)} %get-tuple-element.19), channel_id=1, source_target_pairs={{0,1},{1,2},{2,3},{3,4},{4,5},{5,6},{6,7},{7,8},{8,9},{9,10},{10,1... | collective-permute-start | bytes 98312 | tf_op jit(solution)/shard_map/ppermute | solution.py:14
  82.6 6.8 %collective-permute-done.4 = bf16[1,64,1,256]{3,1,2,0:T(8,128)(2,1)S(1)} collective-permute-done((bf16[1,64,1,256]{3,1,2,0:T(8,128)(2,1)S(1)}, bf16[1,64,1,256]{3,1,2,0:T(8,128)(2,1)S(1)}, u32[]{:S(2)}, u32[]{:S(2)}) %collective-permute-start.4) | collective-permute-done | bytes 32800 | tf_op jit(solution)/shard_map/ppermute | solution.py:14
  89.5 0.5 select_maximum_fusion
  89.9 0.7 slice_bitcast_fusion.5
  90.7 0.8 copy-done.8
  91.6 0.5 fusion.31
  92.0 0.5 fusion.32
  92.5 0.2 copy-done.10
  92.7 0.6 fusion.86
  93.3 1.1 %copy.90 = bf16[1,64,16,256]{3,2,1,0:T(8,128)(2,1)} copy(bf16[1,64,16,256]{3,1,2,0:T(8,128)(2,1)S(1)} %fusion.86) | data formatting | bytes 1048576 | tf_op jit(solution)/shard_map/convert_element_type | solution.py:79
  (39 shorter events, 1.7 us)
Async XLA Ops:
  0.0 37.0 %copy-start = (bf16[128,1024]{1,0:T(8,128)(2,1)S(1)}, bf16[128,1024]{1,0:T(8,128)(2,1)}, u32[]{:S(2)}) copy-start(bf16[128,1024]{1,0:T(8,128)(2,1)} %param.15) | copy-start | bytes 786436
  1.3 9.8 %collective-permute-start = (bf16[1,64,1,256]{3,1,2,0:T(8,128)(2,1)S(1)}, bf16[1,64,1,256]{3,1,2,0:T(8,128)(2,1)S(1)}, u32[]{:S(2)}, u32[]{:S(2)}) collective-permute-start(bf16[1,64,1,256]{3,1,2,0:T(8,128)(2,1)S(1)} %get-tuple-element.25), channel_id=1, source_target_pairs={{0,1},{1,2},{2,3},{3,4},{4,5},{5,6},{6,7},{7,8},{8,9},{9,10},{10,1... | collective-permute-start | bytes 98312 | tf_op jit(solution)/shard_map/ppermute | solution.py:14
  3.2 9.4 %collective-permute-start.1 = (bf16[1,64,1,256]{3,1,2,0:T(8,128)(2,1)S(1)}, bf16[1,64,1,256]{3,1,2,0:T(8,128)(2,1)S(1)}, u32[]{:S(2)}, u32[]{:S(2)}) collective-permute-start(bf16[1,64,1,256]{3,1,2,0:T(8,128)(2,1)S(1)} %get-tuple-element.26), channel_id=1, source_target_pairs={{1,0},{2,1},{3,2},{4,3},{5,4},{6,5},{7,6},{8,7},{9,8},{10,9},{11,1... | collective-permute-start | bytes 98312 | tf_op jit(solution)/shard_map/ppermute | solution.py:17
  13.1 0.9 copy-start.7
  14.5 0.7 copy-start.9
  15.1 21.9 %copy-start.6 = (f32[128]{0:T(128)S(1)}, f32[128]{0:T(128)}, u32[]{:S(2)}) copy-start(f32[128]{0:T(128)} %param.16) | copy-start | bytes 1540
  15.7 39.8 %copy-start.5 = (f32[4,64]{1,0:T(4,128)S(1)}, f32[4,64]{1,0:T(4,128)}, u32[]{:S(2)}) copy-start(f32[4,64]{1,0:T(4,128)} %param.21) | copy-start | bytes 3076
  50.4 5.1 %collective-permute-start.3 = (bf16[16,5,256]{2,0,1:T(8,128)(2,1)S(1)}, bf16[16,5,256]{2,0,1:T(8,128)(2,1)S(1)}, u32[]{:S(2)}, u32[]{:S(2)}) collective-permute-start(bf16[16,5,256]{2,0,1:T(8,128)(2,1)S(1)} %get-tuple-element.38), channel_id=1, source_target_pairs={{1,0},{2,1},{3,2},{4,3},{5,4},{6,5},{7,6},{8,7},{9,8},{10,9},{11,1... | collective-permute-start | bytes 122888 | tf_op jit(solution)/shard_map/ppermute | solution.py:17
  53.4 9.5 %collective-permute-start.2 = (bf16[16,5,256]{2,0,1:T(8,128)(2,1)S(1)}, bf16[16,5,256]{2,0,1:T(8,128)(2,1)S(1)}, u32[]{:S(2)}, u32[]{:S(2)}) collective-permute-start(bf16[16,5,256]{2,0,1:T(8,128)(2,1)S(1)} %get-tuple-element.37), channel_id=1, source_target_pairs={{0,1},{1,2},{2,3},{3,4},{4,5},{5,6},{6,7},{7,8},{8,9},{9,10},{10,1... | collective-permute-start | bytes 122888 | tf_op jit(solution)/shard_map/ppermute | solution.py:14
  63.5 1.0 %copy-start.1 = (bf16[11,11,64,16]{2,3,1,0:T(8,128)(2,1)S(1)}, bf16[11,11,64,16]{2,3,1,0:T(8,128)(2,1)}, u32[]{:S(2)}) copy-start(bf16[11,11,64,16]{2,3,1,0:T(8,128)(2,1)} %param.20) | copy-start | bytes 743428
  69.1 0.9 copy-start.2
  71.5 0.9 copy-start.3
  73.4 0.8 copy-start.4
  78.1 4.6 %collective-permute-start.5 = (bf16[1,64,1,256]{3,1,2,0:T(8,128)(2,1)S(1)}, bf16[1,64,1,256]{3,1,2,0:T(8,128)(2,1)S(1)}, u32[]{:S(2)}, u32[]{:S(2)}) collective-permute-start(bf16[1,64,1,256]{3,1,2,0:T(8,128)(2,1)S(1)} %get-tuple-element.20), channel_id=1, source_target_pairs={{1,0},{2,1},{3,2},{4,3},{5,4},{6,5},{7,6},{8,7},{9,8},{10,9},{11,1... | collective-permute-start | bytes 98312 | tf_op jit(solution)/shard_map/ppermute | solution.py:17
  80.0 9.5 %collective-permute-start.4 = (bf16[1,64,1,256]{3,1,2,0:T(8,128)(2,1)S(1)}, bf16[1,64,1,256]{3,1,2,0:T(8,128)(2,1)S(1)}, u32[]{:S(2)}, u32[]{:S(2)}) collective-permute-start(bf16[1,64,1,256]{3,1,2,0:T(8,128)(2,1)S(1)} %get-tuple-element.19), channel_id=1, source_target_pairs={{0,1},{1,2},{2,3},{3,4},{4,5},{5,6},{6,7},{7,8},{8,9},{9,10},{10,1... | collective-permute-start | bytes 98312 | tf_op jit(solution)/shard_map/ppermute | solution.py:14
  90.6 0.9 copy-start.8
  92.0 0.7 copy-start.10

commit v5 on v4

--- a/solution.py
+++ b/solution.py
@@ -96,18 +96,22 @@
     frame_index = lax.axis_index("frame")
     frames = lax.axis_size("frame")
     channels, row_count, col_count = (features.shape[1], features.shape[2], features.shape[3])
-    padded = padded_2(features, (("space", 2),), 1)
-    encoded = finish(padded, enc_w, enc_b, row_count, col_count)
+    padded = padded_2(features, (("space", 2),), 2)
+    encoded = finish(padded, enc_w, enc_b, row_count + 2, col_count)
     hidden_count = mix_w.shape[0]
     per_group = frames * channels // GROUPS
     group_width = hidden_count // GROUPS
-    local_groups = max(1, channels // per_group)
-    own_groups = project(encoded[0], mix_w, mix_b, frames, group_width)
-    margin = padded_2(own_groups, (("space", 1),), 5)
+    own_groups = project(encoded[0, :, 1:-1], mix_w, mix_b, frames, group_width)
+    margin = padded_2(own_groups, (("space", 1),), 6)
     margin = jnp.pad(margin, ((0, 0), (0, 0), (5, 5)))
-    summed = branches(margin, (branch3, branch5, branch7, branch11), branch_b, row_count, col_count)
-    joined = (summed + encoded[0].astype(jnp.float32)).astype(jnp.bfloat16)[None]
-    padded_dec = padded_2(joined, (("space", 2),), 1)
+    summed = branches(
+        margin, (branch3, branch5, branch7, branch11), branch_b, row_count + 2, col_count
+    )
+    joined = (summed + encoded[0].astype(jnp.float32)).astype(jnp.bfloat16)
+    strip = lax.axis_index("space")
+    rows = lax.broadcasted_iota(jnp.int32, (1, row_count + 2, 1), 1)
+    inside = ((rows > 0) | (strip > 0)) & ((rows < row_count + 1) | (strip < lax.axis_size("space") - 1))
+    padded_dec = jnp.where(inside, joined, jnp.zeros_like(joined))[None]
     return finish(padded_dec, dec_w, dec_b, row_count, col_count)
 
 

time: 94.9 us -> 86.2 us (0.908)
  blocking collectives: 34.4 us -> 21.5 us
  waiting for transfers between devices: 15.8 us -> 17.7 us
    all_to_all x1 -> x0, blocking collectives: 13.1 us -> none  [project(): own = lax.all_to_all(hidden, 'frame', 0, 0, tiled=False)]
    all_to_all x0 -> x1, waiting for transfers between devices: none -> 8.55 us  [project(): own = lax.all_to_all(hidden, 'frame', 0, 0, tiled=False)]
    ppermute x3 -> x2, waiting for transfers between devices: 14.2 us -> 7.57 us  [padded_2(): lax.ppermute(lax.slice_in_dim(block, block.shape[dim] - width, None, axis...]
    all_to_all x0 -> x1, starting transfers between devices: none -> 4.6 us  [project(): own = lax.all_to_all(hidden, 'frame', 0, 0, tiled=False)]
    ppermute x3 -> x2, starting transfers between devices: 6.65 us -> 4.02 us  [padded_2(): lax.ppermute(lax.slice_in_dim(block, block.shape[dim] - width, None, axis...]
    ppermute x3 -> x2, starting transfers between devices: 12.8 us -> 11.2 us  [padded_2(): lax.ppermute(lax.slice_in_dim(block, 0, width, axis=dim), axis, backward)]
    another operation x2 -> x1, other arithmetic: 0.67 us -> 1.68 us  [sweep(): jnp.stack([lax.slice_in_dim(band, start + col_tap, start + col_tap + col_...]
    unnamed x37 -> x41, local copies, waits for them, and re-layouts: 5.38 us -> 5.1 us
  transfers between devices with their start and end apart: 6 -> 5, of which waited for: 3 -> 4; matrix products, arithmetic and copies ran while one was open for 0% -> 0% of each run, Pallas kernels for 0% -> 0%
where the time goes in v5:
time: 86.2 us; the launch traced here: 85.7 us
  blocking collectives  21.5 us (25%)
  starting transfers between devices  19.9 us (23%)
  waiting for transfers between devices  17.7 us (21%)
  matrix products  15.5 us (18%)
  local copies, waits for them, and re-layouts  8.71 us (10%)
  other arithmetic  1.78 us (2%)
    all_to_all x1, blocking collectives, project(): stacked = lax.all_to_all(blocks, 'frame', 0, 0, tiled=False)  21.5 us
    dot_general x26, matrix products, branches(): jnp.einsum('doi,dirw->orw', weight[a], window, preferred_element_type=jnp...  12.2 us
    ppermute x2, starting transfers between devices, padded_2(): lax.ppermute(lax.slice_in_dim(block, 0, width, axis=dim), axis, backward)  11.2 us
    all_to_all x1, waiting for transfers between devices, project(): own = lax.all_to_all(hidden, 'frame', 0, 0, tiled=False)  8.55 us
    ppermute x2, waiting for transfers between devices, padded_2(): lax.ppermute(lax.slice_in_dim(block, block.shape[dim] - width, None, axis...  7.57 us
    unnamed x41, local copies, waits for them, and re-layouts  5.1 us
    all_to_all x1, starting transfers between devices, project(): own = lax.all_to_all(hidden, 'frame', 0, 0, tiled=False)  4.6 us
    ppermute x2, starting transfers between devices, padded_2(): lax.ppermute(lax.slice_in_dim(block, block.shape[dim] - width, None, axis...  4.02 us
  transfers between devices with their start and end apart: 5, of which 4 were waited for; matrix products, arithmetic and copies ran while one was open for 0% of the time, Pallas kernels for 0%

profile of v5, /device:TPU:256, one launch (start us, length us, event | category | flops | bytes accessed | tf_op | source)
XLA Modules:
  0.0 85.7 jit_solution(7810883725147212408)
XLA Ops:
  0.0 1.3 %copy.50 = bf16[1,64,16,256]{3,1,2,0:T(8,128)(2,1)S(1)} copy(bf16[1,64,16,256]{3,2,1,0:T(8,128)(2,1)} %param.12) | data formatting | bytes 1048576 | tf_op args[0]
  1.3 1.9 %collective-permute-start = (bf16[1,64,2,256]{3,1,2,0:T(8,128)(2,1)S(1)}, bf16[1,64,2,256]{3,1,2,0:T(8,128)(2,1)S(1)}, u32[]{:S(2)}, u32[]{:S(2)}) collective-permute-start(bf16[1,64,2,256]{3,1,2,0:T(8,128)(2,1)S(1)} %get-tuple-element.24), channel_id=1, source_target_pairs={{0,1},{1,2},{2,3},{3,4},{4,5},{5,6},{6,7},{7,8},{8,9},{9,10},{10,1... | collective-permute-start | bytes 196616 | tf_op jit(solution)/shard_map/ppermute | solution.py:14
  3.2 7.9 %collective-permute-start.1 = (bf16[1,64,2,256]{3,1,2,0:T(8,128)(2,1)S(1)}, bf16[1,64,2,256]{3,1,2,0:T(8,128)(2,1)S(1)}, u32[]{:S(2)}, u32[]{:S(2)}) collective-permute-start(bf16[1,64,2,256]{3,1,2,0:T(8,128)(2,1)S(1)} %get-tuple-element.23), channel_id=1, source_target_pairs={{1,0},{2,1},{3,2},{4,3},{5,4},{6,5},{7,6},{8,7},{9,8},{10,9},{11,1... | collective-permute-start | bytes 196616 | tf_op jit(solution)/shard_map/ppermute | solution.py:17
  11.2 0.2 constant_dynamic-update-slice_fusion.1
  11.4 1.6 %collective-permute-done.1 = bf16[1,64,2,256]{3,1,2,0:T(8,128)(2,1)S(1)} collective-permute-done((bf16[1,64,2,256]{3,1,2,0:T(8,128)(2,1)S(1)}, bf16[1,64,2,256]{3,1,2,0:T(8,128)(2,1)S(1)}, u32[]{:S(2)}, u32[]{:S(2)}) %collective-permute-start.1) | collective-permute-done | bytes 65568 | tf_op jit(solution)/shard_map/ppermute | solution.py:17
  13.0 1.7 %fusion.83 = (bf16[1,64,1,18,256]{4,1,2,3,0:T(8,128)(2,1)S(1)}, bf16[1,64,1,18,256]{4,1,2,3,0:T(8,128)(2,1)S(1)}, bf16[1,64,1,18,256]{4,1,3,2,0:T(8,128)(2,1)S(1...) fusion(bf16[1,64,20,256]{3,1,2,0:T(8,128)(2,1)S(1)} %constant_d, ...), kind=kLoop, calls=%fused_computation.135 | loop fusion | flops 2359296 | bytes 7208960 | tf_op jit(solution)/shard_map/stack | solution.py:63
  14.7 0.5 fusion.30
  15.2 0.5 fusion.31
  15.7 0.2 copy-done.10
  15.8 0.7 multiply_convert_fusion
  16.6 21.5 %all_to_all.10 = bf16[16,64,1,256]{3,1,2,0:T(8,128)(2,1)S(1)} all-to-all(bf16[16,64,1,256]{3,1,2,0:T(8,128)(2,1)S(1)} %slice_bitcast_fusion.4), channel_id=1, replica_groups=mesh['frame'=16,'space'=32] {'frame'}, dimensions={0} | all-to-all | bytes 1048576 | tf_op jit(solution)/shard_map/all_to_all | solution.py:26
  38.0 0.2 fusion.79
  38.3 0.7 broadcast_in_dim.25
  39.0 4.6 %all-to-all-start.1 = ((bf16[16,16,1,256]{3,1,2,0:T(8,128)(2,1)}), bf16[16,16,1,256]{3,1,2,0:T(8,128)(2,1)S(1)}, u32[]{:S(2)}, u32[]{:S(2)}) async-start(bf16[16,16,1,256]{3,1,2,0:T(8,128)(2,1)} %bitcast.33), calls=%async_computation.1 | async-start | bytes 262144 | tf_op jit(solution)/shard_map/all_to_all | solution.py:34
  43.6 8.5 %all-to-all-done.1 = bf16[16,16,1,256]{3,1,2,0:T(8,128)(2,1)S(1)} async-done(((bf16[16,16,1,256]{3,1,2,0:T(8,128)(2,1)}), bf16[16,16,1,256]{3,1,2,0:T(8,128)(2,1)S(1)}, u32[]{:S(2)}, u32[]{:S(2)}) %all-to-all-start.1) | async-done | bytes 131104 | tf_op jit(solution)/shard_map/all_to_all | solution.py:34
  52.2 3.4 %collective-permute-start.3 = (bf16[16,6,256]{2,0,1:T(8,128)(2,1)S(1)}, bf16[16,6,256]{2,0,1:T(8,128)(2,1)S(1)}, u32[]{:S(2)}, u32[]{:S(2)}) collective-permute-start(bf16[16,6,256]{2,0,1:T(8,128)(2,1)S(1)} %get-tuple-element.36), channel_id=1, source_target_pairs={{1,0},{2,1},{3,2},{4,3},{5,4},{6,5},{7,6},{8,7},{9,8},{10,9},{11,1... | collective-permute-start | bytes 147464 | tf_op jit(solution)/shard_map/ppermute | solution.py:17
  55.5 2.1 %collective-permute-start.2 = (bf16[16,6,256]{2,0,1:T(8,128)(2,1)S(1)}, bf16[16,6,256]{2,0,1:T(8,128)(2,1)S(1)}, u32[]{:S(2)}, u32[]{:S(2)}) collective-permute-start(bf16[16,6,256]{2,0,1:T(8,128)(2,1)S(1)} %get-tuple-element.35), channel_id=1, source_target_pairs={{0,1},{1,2},{2,3},{3,4},{4,5},{5,6},{6,7},{7,8},{8,9},{9,10},{10,1... | collective-permute-start | bytes 147464 | tf_op jit(solution)/shard_map/ppermute | solution.py:14
  57.7 7.5 %collective-permute-done.2 = bf16[16,6,256]{2,0,1:T(8,128)(2,1)S(1)} collective-permute-done((bf16[16,6,256]{2,0,1:T(8,128)(2,1)S(1)}, bf16[16,6,256]{2,0,1:T(8,128)(2,1)S(1)}, u32[]{:S(2)}, u32[]{:S(2)}) %collective-permute-start.2) | collective-permute-done | bytes 49184 | tf_op jit(solution)/shard_map/ppermute | solution.py:14
  65.6 0.1 bitcast_dynamic-update-slice_fusion.2
  65.7 0.1 constant_dynamic-update-slice_fusion.5
  65.9 0.1 constant_dynamic-update-slice_fusion.3
  66.1 0.1 bitcast_dynamic-update-slice_fusion.1
  66.2 0.1 bitcast_dynamic-update-slice_fusion
  66.3 0.1 fusion.100
  66.6 0.3 copy-done.2
  66.9 0.5 convolution_bitcast_fusion
  67.4 0.5 convolution_bitcast_fusion.1
  67.8 0.5 convolution_bitcast_fusion.2
  68.3 0.5 convolution_bitcast_fusion.3
  68.7 0.5 convolution_bitcast_fusion.4
  69.2 0.5 convolution_bitcast_fusion.5
  69.7 0.5 convolution_bitcast_fusion.6
  70.1 0.5 convolution_bitcast_fusion.7
  70.6 0.5 convolution_bitcast_fusion.8
  71.0 0.5 convolution_bitcast_fusion.9
  71.6 0.2 bitcast_dynamic-update-slice_fusion.14
  71.8 0.2 bitcast_dynamic-update-slice_fusion.5
  72.4 0.2 bitcast_dynamic-update-slice_fusion.9
  72.7 0.3 copy-done.3
  73.0 0.4 convolution_bitcast_fusion.11
  73.4 0.4 convolution_bitcast_fusion.12
  73.7 0.4 convolution_bitcast_fusion.13
  74.1 0.4 convolution_bitcast_fusion.14
  74.5 0.4 convolution_bitcast_fusion.15
  74.8 0.4 convolution_bitcast_fusion.16
  75.2 0.2 fusion.103
  75.4 0.2 copy-done.5
  75.6 0.4 convolution_bitcast_fusion.23
  76.0 0.4 convolution_bitcast_fusion.24
  76.3 0.5 copy-done.4
  76.9 0.4 convolution_bitcast_fusion.18
  77.2 0.4 convolution_bitcast_fusion.19
  77.6 0.4 convolution_bitcast_fusion.20
  78.0 0.4 convolution_bitcast_fusion.21
  78.3 0.5 compare_select_fusion.3
  78.8 0.8 compare_select_fusion.1
  79.6 1.1 %compare_select_fusion = f32[64,18,256]{2,0,1:T(8,128)S(1)} fusion(f32[18,256,64]{1,2,0:T(8,128)S(1)} %convolution_bitcast_fusion, f32[18,256,64]{1,2,0:T(8,128)S(1)} %convolution_bitcast_fusion.1, f32[18,256,64]{1,2,0:T(8,128)S(1)} %convolution_bitcast_fusion.2, f32[18,256,64]{1,2,0:T(8,128)S(1)} %convolution_bitcast_fusion.3, ...), kind=kOutput, calls=%fused_computation | convolution fusion | flops 107937792 | bytes 15544832 | tf_op jit(solution)/shard_map/doi,dirw->orw/dot_general | solution.py:51
  80.7 1.0 %fusion.81 = bf16[1,64,18,256]{3,1,2,0:T(8,128)(2,1)S(1)} fusion(bf16[64,18,256]{2,0,1:T(8,128)(2,1)S(1)} %multiply_convert_fusion, f32[64,18,256]{2,0,1:T(8,128)S(1)} %compare_select_fusion, f32[64,18,256]{2,0,1:T(8,128)S(1)} %compare_select_fusion.1, f32[64,18,256]{2,0,1:T(8,128)S(1)} %compare_select_fusion.3, ...), kind=kOutput, calls=%fused_computation.125 | convolution fusion | flops 51609600 | bytes 10605568 | tf_op jit(solution)/shard_map/doi,dirw->orw/dot_general | solution.py:51
  81.7 1.1 %fusion.89 = (bf16[1,64,1,16,256]{4,1,3,2,0:T(8,128)(2,1)S(1)}, bf16[1,64,1,16,256]{4,1,3,2,0:T(8,128)(2,1)S(1)}, bf16[1,64,1,16,256]{4,1,3,2,0:T(8,128)(2,1)S(1...) fusion(bf16[1,64,18,256]{3,1,2,0:T(8,128)(2,1)S(1)} %fusion.81), kind=kLoop, calls=%fused_computation.144 | loop fusion | bytes 6881280 | tf_op jit(solution)/shard_map/stack | solution.py:63
  82.9 0.5 fusion.33
  83.3 0.4 fusion.34
  83.8 0.2 copy-done.11
  84.0 0.6 fusion.82
  84.6 1.1 %copy.88 = bf16[1,64,16,256]{3,2,1,0:T(8,128)(2,1)} copy(bf16[1,64,16,256]{3,1,2,0:T(8,128)(2,1)S(1)} %fusion.82) | data formatting | bytes 1048576 | tf_op jit(solution)/shard_map/convert_element_type | solution.py:79
  (39 shorter events, 1.3 us)
Async XLA Ops:
  0.0 38.0 %copy-start = (bf16[128,1024]{1,0:T(8,128)(2,1)S(1)}, bf16[128,1024]{1,0:T(8,128)(2,1)}, u32[]{:S(2)}) copy-start(bf16[128,1024]{1,0:T(8,128)(2,1)} %param.15) | copy-start | bytes 786436
  0.0 11.2 %copy-start.1 = (bf16[1,64,16,256]{3,2,1,0:T(8,128)(2,1)S(1)}, bf16[1,64,16,256]{3,2,1,0:T(8,128)(2,1)}, u32[]{:S(2)}) copy-start(bf16[1,64,16,256]{3,2,1,0:T(8,128)(2,1)} %param.12) | copy-start | bytes 1572868
  1.3 9.9 %collective-permute-start = (bf16[1,64,2,256]{3,1,2,0:T(8,128)(2,1)S(1)}, bf16[1,64,2,256]{3,1,2,0:T(8,128)(2,1)S(1)}, u32[]{:S(2)}, u32[]{:S(2)}) collective-permute-start(bf16[1,64,2,256]{3,1,2,0:T(8,128)(2,1)S(1)} %get-tuple-element.24), channel_id=1, source_target_pairs={{0,1},{1,2},{2,3},{3,4},{4,5},{5,6},{6,7},{7,8},{8,9},{9,10},{10,1... | collective-permute-start | bytes 196616 | tf_op jit(solution)/shard_map/ppermute | solution.py:14
  3.2 9.8 %collective-permute-start.1 = (bf16[1,64,2,256]{3,1,2,0:T(8,128)(2,1)S(1)}, bf16[1,64,2,256]{3,1,2,0:T(8,128)(2,1)S(1)}, u32[]{:S(2)}, u32[]{:S(2)}) collective-permute-start(bf16[1,64,2,256]{3,1,2,0:T(8,128)(2,1)S(1)} %get-tuple-element.23), channel_id=1, source_target_pairs={{1,0},{2,1},{3,2},{4,3},{5,4},{6,5},{7,6},{8,7},{9,8},{10,9},{11,1... | collective-permute-start | bytes 196616 | tf_op jit(solution)/shard_map/ppermute | solution.py:17
  13.0 1.7 %copy-start.8 = (bf16[3,3,64,64]{3,2,1,0:T(8,128)(2,1)S(1)}, bf16[3,3,64,64]{3,2,1,0:T(8,128)(2,1)}, u32[]{:S(2)}) copy-start(bf16[3,3,64,64]{3,2,1,0:T(8,128)(2,1)} %param.13) | copy-start | bytes 221188
  15.2 0.7 copy-start.10
  16.5 21.6 %copy-start.7 = (f32[128]{0:T(128)S(1)}, f32[128]{0:T(128)}, u32[]{:S(2)}) copy-start(f32[128]{0:T(128)} %param.16) | copy-start | bytes 1540
  16.6 27.0 %copy-start.6 = (f32[4,64]{1,0:T(4,128)S(1)}, f32[4,64]{1,0:T(4,128)}, u32[]{:S(2)}) copy-start(f32[4,64]{1,0:T(4,128)} %param.21) | copy-start | bytes 3076
  39.0 13.2 %all-to-all-start.1 = ((bf16[16,16,1,256]{3,1,2,0:T(8,128)(2,1)}), bf16[16,16,1,256]{3,1,2,0:T(8,128)(2,1)S(1)}, u32[]{:S(2)}, u32[]{:S(2)}) async-start(bf16[16,16,1,256]{3,1,2,0:T(8,128)(2,1)} %bitcast.33), calls=%async_computation.1 | async-start | bytes 262144 | tf_op jit(solution)/shard_map/all_to_all | solution.py:34
  52.2 5.5 %collective-permute-start.3 = (bf16[16,6,256]{2,0,1:T(8,128)(2,1)S(1)}, bf16[16,6,256]{2,0,1:T(8,128)(2,1)S(1)}, u32[]{:S(2)}, u32[]{:S(2)}) collective-permute-start(bf16[16,6,256]{2,0,1:T(8,128)(2,1)S(1)} %get-tuple-element.36), channel_id=1, source_target_pairs={{1,0},{2,1},{3,2},{4,3},{5,4},{6,5},{7,6},{8,7},{9,8},{10,9},{11,1... | collective-permute-start | bytes 147464 | tf_op jit(solution)/shard_map/ppermute | solution.py:17
  55.5 9.6 %collective-permute-start.2 = (bf16[16,6,256]{2,0,1:T(8,128)(2,1)S(1)}, bf16[16,6,256]{2,0,1:T(8,128)(2,1)S(1)}, u32[]{:S(2)}, u32[]{:S(2)}) collective-permute-start(bf16[16,6,256]{2,0,1:T(8,128)(2,1)S(1)} %get-tuple-element.35), channel_id=1, source_target_pairs={{0,1},{1,2},{2,3},{3,4},{4,5},{5,6},{6,7},{7,8},{8,9},{9,10},{10,1... | collective-permute-start | bytes 147464 | tf_op jit(solution)/shard_map/ppermute | solution.py:14
  65.9 1.0 %copy-start.2 = (bf16[11,11,64,16]{2,3,1,0:T(8,128)(2,1)S(1)}, bf16[11,11,64,16]{2,3,1,0:T(8,128)(2,1)}, u32[]{:S(2)}) copy-start(bf16[11,11,64,16]{2,3,1,0:T(8,128)(2,1)} %param.20) | copy-start | bytes 743428
  72.1 0.9 %copy-start.3 = (bf16[7,7,64,16]{2,3,1,0:T(8,128)(2,1)S(1)}, bf16[7,7,64,16]{2,3,1,0:T(8,128)(2,1)}, u32[]{:S(2)}) copy-start(bf16[7,7,64,16]{2,3,1,0:T(8,128)(2,1)} %param.19) | copy-start | bytes 301060
  74.8 0.8 copy-start.5
  76.0 0.9 %copy-start.4 = (bf16[5,5,64,16]{2,3,1,0:T(8,128)(2,1)S(1)}, bf16[5,5,64,16]{2,3,1,0:T(8,128)(2,1)}, u32[]{:S(2)}) copy-start(bf16[5,5,64,16]{2,3,1,0:T(8,128)(2,1)} %param.18) | copy-start | bytes 153604
  81.7 1.2 %copy-start.9 = (bf16[3,3,64,64]{3,2,1,0:T(8,128)(2,1)S(1)}, bf16[3,3,64,64]{3,2,1,0:T(8,128)(2,1)}, u32[]{:S(2)}) copy-start(bf16[3,3,64,64]{3,2,1,0:T(8,128)(2,1)} %param.22) | copy-start | bytes 221188
  83.3 0.7 copy-start.11

commit v6 on v5

--- a/solution.py
+++ b/solution.py
@@ -74,9 +74,17 @@
 
 
 def finish(padded, weight, bias, row_count, col_count):
-    padded = jnp.pad(padded, ((0, 0), (0, 0), (0, 0), (1, 1)))
-    summed = sweep(padded, weight[:, :, None], 3, 0, row_count, col_count)
-    return jax.nn.silu(summed + bias[None, :, None, None]).astype(jnp.bfloat16)
+    padded = jnp.pad(padded[0], ((0, 0), (0, 0), (1, 1)))
+    shifted = jnp.stack(
+        [lax.slice_in_dim(padded, b, b + col_count, axis=2) for b in range(weight.shape[1])]
+    )
+    summed = jnp.zeros((weight.shape[2], row_count, col_count), jnp.float32)
+    for a in range(weight.shape[0]):
+        window = lax.slice_in_dim(shifted, a, a + row_count, axis=2)
+        summed = summed + jnp.einsum(
+            "doi,dirw->orw", weight[a], window, preferred_element_type=jnp.float32
+        )
+    return jax.nn.silu(summed + bias[:, None, None]).astype(jnp.bfloat16)[None]
 
 
 def per_device(

time: 86.2 us -> 86 us (level)
  local copies, waits for them, and re-layouts: 8.71 us -> 10.9 us
  other arithmetic: 1.78 us -> 0.5 us
  waiting for transfers between devices: 17.7 us -> 16.7 us
    another operation x1 -> x2, other arithmetic: 1.68 us -> 0.4 us  [finish(): jnp.stack([lax.slice_in_dim(padded, b, b + col_count, axis=2) for b in ra...]
    unnamed x41 -> x40, local copies, waits for them, and re-layouts: 5.1 us -> 6.28 us
    slice x1, local copies, waits for them, and re-layouts: 0.01 us -> 1.18 us  [padded_2(): lax.slice_in_dim(block, 0, width, axis=dim)]
    broadcast_in_dim x0 -> x1, local copies, waits for them, and re-layouts: none -> 1.09 us  [finish(): return jax.nn.silu(summed + bias[:, None, None]).astype(jnp.bfloat16)[None]]
    convert_element_type x1 -> x0, local copies, waits for them, and re-layouts: 1.09 us -> none  [finish(): return jax.nn.silu(summed + bias[None, :, None, None]).astype(jnp.bfloat16)]
    ppermute x2, waiting for transfers between devices: 1.63 us -> 0.62 us  [padded_2(): lax.ppermute(lax.slice_in_dim(block, 0, width, axis=dim), axis, backward)]
  transfers between devices with their start and end apart: 5 -> 5, of which waited for: 4 -> 4; matrix products, arithmetic and copies ran while one was open for 0% -> 1% of each run, Pallas kernels for 0% -> 0%
where the time goes in v6:
time: 86 us; the launch traced here: 85.4 us
  blocking collectives  21.4 us (25%)
  starting transfers between devices  19.8 us (23%)
  waiting for transfers between devices  16.7 us (19%)
  matrix products  15.5 us (18%)
  local copies, waits for them, and re-layouts  10.9 us (13%)
    all_to_all x1, blocking collectives, project(): stacked = lax.all_to_all(blocks, 'frame', 0, 0, tiled=False)  21.4 us
    dot_general x26, matrix products, branches(): jnp.einsum('doi,dirw->orw', weight[a], window, preferred_element_type=jnp...  12.1 us
    ppermute x2, starting transfers between devices, padded_2(): lax.ppermute(lax.slice_in_dim(block, 0, width, axis=dim), axis, backward)  11.2 us
    all_to_all x1, waiting for transfers between devices, project(): own = lax.all_to_all(hidden, 'frame', 0, 0, tiled=False)  8.55 us
    ppermute x2, waiting for transfers between devices, padded_2(): lax.ppermute(lax.slice_in_dim(block, block.shape[dim] - width, None, axis...  7.55 us
    unnamed x40, local copies, waits for them, and re-layouts  6.28 us
    all_to_all x1, starting transfers between devices, project(): own = lax.all_to_all(hidden, 'frame', 0, 0, tiled=False)  4.6 us
    ppermute x2, starting transfers between devices, padded_2(): lax.ppermute(lax.slice_in_dim(block, block.shape[dim] - width, None, axis...  4.02 us
  transfers between devices with their start and end apart: 5, of which 4 were waited for; matrix products, arithmetic and copies ran while one was open for 1% of the time, Pallas kernels for 0%

profile of v6, /device:TPU:256, one launch (start us, length us, event | category | flops | bytes accessed | tf_op | source)
XLA Modules:
  0.0 85.4 jit_solution(566133945588359742)
XLA Ops:
  0.0 1.2 %fusion.177 = (bf16[1,64,2,256]{3,2,1,0:T(2,128)(2,1)S(1)}, bf16[1,64,2,256]{3,2,1,0:T(2,128)(2,1)S(1)}) fusion(bf16[1,64,16,256]{3,2,1,0:T(8,128)(2,1)} %param.12), kind=kLoop, calls=%fused_computation.222 | loop fusion | bytes 262144 | tf_op jit(solution)/shard_map/slice | solution.py:17
  1.2 1.9 %collective-permute-start = (bf16[1,64,2,256]{3,1,2,0:T(8,128)(2,1)S(1)}, bf16[1,64,2,256]{3,1,2,0:T(8,128)(2,1)S(1)}, u32[]{:S(2)}, u32[]{:S(2)}) collective-permute-start(bf16[1,64,2,256]{3,1,2,0:T(8,128)(2,1)S(1)} %copy.131), channel_id=1, source_target_pairs={{0,1},{1,2},{2,3},{3,4},{4,5},{5,6},{6,7},{7,8},{8,9},{9,10},{10,1... | collective-permute-start | bytes 196616 | tf_op jit(solution)/shard_map/ppermute | solution.py:14
  3.1 7.9 %collective-permute-start.1 = (bf16[1,64,2,256]{3,1,2,0:T(8,128)(2,1)S(1)}, bf16[1,64,2,256]{3,1,2,0:T(8,128)(2,1)S(1)}, u32[]{:S(2)}, u32[]{:S(2)}) collective-permute-start(bf16[1,64,2,256]{3,1,2,0:T(8,128)(2,1)S(1)} %copy.132), channel_id=1, source_target_pairs={{1,0},{2,1},{3,2},{4,3},{5,4},{6,5},{7,6},{8,7},{9,8},{10,9},{11,1... | collective-permute-start | bytes 196616 | tf_op jit(solution)/shard_map/ppermute | solution.py:17
  11.1 1.2 %constant_dynamic-update-slice_fusion.1 = bf16[1,64,20,256]{3,1,2,0:T(8,128)(2,1)S(1)} fusion(bf16[1,64,20,256]{3,1,2,0:T(8,128)(2,1)S(1)} %constant_dynamic-update-slice_fusion.2, bf16[1,64,16,256]{3,2,1,0:T(8,128)(2,1)} %param.12), kind=kLoop, calls=%fused_computation.147 | loop fusion | bytes 1048576
  12.3 0.6 collective-permute-done.1
  12.9 0.5 fusion.98
  13.5 0.2 pad_maximum_fusion
  13.7 0.7 copy-done.4
  14.4 0.5 fusion.18
  14.9 0.5 fusion.15
  15.3 0.2 copy-done.9
  15.5 0.7 multiply_convert_fusion
  16.2 21.4 %all_to_all.10 = bf16[16,64,1,256]{3,1,2,0:T(8,128)(2,1)S(1)} all-to-all(bf16[16,64,1,256]{3,1,2,0:T(8,128)(2,1)S(1)} %slice_bitcast_fusion), channel_id=1, replica_groups=mesh['frame'=16,'space'=32] {'frame'}, dimensions={0} | all-to-all | bytes 1048576 | tf_op jit(solution)/shard_map/all_to_all | solution.py:26
  37.7 0.2 fusion.89
  37.9 0.7 broadcast_in_dim.27
  38.6 4.6 %all-to-all-start.1 = ((bf16[16,16,1,256]{3,1,2,0:T(8,128)(2,1)}), bf16[16,16,1,256]{3,1,2,0:T(8,128)(2,1)S(1)}, u32[]{:S(2)}, u32[]{:S(2)}) async-start(bf16[16,16,1,256]{3,1,2,0:T(8,128)(2,1)} %bitcast.25), calls=%async_computation.1 | async-start | bytes 262144 | tf_op jit(solution)/shard_map/all_to_all | solution.py:34
  43.2 8.5 %all-to-all-done.1 = bf16[16,16,1,256]{3,1,2,0:T(8,128)(2,1)S(1)} async-done(((bf16[16,16,1,256]{3,1,2,0:T(8,128)(2,1)}), bf16[16,16,1,256]{3,1,2,0:T(8,128)(2,1)S(1)}, u32[]{:S(2)}, u32[]{:S(2)}) %all-to-all-start.1) | async-done | bytes 131104 | tf_op jit(solution)/shard_map/all_to_all | solution.py:34
  51.8 3.4 %collective-permute-start.3 = (bf16[16,6,256]{2,0,1:T(8,128)(2,1)S(1)}, bf16[16,6,256]{2,0,1:T(8,128)(2,1)S(1)}, u32[]{:S(2)}, u32[]{:S(2)}) collective-permute-start(bf16[16,6,256]{2,0,1:T(8,128)(2,1)S(1)} %get-tuple-element.22), channel_id=1, source_target_pairs={{1,0},{2,1},{3,2},{4,3},{5,4},{6,5},{7,6},{8,7},{9,8},{10,9},{11,1... | collective-permute-start | bytes 147464 | tf_op jit(solution)/shard_map/ppermute | solution.py:17
  55.2 2.1 %collective-permute-start.2 = (bf16[16,6,256]{2,0,1:T(8,128)(2,1)S(1)}, bf16[16,6,256]{2,0,1:T(8,128)(2,1)S(1)}, u32[]{:S(2)}, u32[]{:S(2)}) collective-permute-start(bf16[16,6,256]{2,0,1:T(8,128)(2,1)S(1)} %get-tuple-element.21), channel_id=1, source_target_pairs={{0,1},{1,2},{2,3},{3,4},{4,5},{5,6},{6,7},{7,8},{8,9},{9,10},{10,1... | collective-permute-start | bytes 147464 | tf_op jit(solution)/shard_map/ppermute | solution.py:14
  57.3 7.5 %collective-permute-done.2 = bf16[16,6,256]{2,0,1:T(8,128)(2,1)S(1)} collective-permute-done((bf16[16,6,256]{2,0,1:T(8,128)(2,1)S(1)}, bf16[16,6,256]{2,0,1:T(8,128)(2,1)S(1)}, u32[]{:S(2)}, u32[]{:S(2)}) %collective-permute-start.2) | collective-permute-done | bytes 49184 | tf_op jit(solution)/shard_map/ppermute | solution.py:14
  65.0 0.1 fusion.105
  65.8 0.1 bitcast_dynamic-update-slice_fusion
  66.2 0.3 copy-done.1
  66.6 0.4 convolution_bitcast_fusion
  67.0 0.5 convolution_bitcast_fusion.1
  67.5 0.5 convolution_bitcast_fusion.2
  67.9 0.5 convolution_bitcast_fusion.3
  68.4 0.5 convolution_bitcast_fusion.4
  68.8 0.5 convolution_bitcast_fusion.5
  69.3 0.5 convolution_bitcast_fusion.6
  69.8 0.5 convolution_bitcast_fusion.7
  70.2 0.5 convolution_bitcast_fusion.8
  70.7 0.5 convolution_bitcast_fusion.9
  71.3 0.2 bitcast_dynamic-update-slice_fusion.14
  71.5 0.2 bitcast_dynamic-update-slice_fusion.5
  72.0 0.2 bitcast_dynamic-update-slice_fusion.9
  72.3 0.3 copy-done.2
  72.6 0.4 convolution_bitcast_fusion.11
  73.0 0.4 convolution_bitcast_fusion.12
  73.4 0.4 convolution_bitcast_fusion.13
  73.7 0.4 convolution_bitcast_fusion.14
  74.1 0.4 convolution_bitcast_fusion.15
  74.5 0.4 convolution_bitcast_fusion.16
  74.8 0.2 fusion.110
  75.1 0.2 copy-done.6
  75.2 0.4 convolution_bitcast_fusion.23
  75.6 0.4 convolution_bitcast_fusion.24
  76.0 0.5 copy-done.3
  76.5 0.4 convolution_bitcast_fusion.18
  76.9 0.4 convolution_bitcast_fusion.19
  77.2 0.4 convolution_bitcast_fusion.20
  77.6 0.4 convolution_bitcast_fusion.21
  78.0 0.5 compare_select_fusion.3
  78.4 0.8 compare_select_fusion.1
  79.2 1.1 %compare_select_fusion = f32[64,18,256]{2,0,1:T(8,128)S(1)} fusion(f32[18,256,64]{1,2,0:T(8,128)S(1)} %convolution_bitcast_fusion, f32[18,256,64]{1,2,0:T(8,128)S(1)} %convolution_bitcast_fusion.1, f32[18,256,64]{1,2,0:T(8,128)S(1)} %convolution_bitcast_fusion.2, f32[18,256,64]{1,2,0:T(8,128)S(1)} %convolution_bitcast_fusion.3, ...), kind=kOutput, calls=%fused_computation | convolution fusion | flops 107937792 | bytes 15544832 | tf_op jit(solution)/shard_map/doi,dirw->orw/dot_general | solution.py:51
  80.3 0.9 %fusion.90 = bf16[64,18,256]{2,0,1:T(8,128)(2,1)S(1)} fusion(bf16[64,18,256]{2,0,1:T(8,128)(2,1)S(1)} %multiply_convert_fusion, f32[64,18,256]{2,0,1:T(8,128)S(1)} %compare_select_fusion, f32[64,18,256]{2,0,1:T(8,128)S(1)} %compare_select_fusion.1, f32[64,18,256]{2,0,1:T(8,128)S(1)} %compare_select_fusion.3, ...), kind=kOutput, calls=%fused_computation.96 | convolution fusion | flops 51609600 | bytes 10605568 | tf_op jit(solution)/shard_map/doi,dirw->orw/dot_general | solution.py:51
  81.3 0.5 fusion.100
  81.8 0.2 pad_maximum_fusion.1
  82.0 0.7 copy-done.5
  82.7 0.4 fusion.21
  83.1 0.5 fusion.72
  83.6 0.2 copy-done.10
  83.8 0.6 fusion.93
  84.4 1.1 %copy.82 = bf16[1,64,16,256]{3,2,1,0:T(8,128)(2,1)} copy(bf16[1,64,16,256]{3,1,2,0:T(8,128)(2,1)S(1)} %fusion.93) | data formatting | bytes 1048576 | tf_op jit(solution)/shard_map/broadcast_in_dim | solution.py:87
  (40 shorter events, 1.9 us)
Async XLA Ops:
  0.0 37.7 %copy-start = (bf16[128,1024]{1,0:T(8,128)(2,1)S(1)}, bf16[128,1024]{1,0:T(8,128)(2,1)}, u32[]{:S(2)}) copy-start(bf16[128,1024]{1,0:T(8,128)(2,1)} %param.15) | copy-start | bytes 786436
  1.2 9.9 %collective-permute-start = (bf16[1,64,2,256]{3,1,2,0:T(8,128)(2,1)S(1)}, bf16[1,64,2,256]{3,1,2,0:T(8,128)(2,1)S(1)}, u32[]{:S(2)}, u32[]{:S(2)}) collective-permute-start(bf16[1,64,2,256]{3,1,2,0:T(8,128)(2,1)S(1)} %copy.131), channel_id=1, source_target_pairs={{0,1},{1,2},{2,3},{3,4},{4,5},{5,6},{6,7},{7,8},{8,9},{9,10},{10,1... | collective-permute-start | bytes 196616 | tf_op jit(solution)/shard_map/ppermute | solution.py:14
  3.1 9.8 %collective-permute-start.1 = (bf16[1,64,2,256]{3,1,2,0:T(8,128)(2,1)S(1)}, bf16[1,64,2,256]{3,1,2,0:T(8,128)(2,1)S(1)}, u32[]{:S(2)}, u32[]{:S(2)}) collective-permute-start(bf16[1,64,2,256]{3,1,2,0:T(8,128)(2,1)S(1)} %copy.132), channel_id=1, source_target_pairs={{1,0},{2,1},{3,2},{4,3},{5,4},{6,5},{7,6},{8,7},{9,8},{10,9},{11,1... | collective-permute-start | bytes 196616 | tf_op jit(solution)/shard_map/ppermute | solution.py:17
  13.4 0.9 %copy-start.4 = (bf16[3,3,64,64]{3,2,1,0:T(8,128)(2,1)S(1)}, bf16[3,3,64,64]{3,2,1,0:T(8,128)(2,1)}, u32[]{:S(2)}) copy-start(bf16[3,3,64,64]{3,2,1,0:T(8,128)(2,1)} %param.13) | copy-start | bytes 221188
  14.8 0.7 copy-start.9
  16.2 21.5 %copy-start.8 = (f32[128]{0:T(128)S(1)}, f32[128]{0:T(128)}, u32[]{:S(2)}) copy-start(f32[128]{0:T(128)} %param.16) | copy-start | bytes 1540
  16.2 27.0 %copy-start.7 = (f32[4,64]{1,0:T(4,128)S(1)}, f32[4,64]{1,0:T(4,128)}, u32[]{:S(2)}) copy-start(f32[4,64]{1,0:T(4,128)} %param.21) | copy-start | bytes 3076
  38.6 13.2 %all-to-all-start.1 = ((bf16[16,16,1,256]{3,1,2,0:T(8,128)(2,1)}), bf16[16,16,1,256]{3,1,2,0:T(8,128)(2,1)S(1)}, u32[]{:S(2)}, u32[]{:S(2)}) async-start(bf16[16,16,1,256]{3,1,2,0:T(8,128)(2,1)} %bitcast.25), calls=%async_computation.1 | async-start | bytes 262144 | tf_op jit(solution)/shard_map/all_to_all | solution.py:34
  51.8 5.5 %collective-permute-start.3 = (bf16[16,6,256]{2,0,1:T(8,128)(2,1)S(1)}, bf16[16,6,256]{2,0,1:T(8,128)(2,1)S(1)}, u32[]{:S(2)}, u32[]{:S(2)}) collective-permute-start(bf16[16,6,256]{2,0,1:T(8,128)(2,1)S(1)} %get-tuple-element.22), channel_id=1, source_target_pairs={{1,0},{2,1},{3,2},{4,3},{5,4},{6,5},{7,6},{8,7},{9,8},{10,9},{11,1... | collective-permute-start | bytes 147464 | tf_op jit(solution)/shard_map/ppermute | solution.py:17
  55.2 9.6 %collective-permute-start.2 = (bf16[16,6,256]{2,0,1:T(8,128)(2,1)S(1)}, bf16[16,6,256]{2,0,1:T(8,128)(2,1)S(1)}, u32[]{:S(2)}, u32[]{:S(2)}) collective-permute-start(bf16[16,6,256]{2,0,1:T(8,128)(2,1)S(1)} %get-tuple-element.21), channel_id=1, source_target_pairs={{0,1},{1,2},{2,3},{3,4},{4,5},{5,6},{6,7},{7,8},{8,9},{9,10},{10,1... | collective-permute-start | bytes 147464 | tf_op jit(solution)/shard_map/ppermute | solution.py:14
  65.5 1.0 %copy-start.1 = (bf16[11,11,64,16]{2,3,1,0:T(8,128)(2,1)S(1)}, bf16[11,11,64,16]{2,3,1,0:T(8,128)(2,1)}, u32[]{:S(2)}) copy-start(bf16[11,11,64,16]{2,3,1,0:T(8,128)(2,1)} %param.20) | copy-start | bytes 743428
  71.7 0.9 %copy-start.2 = (bf16[7,7,64,16]{2,3,1,0:T(8,128)(2,1)S(1)}, bf16[7,7,64,16]{2,3,1,0:T(8,128)(2,1)}, u32[]{:S(2)}) copy-start(bf16[7,7,64,16]{2,3,1,0:T(8,128)(2,1)} %param.19) | copy-start | bytes 301060
  74.5 0.8 copy-start.6
  75.6 0.9 %copy-start.3 = (bf16[5,5,64,16]{2,3,1,0:T(8,128)(2,1)S(1)}, bf16[5,5,64,16]{2,3,1,0:T(8,128)(2,1)}, u32[]{:S(2)}) copy-start(bf16[5,5,64,16]{2,3,1,0:T(8,128)(2,1)} %param.18) | copy-start | bytes 153604
  81.8 0.9 %copy-start.5 = (bf16[3,3,64,64]{3,2,1,0:T(8,128)(2,1)S(1)}, bf16[3,3,64,64]{3,2,1,0:T(8,128)(2,1)}, u32[]{:S(2)}) copy-start(bf16[3,3,64,64]{3,2,1,0:T(8,128)(2,1)} %param.22) | copy-start | bytes 221188
  83.1 0.7 copy-start.10

commit v7 on v6

--- a/solution.py
+++ b/solution.py
@@ -4,6 +4,17 @@
 from jax.sharding import PartitionSpec as P
 
 GROUPS = 8
+
+
+def halo_rows(block, axis, dim, width):
+    count = lax.axis_size(axis)
+    forward = [(i, i + 1) for i in range(count - 1)]
+    backward = [(target, source) for source, target in forward]
+    low = lax.ppermute(
+        lax.slice_in_dim(block, block.shape[dim] - width, None, axis=dim), axis, forward
+    )
+    high = lax.ppermute(lax.slice_in_dim(block, 0, width, axis=dim), axis, backward)
+    return low, high
 
 
 def padded_2(block, sides, width):
@@ -104,8 +115,15 @@
     frame_index = lax.axis_index("frame")
     frames = lax.axis_size("frame")
     channels, row_count, col_count = (features.shape[1], features.shape[2], features.shape[3])
-    padded = padded_2(features, (("space", 2),), 2)
-    encoded = finish(padded, enc_w, enc_b, row_count + 2, col_count)
+    low, high = halo_rows(features, "space", 2, 2)
+    encoded = jnp.concatenate(
+        [
+            finish(jnp.concatenate([low, features[:, :, :2]], axis=2), enc_w, enc_b, 2, col_count),
+            finish(features, enc_w, enc_b, row_count - 2, col_count),
+            finish(jnp.concatenate([features[:, :, -2:], high], axis=2), enc_w, enc_b, 2, col_count),
+        ],
+        axis=2,
+    )
     hidden_count = mix_w.shape[0]
     per_group = frames * channels // GROUPS
     group_width = hidden_count // GROUPS

time: 86 us -> 84.5 us (0.983)
  the two profiles are of different devices: /device:TPU:256 before, /device:TPU:456 now
where the time goes in v7:
time: 84.5 us; the launch traced here: 83.9 us
  blocking collectives  21.1 us (25%)
  starting transfers between devices  17.4 us (21%)
  matrix products  16.5 us (20%)
  waiting for transfers between devices  16.2 us (19%)
  local copies, waits for them, and re-layouts  11.3 us (13%)
    all_to_all x1, blocking collectives, project(): stacked = lax.all_to_all(blocks, 'frame', 0, 0, tiled=False)  21.1 us
    dot_general x26, matrix products, branches(): jnp.einsum('doi,dirw->orw', weight[a], window, preferred_element_type=jnp...  12.1 us
    all_to_all x1, waiting for transfers between devices, project(): own = lax.all_to_all(hidden, 'frame', 0, 0, tiled=False)  7.34 us
    ppermute x1, waiting for transfers between devices, padded_2(): lax.ppermute(lax.slice_in_dim(block, block.shape[dim] - width, None, axis...  6.81 us
    unnamed x42, local copies, waits for them, and re-layouts  6.51 us
    all_to_all x1, starting transfers between devices, project(): own = lax.all_to_all(hidden, 'frame', 0, 0, tiled=False)  4.88 us
    ppermute x1, starting transfers between devices, padded_2(): lax.ppermute(lax.slice_in_dim(block, 0, width, axis=dim), axis, backward)  4.44 us
    ppermute x1, starting transfers between devices, halo_rows(): lax.ppermute(lax.slice_in_dim(block, 0, width, axis=dim), axis, backward)  4.08 us
  transfers between devices with their start and end apart: 5, of which 3 were waited for; matrix products, arithmetic and copies ran while one was open for 5% of the time, Pallas kernels for 0%

profile of v7, /device:TPU:456, one launch (start us, length us, event | category | flops | bytes accessed | tf_op | source)
XLA Modules:
  0.0 83.9 jit_solution(9010650125056194681)
XLA Ops:
  0.0 1.2 %fusion.222 = (bf16[1,64,2,256]{3,2,1,0:T(2,128)(2,1)S(1)}, bf16[1,64,2,256]{3,2,1,0:T(2,128)(2,1)S(1)}) fusion(bf16[1,64,16,256]{3,2,1,0:T(8,128)(2,1)} %param.12), kind=kLoop, calls=%fused_computation.272 | loop fusion | bytes 262144 | tf_op jit(solution)/shard_map/slice | solution.py:14
  1.2 4.1 %collective-permute-start.1 = (bf16[1,64,2,256]{3,1,2,0:T(8,128)(2,1)S(1)}, bf16[1,64,2,256]{3,1,2,0:T(8,128)(2,1)S(1)}, u32[]{:S(2)}, u32[]{:S(2)}) collective-permute-start(bf16[1,64,2,256]{3,1,2,0:T(8,128)(2,1)S(1)} %copy.150), channel_id=1, source_target_pairs={{1,0},{2,1},{3,2},{4,3},{5,4},{6,5},{7,6},{8,7},{9,8},{10,9},{11,1... | collective-permute-start | bytes 196616 | tf_op jit(solution)/shard_map/ppermute | solution.py:16
  5.3 1.9 %collective-permute-start = (bf16[1,64,2,256]{3,1,2,0:T(8,128)(2,1)S(1)}, bf16[1,64,2,256]{3,1,2,0:T(8,128)(2,1)S(1)}, u32[]{:S(2)}, u32[]{:S(2)}) collective-permute-start(bf16[1,64,2,256]{3,1,2,0:T(8,128)(2,1)S(1)} %copy.151), channel_id=1, source_target_pairs={{0,1},{1,2},{2,3},{3,4},{4,5},{5,6},{6,7},{7,8},{8,9},{9,10},{10,1... | collective-permute-start | bytes 196616 | tf_op jit(solution)/shard_map/ppermute | solution.py:13
  7.3 1.2 %copy.152 = bf16[1,64,16,256]{3,1,2,0:T(8,128)(2,1)S(1)} copy(bf16[1,64,16,256]{3,2,1,0:T(8,128)(2,1)} %param.12) | data formatting | bytes 1048576 | tf_op args[0]
  8.7 0.4 fusion.111
  9.3 0.7 copy-done.2
  10.0 0.4 fusion.54
  10.4 0.4 fusion.86
  10.8 0.2 copy-done.10
  11.1 0.5 fusion.106
  11.8 0.2 convolution_bitcast_fusion.26
  12.0 0.2 convolution_bitcast_fusion.27
  12.2 2.1 %collective-permute-done = bf16[1,64,2,256]{3,1,2,0:T(8,128)(2,1)S(1)} collective-permute-done((bf16[1,64,2,256]{3,1,2,0:T(8,128)(2,1)S(1)}, bf16[1,64,2,256]{3,1,2,0:T(8,128)(2,1)S(1)}, u32[]{:S(2)}, u32[]{:S(2)}) %collective-permute-start) | collective-permute-done | bytes 65568 | tf_op jit(solution)/shard_map/ppermute | solution.py:13
  14.6 0.2 convolution_bitcast_fusion.29
  14.8 0.2 convolution_bitcast_fusion.30
  15.0 0.2 fusion.133
  15.2 0.2 fusion.138
  15.6 21.1 %all_to_all.10 = bf16[16,64,1,256]{3,1,2,0:T(8,128)(2,1)S(1)} all-to-all(bf16[16,64,1,256]{3,1,2,0:T(8,128)(2,1)S(1)} %slice_bitcast_fusion), channel_id=1, replica_groups=mesh['frame'=16,'space'=32] {'frame'}, dimensions={0} | all-to-all | bytes 1048576 | tf_op jit(solution)/shard_map/all_to_all | solution.py:37
  36.8 0.2 fusion.97
  37.0 0.7 broadcast_in_dim.37
  37.7 4.9 %all-to-all-start.1 = ((bf16[16,16,1,256]{3,1,2,0:T(8,128)(2,1)}), bf16[16,16,1,256]{3,1,2,0:T(8,128)(2,1)S(1)}, u32[]{:S(2)}, u32[]{:S(2)}) async-start(bf16[16,16,1,256]{3,1,2,0:T(8,128)(2,1)} %bitcast.48), calls=%async_computation.1 | async-start | bytes 262144 | tf_op jit(solution)/shard_map/all_to_all | solution.py:45
  42.6 7.3 %all-to-all-done.1 = bf16[16,16,1,256]{3,1,2,0:T(8,128)(2,1)S(1)} async-done(((bf16[16,16,1,256]{3,1,2,0:T(8,128)(2,1)}), bf16[16,16,1,256]{3,1,2,0:T(8,128)(2,1)S(1)}, u32[]{:S(2)}, u32[]{:S(2)}) %all-to-all-start.1) | async-done | bytes 131104 | tf_op jit(solution)/shard_map/all_to_all | solution.py:45
  49.9 4.4 %collective-permute-start.3 = (bf16[16,6,256]{2,0,1:T(8,128)(2,1)S(1)}, bf16[16,6,256]{2,0,1:T(8,128)(2,1)S(1)}, u32[]{:S(2)}, u32[]{:S(2)}) collective-permute-start(bf16[16,6,256]{2,0,1:T(8,128)(2,1)S(1)} %get-tuple-element.22), channel_id=1, source_target_pairs={{1,0},{2,1},{3,2},{4,3},{5,4},{6,5},{7,6},{8,7},{9,8},{10,9},{11,1... | collective-permute-start | bytes 147464 | tf_op jit(solution)/shard_map/ppermute | solution.py:28
  54.4 2.1 %collective-permute-start.2 = (bf16[16,6,256]{2,0,1:T(8,128)(2,1)S(1)}, bf16[16,6,256]{2,0,1:T(8,128)(2,1)S(1)}, u32[]{:S(2)}, u32[]{:S(2)}) collective-permute-start(bf16[16,6,256]{2,0,1:T(8,128)(2,1)S(1)} %get-tuple-element.21), channel_id=1, source_target_pairs={{0,1},{1,2},{2,3},{3,4},{4,5},{5,6},{6,7},{7,8},{8,9},{9,10},{10,1... | collective-permute-start | bytes 147464 | tf_op jit(solution)/shard_map/ppermute | solution.py:25
  56.5 6.8 %collective-permute-done.2 = bf16[16,6,256]{2,0,1:T(8,128)(2,1)S(1)} collective-permute-done((bf16[16,6,256]{2,0,1:T(8,128)(2,1)S(1)}, bf16[16,6,256]{2,0,1:T(8,128)(2,1)S(1)}, u32[]{:S(2)}, u32[]{:S(2)}) %collective-permute-start.2) | collective-permute-done | bytes 49184 | tf_op jit(solution)/shard_map/ppermute | solution.py:25
  64.8 0.3 copy-done.3
  65.1 0.4 convolution_bitcast_fusion
  65.5 0.5 convolution_bitcast_fusion.1
  66.0 0.5 convolution_bitcast_fusion.2
  66.4 0.5 convolution_bitcast_fusion.3
  66.9 0.5 convolution_bitcast_fusion.4
  67.3 0.5 convolution_bitcast_fusion.5
  67.8 0.5 convolution_bitcast_fusion.6
  68.3 0.5 convolution_bitcast_fusion.7
  68.7 0.5 convolution_bitcast_fusion.8
  69.2 0.5 convolution_bitcast_fusion.9
  69.8 0.2 bitcast_dynamic-update-slice_fusion.14
  70.0 0.2 bitcast_dynamic-update-slice_fusion.5
  70.8 0.3 copy-done.4
  71.1 0.4 convolution_bitcast_fusion.11
  71.5 0.4 convolution_bitcast_fusion.12
  71.9 0.4 convolution_bitcast_fusion.13
  72.2 0.4 convolution_bitcast_fusion.14
  72.6 0.4 convolution_bitcast_fusion.15
  73.0 0.4 convolution_bitcast_fusion.16
  73.3 0.2 fusion.141
  73.7 0.4 convolution_bitcast_fusion.23
  74.1 0.4 convolution_bitcast_fusion.24
  74.5 0.5 copy-done.5
  75.0 0.4 convolution_bitcast_fusion.18
  75.4 0.4 convolution_bitcast_fusion.19
  75.7 0.4 convolution_bitcast_fusion.20
  76.1 0.4 convolution_bitcast_fusion.21
  76.5 0.5 compare_select_fusion.3
  76.9 0.8 compare_select_fusion.1
  77.7 1.1 %compare_select_fusion = f32[64,18,256]{2,0,1:T(8,128)S(1)} fusion(f32[18,256,64]{1,2,0:T(8,128)S(1)} %convolution_bitcast_fusion, f32[18,256,64]{1,2,0:T(8,128)S(1)} %convolution_bitcast_fusion.1, f32[18,256,64]{1,2,0:T(8,128)S(1)} %convolution_bitcast_fusion.2, f32[18,256,64]{1,2,0:T(8,128)S(1)} %convolution_bitcast_fusion.3, ...), kind=kOutput, calls=%fused_computation | convolution fusion | flops 107937792 | bytes 15544832 | tf_op jit(solution)/shard_map/doi,dirw->orw/dot_general | solution.py:62
  78.8 1.0 %fusion.98 = bf16[64,18,256]{2,0,1:T(8,128)(2,1)S(1)} fusion(f32[64,18,256]{2,0,1:T(8,128)S(1)} %compare_select_fusion, f32[64,18,256]{2,0,1:T(8,128)S(1)} %compare_select_fusion.1, f32[64,18,256]{2,0,1:T(8,128)S(1)} %compare_select_fusion.3, f32[18,256,64]{1,2,0:T(8,128)S(1)} %convolution_bitcast_fusion.18, ...), kind=kOutput, calls=%fused_computation.109 | convolution fusion | flops 52199424 | bytes 10605568 | tf_op jit(solution)/shard_map/doi,dirw->orw/dot_general | solution.py:62
  79.8 0.5 fusion.109
  80.3 0.2 pad_maximum_fusion
  80.5 0.7 copy-done.6
  81.2 0.4 fusion.12
  81.7 0.5 fusion.51
  82.3 0.6 fusion.101
  82.9 1.1 %copy.92 = bf16[1,64,16,256]{3,2,1,0:T(8,128)(2,1)} copy(bf16[1,64,16,256]{3,1,2,0:T(8,128)(2,1)S(1)} %fusion.101) | data formatting | bytes 1048576 | tf_op jit(solution)/shard_map/broadcast_in_dim | solution.py:98
  (54 shorter events, 3.4 us)
Async XLA Ops:
  0.0 36.8 %copy-start = (bf16[128,1024]{1,0:T(8,128)(2,1)S(1)}, bf16[128,1024]{1,0:T(8,128)(2,1)}, u32[]{:S(2)}) copy-start(bf16[128,1024]{1,0:T(8,128)(2,1)} %param.15) | copy-start | bytes 786436
  0.0 8.5 %copy-start.1 = (bf16[1,64,16,256]{3,2,1,0:T(8,128)(2,1)S(1)}, bf16[1,64,16,256]{3,2,1,0:T(8,128)(2,1)}, u32[]{:S(2)}) copy-start(bf16[1,64,16,256]{3,2,1,0:T(8,128)(2,1)} %param.12) | copy-start | bytes 1572868
  1.2 10.4 %collective-permute-start.1 = (bf16[1,64,2,256]{3,1,2,0:T(8,128)(2,1)S(1)}, bf16[1,64,2,256]{3,1,2,0:T(8,128)(2,1)S(1)}, u32[]{:S(2)}, u32[]{:S(2)}) collective-permute-start(bf16[1,64,2,256]{3,1,2,0:T(8,128)(2,1)S(1)} %copy.150), channel_id=1, source_target_pairs={{1,0},{2,1},{3,2},{4,3},{5,4},{6,5},{7,6},{8,7},{9,8},{10,9},{11,1... | collective-permute-start | bytes 196616 | tf_op jit(solution)/shard_map/ppermute | solution.py:16
  5.3 9.0 %collective-permute-start = (bf16[1,64,2,256]{3,1,2,0:T(8,128)(2,1)S(1)}, bf16[1,64,2,256]{3,1,2,0:T(8,128)(2,1)S(1)}, u32[]{:S(2)}, u32[]{:S(2)}) collective-permute-start(bf16[1,64,2,256]{3,1,2,0:T(8,128)(2,1)S(1)} %copy.151), channel_id=1, source_target_pairs={{0,1},{1,2},{2,3},{3,4},{4,5},{5,6},{6,7},{7,8},{8,9},{9,10},{10,1... | collective-permute-start | bytes 196616 | tf_op jit(solution)/shard_map/ppermute | solution.py:13
  9.1 0.9 %copy-start.2 = (bf16[3,3,64,64]{3,2,1,0:T(8,128)(2,1)S(1)}, bf16[3,3,64,64]{3,2,1,0:T(8,128)(2,1)}, u32[]{:S(2)}) copy-start(bf16[3,3,64,64]{3,2,1,0:T(8,128)(2,1)} %param.13) | copy-start | bytes 221188
  10.4 0.7 copy-start.10
  15.5 21.3 %copy-start.9 = (f32[128]{0:T(128)S(1)}, f32[128]{0:T(128)}, u32[]{:S(2)}) copy-start(f32[128]{0:T(128)} %param.16) | copy-start | bytes 1540
  15.6 27.0 %copy-start.8 = (f32[4,64]{1,0:T(4,128)S(1)}, f32[4,64]{1,0:T(4,128)}, u32[]{:S(2)}) copy-start(f32[4,64]{1,0:T(4,128)} %param.21) | copy-start | bytes 3076
  37.7 12.2 %all-to-all-start.1 = ((bf16[16,16,1,256]{3,1,2,0:T(8,128)(2,1)}), bf16[16,16,1,256]{3,1,2,0:T(8,128)(2,1)S(1)}, u32[]{:S(2)}, u32[]{:S(2)}) async-start(bf16[16,16,1,256]{3,1,2,0:T(8,128)(2,1)} %bitcast.48), calls=%async_computation.1 | async-start | bytes 262144 | tf_op jit(solution)/shard_map/all_to_all | solution.py:45
  49.9 6.6 %collective-permute-start.3 = (bf16[16,6,256]{2,0,1:T(8,128)(2,1)S(1)}, bf16[16,6,256]{2,0,1:T(8,128)(2,1)S(1)}, u32[]{:S(2)}, u32[]{:S(2)}) collective-permute-start(bf16[16,6,256]{2,0,1:T(8,128)(2,1)S(1)} %get-tuple-element.22), channel_id=1, source_target_pairs={{1,0},{2,1},{3,2},{4,3},{5,4},{6,5},{7,6},{8,7},{9,8},{10,9},{11,1... | collective-permute-start | bytes 147464 | tf_op jit(solution)/shard_map/ppermute | solution.py:28
  54.4 8.9 %collective-permute-start.2 = (bf16[16,6,256]{2,0,1:T(8,128)(2,1)S(1)}, bf16[16,6,256]{2,0,1:T(8,128)(2,1)S(1)}, u32[]{:S(2)}, u32[]{:S(2)}) collective-permute-start(bf16[16,6,256]{2,0,1:T(8,128)(2,1)S(1)} %get-tuple-element.21), channel_id=1, source_target_pairs={{0,1},{1,2},{2,3},{3,4},{4,5},{5,6},{6,7},{7,8},{8,9},{9,10},{10,1... | collective-permute-start | bytes 147464 | tf_op jit(solution)/shard_map/ppermute | solution.py:25
  64.0 1.0 %copy-start.3 = (bf16[11,11,64,16]{2,3,1,0:T(8,128)(2,1)S(1)}, bf16[11,11,64,16]{2,3,1,0:T(8,128)(2,1)}, u32[]{:S(2)}) copy-start(bf16[11,11,64,16]{2,3,1,0:T(8,128)(2,1)} %param.20) | copy-start | bytes 743428
  70.2 0.9 %copy-start.4 = (bf16[7,7,64,16]{2,3,1,0:T(8,128)(2,1)S(1)}, bf16[7,7,64,16]{2,3,1,0:T(8,128)(2,1)}, u32[]{:S(2)}) copy-start(bf16[7,7,64,16]{2,3,1,0:T(8,128)(2,1)} %param.19) | copy-start | bytes 301060
  73.0 0.8 copy-start.7
  74.1 0.9 %copy-start.5 = (bf16[5,5,64,16]{2,3,1,0:T(8,128)(2,1)S(1)}, bf16[5,5,64,16]{2,3,1,0:T(8,128)(2,1)}, u32[]{:S(2)}) copy-start(bf16[5,5,64,16]{2,3,1,0:T(8,128)(2,1)} %param.18) | copy-start | bytes 153604
  80.3 0.9 %copy-start.6 = (bf16[3,3,64,64]{3,2,1,0:T(8,128)(2,1)S(1)}, bf16[3,3,64,64]{3,2,1,0:T(8,128)(2,1)}, u32[]{:S(2)}) copy-start(bf16[3,3,64,64]{3,2,1,0:T(8,128)(2,1)} %param.22) | copy-start | bytes 221188
  81.6 0.7 copy-start.11

commit v8 on v7

--- a/solution.py
+++ b/solution.py
@@ -2,6 +2,7 @@
 import jax.numpy as jnp
 from jax import lax
 from jax.sharding import PartitionSpec as P
+
 
 GROUPS = 8
 
@@ -15,19 +16,6 @@
     )
     high = lax.ppermute(lax.slice_in_dim(block, 0, width, axis=dim), axis, backward)
     return low, high
-
-
-def padded_2(block, sides, width):
-    for axis, dim in sides:
-        count = lax.axis_size(axis)
-        forward = [(i, i + 1) for i in range(count - 1)]
-        backward = [(target, source) for source, target in forward]
-        low = lax.ppermute(
-            lax.slice_in_dim(block, block.shape[dim] - width, None, axis=dim), axis, forward
-        )
-        high = lax.ppermute(lax.slice_in_dim(block, 0, width, axis=dim), axis, backward)
-        block = jnp.concatenate([low, block, high], axis=dim)
-    return block
 
 
 def project(encoded, mix_w, mix_b, frames, group_width):
@@ -67,23 +55,6 @@
     return summed
 
 
-def sweep(padded, weight, kernel_size, start, row_count, col_count):
-    summed = jnp.zeros((padded.shape[0], weight.shape[3], row_count, col_count), jnp.float32)
-    for row_tap in range(kernel_size):
-        band = lax.slice_in_dim(padded, start + row_tap, start + row_tap + row_count, axis=2)
-        window = jnp.stack(
-            [
-                lax.slice_in_dim(band, start + col_tap, start + col_tap + col_count, axis=3)
-                for col_tap in range(kernel_size)
-            ],
-            axis=2,
-        )
-        summed = summed + jnp.einsum(
-            "dgoi,gidrw->gorw", weight[row_tap], window, preferred_element_type=jnp.float32
-        )
-    return summed
-
-
 def finish(padded, weight, bias, row_count, col_count):
     padded = jnp.pad(padded[0], ((0, 0), (0, 0), (1, 1)))
     shifted = jnp.stack(
@@ -112,9 +83,8 @@
     dec_w,
     dec_b,
 ):
-    frame_index = lax.axis_index("frame")
     frames = lax.axis_size("frame")
-    channels, row_count, col_count = (features.shape[1], features.shape[2], features.shape[3])
+    row_count, col_count = (features.shape[2], features.shape[3])
     low, high = halo_rows(features, "space", 2, 2)
     encoded = jnp.concatenate(
         [
@@ -125,13 +95,27 @@
         axis=2,
     )
     hidden_count = mix_w.shape[0]
-    per_group = frames * channels // GROUPS
     group_width = hidden_count // GROUPS
     own_groups = project(encoded[0, :, 1:-1], mix_w, mix_b, frames, group_width)
-    margin = padded_2(own_groups, (("space", 1),), 6)
-    margin = jnp.pad(margin, ((0, 0), (0, 0), (5, 5)))
-    summed = branches(
-        margin, (branch3, branch5, branch7, branch11), branch_b, row_count + 2, col_count
+    kernels = (branch3, branch5, branch7, branch11)
+    reach = 6
+    low, high = halo_rows(own_groups, "space", 1, reach)
+    middle = branches(
+        jnp.pad(own_groups, ((0, 0), (0, 0), (5, 5))),
+        kernels,
+        branch_b,
+        row_count - 2 * (reach - 1),
+        col_count,
+    )
+    top = jnp.concatenate([low, own_groups[:, : 2 * reach - 2]], axis=1)
+    bottom = jnp.concatenate([own_groups[:, row_count - 2 * reach + 2 :], high], axis=1)
+    side = jnp.pad(
+        jnp.concatenate([top, jnp.zeros_like(top[:, :, :10]), bottom], axis=2),
+        ((0, 0), (0, 0), (5, 5)),
+    )
+    edges = branches(side, kernels, branch_b, reach, 2 * col_count + 10)
+    summed = jnp.concatenate(
+        [edges[:, :, :col_count], middle, edges[:, :, col_count + 10 :]], axis=1
     )
     joined = (summed + encoded[0].astype(jnp.float32)).astype(jnp.bfloat16)
     strip = lax.axis_index("space")
@@ -156,6 +140,7 @@
         P(),
         P(),
     )
+
     return jax.shard_map(
         per_device,
         mesh=mesh,

time: 84.5 us -> 92.3 us (1.092)
  blocking collectives: 21.1 us -> 0 us
  waiting for transfers between devices: 16.2 us -> 27.6 us
  starting transfers between devices: 17.4 us -> 25.9 us
  matrix products: 16.5 us -> 22.3 us
  local copies, waits for them, and re-layouts: 11.3 us -> 13.7 us
    all_to_all x1 -> x0, blocking collectives: 21.1 us -> none  [project(): stacked = lax.all_to_all(blocks, 'frame', 0, 0, tiled=False)]
    all_to_all x0 -> x1, waiting for transfers between devices: none -> 12.9 us  [project(): stacked = lax.all_to_all(blocks, 'frame', 0, 0, tiled=False)]
    all_to_all x0 -> x1, starting transfers between devices: none -> 8.47 us  [project(): stacked = lax.all_to_all(blocks, 'frame', 0, 0, tiled=False)]
    ppermute x2 -> x0, waiting for transfers between devices: 6.81 us -> none  [the longest x1 6.81 us: padded_2(): lax.ppermute(lax.slice_in_dim(block, block.shape[dim] - width, None, axis...]
    ppermute x2 -> x0, starting transfers between devices: 6.54 us -> none  [the longest x1 4.44 us: padded_2(): lax.ppermute(lax.slice_in_dim(block, 0, width, axis=dim), axis, backward)]
    dot_general x26 -> x52, matrix products: 12.1 us -> 18 us  [branches(): jnp.einsum('doi,dirw->orw', weight[a], window, preferred_element_type=jnp...]
    ppermute x1 -> x2, waiting for transfers between devices: 2.1 us -> 7.37 us  [halo_rows(): lax.ppermute(lax.slice_in_dim(block, block.shape[dim] - width, None, axis...]
    ppermute x1 -> x2, starting transfers between devices: 4.08 us -> 8.5 us  [halo_rows(): lax.ppermute(lax.slice_in_dim(block, 0, width, axis=dim), axis, backward)]
  transfers between devices with their start and end apart: 5 -> 6, of which waited for: 3 -> 4; matrix products, arithmetic and copies ran while one was open for 5% -> 6% of each run, Pallas kernels for 0% -> 0%
where the time goes in v8:
time: 92.3 us; the launch traced here: 91.7 us
  waiting for transfers between devices  27.6 us (30%)
  starting transfers between devices  25.9 us (28%)
  matrix products  22.3 us (24%)
  local copies, waits for them, and re-layouts  13.7 us (15%)
  other arithmetic  1.32 us (1%)
    dot_general x52, matrix products, branches(): jnp.einsum('doi,dirw->orw', weight[a], window, preferred_element_type=jnp...  18 us
    all_to_all x1, waiting for transfers between devices, project(): stacked = lax.all_to_all(blocks, 'frame', 0, 0, tiled=False)  12.9 us
    ppermute x2, starting transfers between devices, halo_rows(): lax.ppermute(lax.slice_in_dim(block, 0, width, axis=dim), axis, backward)  8.5 us
    all_to_all x1, starting transfers between devices, project(): stacked = lax.all_to_all(blocks, 'frame', 0, 0, tiled=False)  8.47 us
    ppermute x2, waiting for transfers between devices, halo_rows(): lax.ppermute(lax.slice_in_dim(block, block.shape[dim] - width, None, axis...  7.37 us
    all_to_all x1, waiting for transfers between devices, project(): own = lax.all_to_all(hidden, 'frame', 0, 0, tiled=False)  7.3 us
    unnamed x57, local copies, waits for them, and re-layouts  7.25 us
    all_to_all x1, starting transfers between devices, project(): own = lax.all_to_all(hidden, 'frame', 0, 0, tiled=False)  4.88 us
  transfers between devices with their start and end apart: 6, of which 4 were waited for; matrix products, arithmetic and copies ran while one was open for 6% of the time, Pallas kernels for 0%

profile of v8, /device:TPU:456, one launch (start us, length us, event | category | flops | bytes accessed | tf_op | source)
XLA Modules:
  0.0 91.7 jit_solution(5843375795504481998)
XLA Ops:
  0.0 1.2 %fusion.317 = (bf16[1,64,2,256]{3,2,1,0:T(2,128)(2,1)S(1)}, bf16[1,64,2,256]{3,2,1,0:T(2,128)(2,1)S(1)}) fusion(bf16[1,64,16,256]{3,2,1,0:T(8,128)(2,1)} %param.12), kind=kLoop, calls=%fused_computation.423 | loop fusion | bytes 262144 | tf_op jit(solution)/shard_map/slice | solution.py:15
  1.2 4.1 %collective-permute-start.1 = (bf16[1,64,2,256]{3,1,2,0:T(8,128)(2,1)S(1)}, bf16[1,64,2,256]{3,1,2,0:T(8,128)(2,1)S(1)}, u32[]{:S(2)}, u32[]{:S(2)}) collective-permute-start(bf16[1,64,2,256]{3,1,2,0:T(8,128)(2,1)S(1)} %copy.242), channel_id=1, source_target_pairs={{1,0},{2,1},{3,2},{4,3},{5,4},{6,5},{7,6},{8,7},{9,8},{10,9},{11,1... | collective-permute-start | bytes 196616 | tf_op jit(solution)/shard_map/ppermute | solution.py:17
  5.3 1.9 %collective-permute-start = (bf16[1,64,2,256]{3,1,2,0:T(8,128)(2,1)S(1)}, bf16[1,64,2,256]{3,1,2,0:T(8,128)(2,1)S(1)}, u32[]{:S(2)}, u32[]{:S(2)}) collective-permute-start(bf16[1,64,2,256]{3,1,2,0:T(8,128)(2,1)S(1)} %copy.243), channel_id=1, source_target_pairs={{0,1},{1,2},{2,3},{3,4},{4,5},{5,6},{6,7},{7,8},{8,9},{9,10},{10,1... | collective-permute-start | bytes 196616 | tf_op jit(solution)/shard_map/ppermute | solution.py:14
  7.3 1.2 %copy.244 = bf16[1,64,16,256]{3,1,2,0:T(8,128)(2,1)S(1)} copy(bf16[1,64,16,256]{3,2,1,0:T(8,128)(2,1)} %param.12) | data formatting | bytes 1048576 | tf_op args[0]
  8.7 0.4 fusion.146
  9.3 0.7 copy-done.5
  10.0 0.4 fusion.33
  10.4 0.4 fusion.72
  11.1 0.5 fusion.136
  12.2 2.1 %collective-permute-done = bf16[1,64,2,256]{3,1,2,0:T(8,128)(2,1)S(1)} collective-permute-done((bf16[1,64,2,256]{3,1,2,0:T(8,128)(2,1)S(1)}, bf16[1,64,2,256]{3,1,2,0:T(8,128)(2,1)S(1)}, u32[]{:S(2)}, u32[]{:S(2)}) %collective-permute-start) | collective-permute-done | bytes 65568 | tf_op jit(solution)/shard_map/ppermute | solution.py:14
  15.6 0.8 slice_bitcast_fusion
  16.4 8.5 %all-to-all-start = ((bf16[16,64,1,256]{3,1,2,0:T(8,128)(2,1)}), bf16[16,64,1,256]{3,1,2,0:T(8,128)(2,1)S(1)}, u32[]{:S(2)}, u32[]{:S(2)}) async-start(bf16[16,64,1,256]{3,1,2,0:T(8,128)(2,1)} %slice_bitcast_fusion), calls=%async_computation | async-start | bytes 1048576 | tf_op jit(solution)/shard_map/all_to_all | solution.py:25
  24.9 12.9 %all-to-all-done = bf16[16,64,1,256]{3,1,2,0:T(8,128)(2,1)S(1)} async-done(((bf16[16,64,1,256]{3,1,2,0:T(8,128)(2,1)}), bf16[16,64,1,256]{3,1,2,0:T(8,128)(2,1)S(1)}, u32[]{:S(2)}, u32[]{:S(2)}) %all-to-all-start) | async-done | bytes 524320 | tf_op jit(solution)/shard_map/all_to_all | solution.py:25
  38.0 0.7 broadcast_in_dim.44
  38.7 4.9 %all-to-all-start.1 = ((bf16[16,16,1,256]{3,1,2,0:T(8,128)(2,1)}), bf16[16,16,1,256]{3,1,2,0:T(8,128)(2,1)S(1)}, u32[]{:S(2)}, u32[]{:S(2)}) async-start(bf16[16,16,1,256]{3,1,2,0:T(8,128)(2,1)} %bitcast.48), calls=%async_computation.1 | async-start | bytes 262144 | tf_op jit(solution)/shard_map/all_to_all | solution.py:33
  43.6 7.3 %all-to-all-done.1 = bf16[16,16,1,256]{3,1,2,0:T(8,128)(2,1)S(1)} async-done(((bf16[16,16,1,256]{3,1,2,0:T(8,128)(2,1)}), bf16[16,16,1,256]{3,1,2,0:T(8,128)(2,1)S(1)}, u32[]{:S(2)}, u32[]{:S(2)}) %all-to-all-start.1) | async-done | bytes 131104 | tf_op jit(solution)/shard_map/all_to_all | solution.py:33
  56.0 0.3 convolution_bitcast_fusion.26
  56.5 0.3 convolution_bitcast_fusion.28
  57.1 0.3 convolution_bitcast_fusion.30
  57.6 0.3 convolution_bitcast_fusion.32
  58.1 0.3 convolution_bitcast_fusion.34
  58.4 0.3 convolution_bitcast_fusion.35
  58.7 4.4 %collective-permute-start.3 = (bf16[16,6,256]{2,0,1:T(8,128)(2,1)S(1)}, bf16[16,6,256]{2,0,1:T(8,128)(2,1)S(1)}, u32[]{:S(2)}, u32[]{:S(2)}) collective-permute-start(bf16[16,6,256]{2,0,1:T(8,128)(2,1)S(1)} %get-tuple-element.44), channel_id=1, source_target_pairs={{1,0},{2,1},{3,2},{4,3},{5,4},{6,5},{7,6},{8,7},{9,8},{10,9},{11,1... | collective-permute-start | bytes 147464 | tf_op jit(solution)/shard_map/ppermute | solution.py:17
  63.1 2.1 %collective-permute-start.2 = (bf16[16,6,256]{2,0,1:T(8,128)(2,1)S(1)}, bf16[16,6,256]{2,0,1:T(8,128)(2,1)S(1)}, u32[]{:S(2)}, u32[]{:S(2)}) collective-permute-start(bf16[16,6,256]{2,0,1:T(8,128)(2,1)S(1)} %get-tuple-element.43), channel_id=1, source_target_pairs={{0,1},{1,2},{2,3},{3,4},{4,5},{5,6},{6,7},{7,8},{8,9},{9,10},{10,1... | collective-permute-start | bytes 147464 | tf_op jit(solution)/shard_map/ppermute | solution.py:14
  65.2 0.3 compare_select_fusion.7
  65.5 0.4 fusion.141
  65.9 0.4 fusion.140
  66.3 0.5 fusion.139
  66.8 5.3 %collective-permute-done.2 = bf16[16,6,256]{2,0,1:T(8,128)(2,1)S(1)} collective-permute-done((bf16[16,6,256]{2,0,1:T(8,128)(2,1)S(1)}, bf16[16,6,256]{2,0,1:T(8,128)(2,1)S(1)}, u32[]{:S(2)}, u32[]{:S(2)}) %collective-permute-start.2) | collective-permute-done | bytes 49184 | tf_op jit(solution)/shard_map/ppermute | solution.py:14
  74.0 0.4 convolution_bitcast_fusion.15
  74.4 0.4 convolution_bitcast_fusion.16
  74.9 0.4 convolution_bitcast_fusion.17
  75.3 0.4 convolution_bitcast_fusion.18
  75.7 0.4 convolution_bitcast_fusion.19
  76.1 0.4 convolution_bitcast_fusion.20
  76.5 0.4 convolution_bitcast_fusion.21
  76.9 0.4 convolution_bitcast_fusion.22
  77.3 0.4 convolution_bitcast_fusion.23
  77.7 0.4 convolution_bitcast_fusion.24
  78.4 0.3 bitcast_dynamic-update-slice_fusion.18
  79.2 0.3 bitcast_dynamic-update-slice_fusion.8
  79.5 0.3 bitcast_dynamic-update-slice_fusion.13
  79.8 0.3 convolution_bitcast_fusion.3
  80.2 0.3 convolution_bitcast_fusion.4
  80.5 0.3 convolution_bitcast_fusion.5
  80.8 0.3 convolution_bitcast_fusion.6
  81.2 0.3 convolution_bitcast_fusion.7
  81.5 0.3 convolution_bitcast_fusion.8
  81.9 0.3 convolution_bitcast_fusion.10
  82.2 0.3 convolution_bitcast_fusion.11
  82.6 0.3 convolution_bitcast_fusion.12
  82.9 0.3 convolution_bitcast_fusion.13
  83.5 0.3 convolution_bitcast_fusion
  83.9 0.3 convolution_bitcast_fusion.1
  84.2 0.5 compare_select_fusion.2
  84.7 0.6 compare_select_fusion.1
  85.4 0.9 compare_select_fusion
  86.3 0.8 fusion.48
  87.4 0.5 fusion.142
  88.3 0.7 copy-done.8
  89.0 0.4 fusion.12
  89.4 0.5 fusion.30
  90.1 0.6 fusion.131
  90.6 1.1 %copy.144 = bf16[1,64,16,256]{3,2,1,0:T(8,128)(2,1)} copy(bf16[1,64,16,256]{3,1,2,0:T(8,128)(2,1)S(1)} %fusion.131) | data formatting | bytes 1048576 | tf_op jit(solution)/shard_map/broadcast_in_dim | solution.py:69
  (104 shorter events, 12.3 us)
Async XLA Ops:
  0.0 37.8 %copy-start = (bf16[128,1024]{1,0:T(8,128)(2,1)S(1)}, bf16[128,1024]{1,0:T(8,128)(2,1)}, u32[]{:S(2)}) copy-start(bf16[128,1024]{1,0:T(8,128)(2,1)} %param.15) | copy-start | bytes 786436
  0.0 8.5 %copy-start.2 = (bf16[1,64,16,256]{3,2,1,0:T(8,128)(2,1)S(1)}, bf16[1,64,16,256]{3,2,1,0:T(8,128)(2,1)}, u32[]{:S(2)}) copy-start(bf16[1,64,16,256]{3,2,1,0:T(8,128)(2,1)} %param.12) | copy-start | bytes 1572868
  1.2 10.4 %collective-permute-start.1 = (bf16[1,64,2,256]{3,1,2,0:T(8,128)(2,1)S(1)}, bf16[1,64,2,256]{3,1,2,0:T(8,128)(2,1)S(1)}, u32[]{:S(2)}, u32[]{:S(2)}) collective-permute-start(bf16[1,64,2,256]{3,1,2,0:T(8,128)(2,1)S(1)} %copy.242), channel_id=1, source_target_pairs={{1,0},{2,1},{3,2},{4,3},{5,4},{6,5},{7,6},{8,7},{9,8},{10,9},{11,1... | collective-permute-start | bytes 196616 | tf_op jit(solution)/shard_map/ppermute | solution.py:17
  5.3 9.0 %collective-permute-start = (bf16[1,64,2,256]{3,1,2,0:T(8,128)(2,1)S(1)}, bf16[1,64,2,256]{3,1,2,0:T(8,128)(2,1)S(1)}, u32[]{:S(2)}, u32[]{:S(2)}) collective-permute-start(bf16[1,64,2,256]{3,1,2,0:T(8,128)(2,1)S(1)} %copy.243), channel_id=1, source_target_pairs={{0,1},{1,2},{2,3},{3,4},{4,5},{5,6},{6,7},{7,8},{8,9},{9,10},{10,1... | collective-permute-start | bytes 196616 | tf_op jit(solution)/shard_map/ppermute | solution.py:14
  9.1 0.9 copy-start.5
  10.4 0.7 copy-start.11
  15.5 22.3 %copy-start.10 = (f32[128]{0:T(128)S(1)}, f32[128]{0:T(128)}, u32[]{:S(2)}) copy-start(f32[128]{0:T(128)} %param.16) | copy-start | bytes 1540
  15.5 28.1 %copy-start.9 = (f32[4,64]{1,0:T(4,128)S(1)}, f32[4,64]{1,0:T(4,128)}, u32[]{:S(2)}) copy-start(f32[4,64]{1,0:T(4,128)} %param.21) | copy-start | bytes 3076
  15.6 35.5 %copy-start.7 = (bf16[3,3,64,16]{2,3,1,0:T(8,128)(2,1)S(1)}, bf16[3,3,64,16]{2,3,1,0:T(8,128)(2,1)}, u32[]{:S(2)}) copy-start(bf16[3,3,64,16]{2,3,1,0:T(8,128)(2,1)} %param.17) | copy-start | bytes 55300
  16.4 21.4 %all-to-all-start = ((bf16[16,64,1,256]{3,1,2,0:T(8,128)(2,1)}), bf16[16,64,1,256]{3,1,2,0:T(8,128)(2,1)S(1)}, u32[]{:S(2)}, u32[]{:S(2)}) async-start(bf16[16,64,1,256]{3,1,2,0:T(8,128)(2,1)} %slice_bitcast_fusion), calls=%async_computation | async-start | bytes 1048576 | tf_op jit(solution)/shard_map/all_to_all | solution.py:25
  38.7 12.2 %all-to-all-start.1 = ((bf16[16,16,1,256]{3,1,2,0:T(8,128)(2,1)}), bf16[16,16,1,256]{3,1,2,0:T(8,128)(2,1)S(1)}, u32[]{:S(2)}, u32[]{:S(2)}) async-start(bf16[16,16,1,256]{3,1,2,0:T(8,128)(2,1)} %bitcast.48), calls=%async_computation.1 | async-start | bytes 262144 | tf_op jit(solution)/shard_map/all_to_all | solution.py:33
  52.2 1.3 %copy-start.6 = (bf16[5,5,64,16]{2,3,1,0:T(8,128)(2,1)S(1)}, bf16[5,5,64,16]{2,3,1,0:T(8,128)(2,1)}, u32[]{:S(2)}) copy-start(bf16[5,5,64,16]{2,3,1,0:T(8,128)(2,1)} %param.18) | copy-start | bytes 153604
  53.2 1.3 %copy-start.4 = (bf16[7,7,64,16]{2,3,1,0:T(8,128)(2,1)S(1)}, bf16[7,7,64,16]{2,3,1,0:T(8,128)(2,1)}, u32[]{:S(2)}) copy-start(bf16[7,7,64,16]{2,3,1,0:T(8,128)(2,1)} %param.19) | copy-start | bytes 301060
  55.0 1.0 %copy-start.3 = (bf16[11,11,64,16]{2,3,1,0:T(8,128)(2,1)S(1)}, bf16[11,11,64,16]{2,3,1,0:T(8,128)(2,1)}, u32[]{:S(2)}) copy-start(bf16[11,11,64,16]{2,3,1,0:T(8,128)(2,1)} %param.20) | copy-start | bytes 743428
  58.7 8.1 %collective-permute-start.3 = (bf16[16,6,256]{2,0,1:T(8,128)(2,1)S(1)}, bf16[16,6,256]{2,0,1:T(8,128)(2,1)S(1)}, u32[]{:S(2)}, u32[]{:S(2)}) collective-permute-start(bf16[16,6,256]{2,0,1:T(8,128)(2,1)S(1)} %get-tuple-element.44), channel_id=1, source_target_pairs={{1,0},{2,1},{3,2},{4,3},{5,4},{6,5},{7,6},{8,7},{9,8},{10,9},{11,1... | collective-permute-start | bytes 147464 | tf_op jit(solution)/shard_map/ppermute | solution.py:17
  63.1 8.9 %collective-permute-start.2 = (bf16[16,6,256]{2,0,1:T(8,128)(2,1)S(1)}, bf16[16,6,256]{2,0,1:T(8,128)(2,1)S(1)}, u32[]{:S(2)}, u32[]{:S(2)}) collective-permute-start(bf16[16,6,256]{2,0,1:T(8,128)(2,1)S(1)} %get-tuple-element.43), channel_id=1, source_target_pairs={{0,1},{1,2},{2,3},{3,4},{4,5},{5,6},{6,7},{7,8},{8,9},{9,10},{10,1... | collective-permute-start | bytes 147464 | tf_op jit(solution)/shard_map/ppermute | solution.py:14
  88.1 0.9 copy-start.8
  89.4 0.7 copy-start.12
  90.1 1.6 %copy-start.1 = (bf16[128,1024]{1,0:T(8,128)(2,1)S(1)}, bf16[128,1024]{1,0:T(8,128)(2,1)}, u32[]{:S(2)}) copy-start(bf16[128,1024]{1,0:T(8,128)(2,1)} %param.15) | copy-start | bytes 786436

commit v9 on v7

--- a/solution.py
+++ b/solution.py
@@ -32,18 +32,16 @@
 
 def project(encoded, mix_w, mix_b, frames, group_width):
     channels, row_count, col_count = encoded.shape
-    rows = row_count // frames
-    blocks = encoded.reshape(channels, frames, rows, col_count).transpose(1, 0, 2, 3)
-    stacked = lax.all_to_all(blocks, "frame", 0, 0, tiled=False)
-    stacked = stacked.reshape(frames * channels, rows, col_count)
+    stacked = lax.all_to_all(encoded, "frame", 1, 0, tiled=True)
     hidden = (
         jnp.einsum("ji,irw->jrw", mix_w, stacked, preferred_element_type=jnp.float32)
         + mix_b[:, None, None]
     ).astype(jnp.bfloat16)
+    rows = hidden.shape[1]
     hidden = hidden.reshape(GROUPS, group_width, rows, col_count)
     hidden = jnp.repeat(hidden, frames // GROUPS, axis=0)
-    own = lax.all_to_all(hidden, "frame", 0, 0, tiled=False)
-    return own.transpose(1, 0, 2, 3).reshape(group_width, row_count, col_count)
+    hidden = hidden.reshape(frames * group_width, rows, col_count)
+    return lax.all_to_all(hidden, "frame", 0, 1, tiled=True)
 
 
 def branches(margin, weights, biases, row_count, col_count):

time: 84.5 us -> 86 us (1.018)
    unnamed x42 -> x45, local copies, waits for them, and re-layouts: 6.51 us -> 7.34 us
where the time goes in v9:
time: 86 us; the launch traced here: 85.4 us
  blocking collectives  21.1 us (25%)
  starting transfers between devices  17.4 us (20%)
  matrix products  16.5 us (19%)
  waiting for transfers between devices  16.2 us (19%)
  local copies, waits for them, and re-layouts  12 us (14%)
  other arithmetic  1.33 us (2%)
    all_to_all x1, blocking collectives, project(): stacked = lax.all_to_all(encoded, 'frame', 1, 0, tiled=True)  21.1 us
    dot_general x26, matrix products, branches(): jnp.einsum('doi,dirw->orw', weight[a], window, preferred_element_type=jnp...  12.1 us
    unnamed x45, local copies, waits for them, and re-layouts  7.34 us
    all_to_all x1, waiting for transfers between devices, project(): return lax.all_to_all(hidden, 'frame', 0, 1, tiled=True)  7.34 us
    ppermute x1, waiting for transfers between devices, padded_2(): lax.ppermute(lax.slice_in_dim(block, block.shape[dim] - width, None, axis...  6.81 us
    all_to_all x1, starting transfers between devices, project(): return lax.all_to_all(hidden, 'frame', 0, 1, tiled=True)  4.88 us
    ppermute x1, starting transfers between devices, padded_2(): lax.ppermute(lax.slice_in_dim(block, 0, width, axis=dim), axis, backward)  4.44 us
    ppermute x1, starting transfers between devices, halo_rows(): lax.ppermute(lax.slice_in_dim(block, 0, width, axis=dim), axis, backward)  4.08 us
  transfers between devices with their start and end apart: 5, of which 3 were waited for; matrix products, arithmetic and copies ran while one was open for 5% of the time, Pallas kernels for 0%

profile of v9, /device:TPU:456, one launch (start us, length us, event | category | flops | bytes accessed | tf_op | source)
XLA Modules:
  0.0 85.4 jit_solution(14585688139348403231)
XLA Ops:
  0.0 1.2 %fusion.222 = (bf16[1,64,2,256]{3,2,1,0:T(2,128)(2,1)S(1)}, bf16[1,64,2,256]{3,2,1,0:T(2,128)(2,1)S(1)}) fusion(bf16[1,64,16,256]{3,2,1,0:T(8,128)(2,1)} %param.12), kind=kLoop, calls=%fused_computation.272 | loop fusion | bytes 262144 | tf_op jit(solution)/shard_map/slice | solution.py:14
  1.2 4.1 %collective-permute-start.1 = (bf16[1,64,2,256]{3,1,2,0:T(8,128)(2,1)S(1)}, bf16[1,64,2,256]{3,1,2,0:T(8,128)(2,1)S(1)}, u32[]{:S(2)}, u32[]{:S(2)}) collective-permute-start(bf16[1,64,2,256]{3,1,2,0:T(8,128)(2,1)S(1)} %copy.153), channel_id=1, source_target_pairs={{1,0},{2,1},{3,2},{4,3},{5,4},{6,5},{7,6},{8,7},{9,8},{10,9},{11,1... | collective-permute-start | bytes 196616 | tf_op jit(solution)/shard_map/ppermute | solution.py:16
  5.3 1.9 %collective-permute-start = (bf16[1,64,2,256]{3,1,2,0:T(8,128)(2,1)S(1)}, bf16[1,64,2,256]{3,1,2,0:T(8,128)(2,1)S(1)}, u32[]{:S(2)}, u32[]{:S(2)}) collective-permute-start(bf16[1,64,2,256]{3,1,2,0:T(8,128)(2,1)S(1)} %copy.154), channel_id=1, source_target_pairs={{0,1},{1,2},{2,3},{3,4},{4,5},{5,6},{6,7},{7,8},{8,9},{9,10},{10,1... | collective-permute-start | bytes 196616 | tf_op jit(solution)/shard_map/ppermute | solution.py:13
  7.3 1.2 %copy.155 = bf16[1,64,16,256]{3,1,2,0:T(8,128)(2,1)S(1)} copy(bf16[1,64,16,256]{3,2,1,0:T(8,128)(2,1)} %param.12) | data formatting | bytes 1048576 | tf_op args[0]
  8.7 0.4 fusion.111
  9.3 0.7 copy-done.2
  10.0 0.4 fusion.54
  10.4 0.4 fusion.86
  10.8 0.2 copy-done.10
  11.1 0.5 fusion.106
  12.0 0.2 convolution_bitcast_fusion.27
  12.2 2.1 %collective-permute-done = bf16[1,64,2,256]{3,1,2,0:T(8,128)(2,1)S(1)} collective-permute-done((bf16[1,64,2,256]{3,1,2,0:T(8,128)(2,1)S(1)}, bf16[1,64,2,256]{3,1,2,0:T(8,128)(2,1)S(1)}, u32[]{:S(2)}, u32[]{:S(2)}) %collective-permute-start) | collective-permute-done | bytes 65568 | tf_op jit(solution)/shard_map/ppermute | solution.py:13
  14.8 0.2 convolution_bitcast_fusion.30
  15.0 0.2 fusion.133
  15.2 0.2 fusion.138
  15.6 21.1 %all_to_all.33 = bf16[64,16,256]{2,0,1:T(8,128)(2,1)S(1)} all-to-all(bf16[64,16,256]{2,0,1:T(8,128)(2,1)S(1)} %slice_bitcast_fusion), channel_id=1, replica_groups=mesh['frame'=16,'space'=32] {'frame'}, dimensions={1} | all-to-all | bytes 1048576 | tf_op jit(solution)/shard_map/all_to_all | solution.py:35
  36.8 0.2 fusion.97
  37.0 0.5 broadcast.83
  37.5 0.7 reduce
  38.2 0.7 reshape.118
  38.9 4.9 %all-to-all-start.1 = ((bf16[16,2,2048]{2,1,0:T(2,128)(2,1)}), bf16[16,2,2048]{2,1,0:T(2,128)(2,1)S(1)}, u32[]{:S(2)}, u32[]{:S(2)}) async-start(bf16[16,2,2048]{2,1,0:T(2,128)(2,1)} %reshape.118), calls=%async_computation.1 | async-start | bytes 262144 | tf_op jit(solution)/shard_map/all_to_all | solution.py:44
  43.8 7.3 %all-to-all-done.1 = bf16[16,2,2048]{2,1,0:T(2,128)(2,1)S(1)} async-done(((bf16[16,2,2048]{2,1,0:T(2,128)(2,1)}), bf16[16,2,2048]{2,1,0:T(2,128)(2,1)S(1)}, u32[]{:S(2)}, u32[]{:S(2)}) %all-to-all-start.1) | async-done | bytes 131104 | tf_op jit(solution)/shard_map/all_to_all | solution.py:44
  51.3 4.4 %collective-permute-start.3 = (bf16[16,6,256]{2,0,1:T(8,128)(2,1)S(1)}, bf16[16,6,256]{2,0,1:T(8,128)(2,1)S(1)}, u32[]{:S(2)}, u32[]{:S(2)}) collective-permute-start(bf16[16,6,256]{2,0,1:T(8,128)(2,1)S(1)} %get-tuple-element.22), channel_id=1, source_target_pairs={{1,0},{2,1},{3,2},{4,3},{5,4},{6,5},{7,6},{8,7},{9,8},{10,9},{11,1... | collective-permute-start | bytes 147464 | tf_op jit(solution)/shard_map/ppermute | solution.py:28
  55.8 2.1 %collective-permute-start.2 = (bf16[16,6,256]{2,0,1:T(8,128)(2,1)S(1)}, bf16[16,6,256]{2,0,1:T(8,128)(2,1)S(1)}, u32[]{:S(2)}, u32[]{:S(2)}) collective-permute-start(bf16[16,6,256]{2,0,1:T(8,128)(2,1)S(1)} %get-tuple-element.21), channel_id=1, source_target_pairs={{0,1},{1,2},{2,3},{3,4},{4,5},{5,6},{6,7},{7,8},{8,9},{9,10},{10,1... | collective-permute-start | bytes 147464 | tf_op jit(solution)/shard_map/ppermute | solution.py:25
  57.9 6.8 %collective-permute-done.2 = bf16[16,6,256]{2,0,1:T(8,128)(2,1)S(1)} collective-permute-done((bf16[16,6,256]{2,0,1:T(8,128)(2,1)S(1)}, bf16[16,6,256]{2,0,1:T(8,128)(2,1)S(1)}, u32[]{:S(2)}, u32[]{:S(2)}) %collective-permute-start.2) | collective-permute-done | bytes 49184 | tf_op jit(solution)/shard_map/ppermute | solution.py:25
  66.2 0.3 copy-done.3
  66.5 0.4 convolution_bitcast_fusion
  66.9 0.5 convolution_bitcast_fusion.1
  67.4 0.5 convolution_bitcast_fusion.2
  67.8 0.5 convolution_bitcast_fusion.3
  68.3 0.5 convolution_bitcast_fusion.4
  68.7 0.5 convolution_bitcast_fusion.5
  69.2 0.5 convolution_bitcast_fusion.6
  69.7 0.5 convolution_bitcast_fusion.7
  70.1 0.5 convolution_bitcast_fusion.8
  70.6 0.5 convolution_bitcast_fusion.9
  71.2 0.2 bitcast_dynamic-update-slice_fusion.14
  71.4 0.2 bitcast_dynamic-update-slice_fusion.5
  72.2 0.3 copy-done.4
  72.5 0.4 convolution_bitcast_fusion.11
  72.9 0.4 convolution_bitcast_fusion.12
  73.3 0.4 convolution_bitcast_fusion.13
  73.6 0.4 convolution_bitcast_fusion.14
  74.0 0.4 convolution_bitcast_fusion.15
  74.4 0.4 convolution_bitcast_fusion.16
  74.8 0.2 fusion.141
  75.1 0.4 convolution_bitcast_fusion.23
  75.5 0.4 convolution_bitcast_fusion.24
  75.9 0.5 copy-done.5
  76.4 0.4 convolution_bitcast_fusion.18
  76.8 0.4 convolution_bitcast_fusion.19
  77.1 0.4 convolution_bitcast_fusion.20
  77.5 0.4 convolution_bitcast_fusion.21
  77.9 0.5 compare_select_fusion.3
  78.3 0.8 compare_select_fusion.1
  79.1 1.1 %compare_select_fusion = f32[64,18,256]{2,0,1:T(8,128)S(1)} fusion(f32[18,256,64]{1,2,0:T(8,128)S(1)} %convolution_bitcast_fusion, f32[18,256,64]{1,2,0:T(8,128)S(1)} %convolution_bitcast_fusion.1, f32[18,256,64]{1,2,0:T(8,128)S(1)} %convolution_bitcast_fusion.2, f32[18,256,64]{1,2,0:T(8,128)S(1)} %convolution_bitcast_fusion.3, ...), kind=kOutput, calls=%fused_computation | convolution fusion | flops 107937792 | bytes 15544832 | tf_op jit(solution)/shard_map/doi,dirw->orw/dot_general | solution.py:60
  80.2 1.0 %fusion.98 = bf16[64,18,256]{2,0,1:T(8,128)(2,1)S(1)} fusion(f32[64,18,256]{2,0,1:T(8,128)S(1)} %compare_select_fusion, f32[64,18,256]{2,0,1:T(8,128)S(1)} %compare_select_fusion.1, f32[64,18,256]{2,0,1:T(8,128)S(1)} %compare_select_fusion.3, f32[18,256,64]{1,2,0:T(8,128)S(1)} %convolution_bitcast_fusion.18, ...), kind=kOutput, calls=%fused_computation.109 | convolution fusion | flops 52199424 | bytes 10605568 | tf_op jit(solution)/shard_map/doi,dirw->orw/dot_general | solution.py:60
  81.2 0.5 fusion.109
  81.7 0.2 pad_maximum_fusion
  81.9 0.7 copy-done.6
  82.6 0.4 fusion.12
  83.1 0.5 fusion.51
  83.7 0.6 fusion.101
  84.3 1.1 %copy.112 = bf16[1,64,16,256]{3,2,1,0:T(8,128)(2,1)} copy(bf16[1,64,16,256]{3,1,2,0:T(8,128)(2,1)S(1)} %fusion.101) | data formatting | bytes 1048576 | tf_op jit(solution)/shard_map/broadcast_in_dim | solution.py:96
  (59 shorter events, 3.9 us)
Async XLA Ops:
  0.0 36.8 %copy-start = (bf16[128,1024]{1,0:T(8,128)(2,1)S(1)}, bf16[128,1024]{1,0:T(8,128)(2,1)}, u32[]{:S(2)}) copy-start(bf16[128,1024]{1,0:T(8,128)(2,1)} %param.15) | copy-start | bytes 786436
  0.0 8.5 %copy-start.1 = (bf16[1,64,16,256]{3,2,1,0:T(8,128)(2,1)S(1)}, bf16[1,64,16,256]{3,2,1,0:T(8,128)(2,1)}, u32[]{:S(2)}) copy-start(bf16[1,64,16,256]{3,2,1,0:T(8,128)(2,1)} %param.12) | copy-start | bytes 1572868
  1.2 10.4 %collective-permute-start.1 = (bf16[1,64,2,256]{3,1,2,0:T(8,128)(2,1)S(1)}, bf16[1,64,2,256]{3,1,2,0:T(8,128)(2,1)S(1)}, u32[]{:S(2)}, u32[]{:S(2)}) collective-permute-start(bf16[1,64,2,256]{3,1,2,0:T(8,128)(2,1)S(1)} %copy.153), channel_id=1, source_target_pairs={{1,0},{2,1},{3,2},{4,3},{5,4},{6,5},{7,6},{8,7},{9,8},{10,9},{11,1... | collective-permute-start | bytes 196616 | tf_op jit(solution)/shard_map/ppermute | solution.py:16
  5.3 9.0 %collective-permute-start = (bf16[1,64,2,256]{3,1,2,0:T(8,128)(2,1)S(1)}, bf16[1,64,2,256]{3,1,2,0:T(8,128)(2,1)S(1)}, u32[]{:S(2)}, u32[]{:S(2)}) collective-permute-start(bf16[1,64,2,256]{3,1,2,0:T(8,128)(2,1)S(1)} %copy.154), channel_id=1, source_target_pairs={{0,1},{1,2},{2,3},{3,4},{4,5},{5,6},{6,7},{7,8},{8,9},{9,10},{10,1... | collective-permute-start | bytes 196616 | tf_op jit(solution)/shard_map/ppermute | solution.py:13
  9.1 0.9 %copy-start.2 = (bf16[3,3,64,64]{3,2,1,0:T(8,128)(2,1)S(1)}, bf16[3,3,64,64]{3,2,1,0:T(8,128)(2,1)}, u32[]{:S(2)}) copy-start(bf16[3,3,64,64]{3,2,1,0:T(8,128)(2,1)} %param.13) | copy-start | bytes 221188
  10.4 0.7 copy-start.10
  15.5 21.3 %copy-start.9 = (f32[128]{0:T(128)S(1)}, f32[128]{0:T(128)}, u32[]{:S(2)}) copy-start(f32[128]{0:T(128)} %param.16) | copy-start | bytes 1540
  15.6 28.2 %copy-start.8 = (f32[4,64]{1,0:T(4,128)S(1)}, f32[4,64]{1,0:T(4,128)}, u32[]{:S(2)}) copy-start(f32[4,64]{1,0:T(4,128)} %param.21) | copy-start | bytes 3076
  38.9 12.2 %all-to-all-start.1 = ((bf16[16,2,2048]{2,1,0:T(2,128)(2,1)}), bf16[16,2,2048]{2,1,0:T(2,128)(2,1)S(1)}, u32[]{:S(2)}, u32[]{:S(2)}) async-start(bf16[16,2,2048]{2,1,0:T(2,128)(2,1)} %reshape.118), calls=%async_computation.1 | async-start | bytes 262144 | tf_op jit(solution)/shard_map/all_to_all | solution.py:44
  51.3 6.6 %collective-permute-start.3 = (bf16[16,6,256]{2,0,1:T(8,128)(2,1)S(1)}, bf16[16,6,256]{2,0,1:T(8,128)(2,1)S(1)}, u32[]{:S(2)}, u32[]{:S(2)}) collective-permute-start(bf16[16,6,256]{2,0,1:T(8,128)(2,1)S(1)} %get-tuple-element.22), channel_id=1, source_target_pairs={{1,0},{2,1},{3,2},{4,3},{5,4},{6,5},{7,6},{8,7},{9,8},{10,9},{11,1... | collective-permute-start | bytes 147464 | tf_op jit(solution)/shard_map/ppermute | solution.py:28
  55.8 8.9 %collective-permute-start.2 = (bf16[16,6,256]{2,0,1:T(8,128)(2,1)S(1)}, bf16[16,6,256]{2,0,1:T(8,128)(2,1)S(1)}, u32[]{:S(2)}, u32[]{:S(2)}) collective-permute-start(bf16[16,6,256]{2,0,1:T(8,128)(2,1)S(1)} %get-tuple-element.21), channel_id=1, source_target_pairs={{0,1},{1,2},{2,3},{3,4},{4,5},{5,6},{6,7},{7,8},{8,9},{9,10},{10,1... | collective-permute-start | bytes 147464 | tf_op jit(solution)/shard_map/ppermute | solution.py:25
  65.4 1.0 %copy-start.3 = (bf16[11,11,64,16]{2,3,1,0:T(8,128)(2,1)S(1)}, bf16[11,11,64,16]{2,3,1,0:T(8,128)(2,1)}, u32[]{:S(2)}) copy-start(bf16[11,11,64,16]{2,3,1,0:T(8,128)(2,1)} %param.20) | copy-start | bytes 743428
  71.6 0.9 %copy-start.4 = (bf16[7,7,64,16]{2,3,1,0:T(8,128)(2,1)S(1)}, bf16[7,7,64,16]{2,3,1,0:T(8,128)(2,1)}, u32[]{:S(2)}) copy-start(bf16[7,7,64,16]{2,3,1,0:T(8,128)(2,1)} %param.19) | copy-start | bytes 301060
  74.4 0.8 copy-start.7
  75.5 0.9 %copy-start.5 = (bf16[5,5,64,16]{2,3,1,0:T(8,128)(2,1)S(1)}, bf16[5,5,64,16]{2,3,1,0:T(8,128)(2,1)}, u32[]{:S(2)}) copy-start(bf16[5,5,64,16]{2,3,1,0:T(8,128)(2,1)} %param.18) | copy-start | bytes 153604
  81.7 0.9 %copy-start.6 = (bf16[3,3,64,64]{3,2,1,0:T(8,128)(2,1)S(1)}, bf16[3,3,64,64]{3,2,1,0:T(8,128)(2,1)}, u32[]{:S(2)}) copy-start(bf16[3,3,64,64]{3,2,1,0:T(8,128)(2,1)} %param.22) | copy-start | bytes 221188
  83.0 0.7 copy-start.11

commit v10 on v7

--- a/solution.py
+++ b/solution.py
@@ -116,18 +116,28 @@
     frames = lax.axis_size("frame")
     channels, row_count, col_count = (features.shape[1], features.shape[2], features.shape[3])
     low, high = halo_rows(features, "space", 2, 2)
+    above = jnp.concatenate([low, features[:, :, :2]], axis=2)
+    below = jnp.concatenate([features[:, :, -2:], high], axis=2)
+    inner = jnp.concatenate(
+        [
+            finish(above[:, :, 1:], enc_w, enc_b, 1, col_count),
+            finish(features, enc_w, enc_b, row_count - 2, col_count),
+            finish(below[:, :, :-1], enc_w, enc_b, 1, col_count),
+        ],
+        axis=2,
+    )
     encoded = jnp.concatenate(
         [
-            finish(jnp.concatenate([low, features[:, :, :2]], axis=2), enc_w, enc_b, 2, col_count),
-            finish(features, enc_w, enc_b, row_count - 2, col_count),
-            finish(jnp.concatenate([features[:, :, -2:], high], axis=2), enc_w, enc_b, 2, col_count),
+            finish(above[:, :, :-1], enc_w, enc_b, 1, col_count),
+            inner,
+            finish(below[:, :, 1:], enc_w, enc_b, 1, col_count),
         ],
         axis=2,
     )
     hidden_count = mix_w.shape[0]
     per_group = frames * channels // GROUPS
     group_width = hidden_count // GROUPS
-    own_groups = project(encoded[0, :, 1:-1], mix_w, mix_b, frames, group_width)
+    own_groups = project(inner[0], mix_w, mix_b, frames, group_width)
     margin = padded_2(own_groups, (("space", 1),), 6)
     margin = jnp.pad(margin, ((0, 0), (0, 0), (5, 5)))
     summed = branches(

time: 84.5 us -> 86.3 us (1.021)
  the two profiles are of different devices: /device:TPU:456 before, /device:TPU:256 now
where the time goes in v10:
time: 86.3 us; the launch traced here: 85.6 us
  waiting for transfers between devices  27.3 us (32%)
  starting transfers between devices  27.2 us (32%)
  matrix products  17.6 us (20%)
  local copies, waits for them, and re-layouts  11.3 us (13%)
  other arithmetic  1.5 us (2%)
    dot_general x26, matrix products, branches(): jnp.einsum('doi,dirw->orw', weight[a], window, preferred_element_type=jnp...  12.1 us
    all_to_all x1, waiting for transfers between devices, project(): stacked = lax.all_to_all(blocks, 'frame', 0, 0, tiled=False)  11.9 us
    all_to_all x1, waiting for transfers between devices, project(): own = lax.all_to_all(hidden, 'frame', 0, 0, tiled=False)  8.15 us
    all_to_all x1, starting transfers between devices, project(): stacked = lax.all_to_all(blocks, 'frame', 0, 0, tiled=False)  8.11 us
    ppermute x1, starting transfers between devices, halo_rows(): lax.ppermute(lax.slice_in_dim(block, 0, width, axis=dim), axis, backward)  7.86 us
    ppermute x1, waiting for transfers between devices, padded_2(): lax.ppermute(lax.slice_in_dim(block, block.shape[dim] - width, None, axis...  7.28 us
    unnamed x42, local copies, waits for them, and re-layouts  6.29 us
    dot_general x18, matrix products, finish(): jnp.einsum('doi,dirw->orw', weight[a], window, preferred_element_type=jnp...  5.22 us
  transfers between devices with their start and end apart: 6, of which 3 were waited for; matrix products, arithmetic and copies ran while one was open for 5% of the time, Pallas kernels for 0%

profile of v10, /device:TPU:256, one launch (start us, length us, event | category | flops | bytes accessed | tf_op | source)
XLA Modules:
  0.0 85.6 jit_solution(10216978203281644792)
XLA Ops:
  0.0 1.2 %fusion.238 = (bf16[1,64,2,256]{3,2,1,0:T(2,128)(2,1)S(1)}, bf16[1,64,2,256]{3,2,1,0:T(2,128)(2,1)S(1)}) fusion(bf16[1,64,16,256]{3,2,1,0:T(8,128)(2,1)} %param.12), kind=kLoop, calls=%fused_computation.328 | loop fusion | bytes 262144 | tf_op jit(solution)/shard_map/slice | solution.py:119
  1.2 1.9 %collective-permute-start = (bf16[1,64,2,256]{3,1,2,0:T(8,128)(2,1)S(1)}, bf16[1,64,2,256]{3,1,2,0:T(8,128)(2,1)S(1)}, u32[]{:S(2)}, u32[]{:S(2)}) collective-permute-start(bf16[1,64,2,256]{3,1,2,0:T(8,128)(2,1)S(1)} %copy.135), channel_id=1, source_target_pairs={{0,1},{1,2},{2,3},{3,4},{4,5},{5,6},{6,7},{7,8},{8,9},{9,10},{10,1... | collective-permute-start | bytes 196616 | tf_op jit(solution)/shard_map/ppermute | solution.py:13
  3.2 7.9 %collective-permute-start.1 = (bf16[1,64,2,256]{3,1,2,0:T(8,128)(2,1)S(1)}, bf16[1,64,2,256]{3,1,2,0:T(8,128)(2,1)S(1)}, u32[]{:S(2)}, u32[]{:S(2)}) collective-permute-start(bf16[1,64,2,256]{3,1,2,0:T(8,128)(2,1)S(1)} %copy.136), channel_id=1, source_target_pairs={{1,0},{2,1},{3,2},{4,3},{5,4},{6,5},{7,6},{8,7},{9,8},{10,9},{11,1... | collective-permute-start | bytes 196616 | tf_op jit(solution)/shard_map/ppermute | solution.py:16
  11.0 1.2 %copy.137 = bf16[1,64,16,256]{3,1,2,0:T(8,128)(2,1)S(1)} copy(bf16[1,64,16,256]{3,2,1,0:T(8,128)(2,1)} %param.12) | data formatting | bytes 1048576 | tf_op args[0]
  12.4 0.4 fusion.119
  13.0 0.7 copy-done.2
  13.8 0.4 fusion.54
  14.2 0.4 fusion.86
  14.8 0.2 convolution_bitcast_fusion.29
  15.4 0.2 convolution_bitcast_fusion.35
  16.4 0.2 fusion.144
  16.6 0.2 constant_dynamic-update-slice_fusion.5
  16.8 0.5 constant_dynamic-update-slice_fusion.4
  17.4 0.2 constant_dynamic-update-slice_fusion.3
  17.6 0.9 %maximum_bitcast_fusion = bf16[16,64,1,256]{3,1,2,0:T(8,128)(2,1)} fusion(bf16[1,64,1,256]{3,1,2,0:T(8,128)(2,1)S(1)} %get-tuple-element.45, bf16[1,64,14,256]{3,1,2,0:T(8,128)(2,1)S(1)} %get-tuple-element.43, bf16[1,64,1,256]{3,1,2,0:T(8,128)(2,1)S(1)} %get-tuple-element.41), kind=kLoop, calls=%fused_computation.137 | loop fusion | flops 524288 | bytes 1048576 | tf_op jit(solution)/shard_map/transpose | solution.py:36
  18.5 8.1 %all-to-all-start = ((bf16[16,64,1,256]{3,1,2,0:T(8,128)(2,1)}), bf16[16,64,1,256]{3,1,2,0:T(8,128)(2,1)S(1)}, u32[]{:S(2)}, u32[]{:S(2)}) async-start(bf16[16,64,1,256]{3,1,2,0:T(8,128)(2,1)} %maximum_bitcast_fusion), calls=%async_computation | async-start | bytes 1048576 | tf_op jit(solution)/shard_map/all_to_all | solution.py:37
  26.8 11.9 %all-to-all-done = bf16[16,64,1,256]{3,1,2,0:T(8,128)(2,1)S(1)} async-done(((bf16[16,64,1,256]{3,1,2,0:T(8,128)(2,1)}), bf16[16,64,1,256]{3,1,2,0:T(8,128)(2,1)S(1)}, u32[]{:S(2)}, u32[]{:S(2)}) %all-to-all-start) | async-done | bytes 524320 | tf_op jit(solution)/shard_map/all_to_all | solution.py:37
  38.6 0.2 fusion.89
  38.9 0.7 broadcast_in_dim.45
  39.6 4.0 %all-to-all-start.1 = ((bf16[16,16,1,256]{3,1,2,0:T(8,128)(2,1)}), bf16[16,16,1,256]{3,1,2,0:T(8,128)(2,1)S(1)}, u32[]{:S(2)}, u32[]{:S(2)}) async-start(bf16[16,16,1,256]{3,1,2,0:T(8,128)(2,1)} %bitcast.48), calls=%async_computation.1 | async-start | bytes 262144 | tf_op jit(solution)/shard_map/all_to_all | solution.py:45
  44.0 8.1 %all-to-all-done.1 = bf16[16,16,1,256]{3,1,2,0:T(8,128)(2,1)S(1)} async-done(((bf16[16,16,1,256]{3,1,2,0:T(8,128)(2,1)}), bf16[16,16,1,256]{3,1,2,0:T(8,128)(2,1)S(1)}, u32[]{:S(2)}, u32[]{:S(2)}) %all-to-all-start.1) | async-done | bytes 131104 | tf_op jit(solution)/shard_map/all_to_all | solution.py:45
  52.2 3.2 %collective-permute-start.3 = (bf16[16,6,256]{2,0,1:T(8,128)(2,1)S(1)}, bf16[16,6,256]{2,0,1:T(8,128)(2,1)S(1)}, u32[]{:S(2)}, u32[]{:S(2)}) collective-permute-start(bf16[16,6,256]{2,0,1:T(8,128)(2,1)S(1)} %get-tuple-element.27), channel_id=1, source_target_pairs={{1,0},{2,1},{3,2},{4,3},{5,4},{6,5},{7,6},{8,7},{9,8},{10,9},{11,1... | collective-permute-start | bytes 147464 | tf_op jit(solution)/shard_map/ppermute | solution.py:28
  55.4 2.1 %collective-permute-start.2 = (bf16[16,6,256]{2,0,1:T(8,128)(2,1)S(1)}, bf16[16,6,256]{2,0,1:T(8,128)(2,1)S(1)}, u32[]{:S(2)}, u32[]{:S(2)}) collective-permute-start(bf16[16,6,256]{2,0,1:T(8,128)(2,1)S(1)} %get-tuple-element.26), channel_id=1, source_target_pairs={{0,1},{1,2},{2,3},{3,4},{4,5},{5,6},{6,7},{7,8},{8,9},{9,10},{10,1... | collective-permute-start | bytes 147464 | tf_op jit(solution)/shard_map/ppermute | solution.py:25
  57.5 0.2 fusion.142
  57.7 7.3 %collective-permute-done.2 = bf16[16,6,256]{2,0,1:T(8,128)(2,1)S(1)} collective-permute-done((bf16[16,6,256]{2,0,1:T(8,128)(2,1)S(1)}, bf16[16,6,256]{2,0,1:T(8,128)(2,1)S(1)}, u32[]{:S(2)}, u32[]{:S(2)}) %collective-permute-start.2) | collective-permute-done | bytes 49184 | tf_op jit(solution)/shard_map/ppermute | solution.py:25
  66.5 0.3 copy-done.3
  66.8 0.4 convolution_bitcast_fusion
  67.2 0.5 convolution_bitcast_fusion.1
  67.7 0.5 convolution_bitcast_fusion.2
  68.1 0.5 convolution_bitcast_fusion.3
  68.6 0.5 convolution_bitcast_fusion.4
  69.0 0.5 convolution_bitcast_fusion.5
  69.5 0.5 convolution_bitcast_fusion.6
  69.9 0.5 convolution_bitcast_fusion.7
  70.4 0.5 convolution_bitcast_fusion.8
  70.9 0.5 convolution_bitcast_fusion.9
  71.4 0.2 bitcast_dynamic-update-slice_fusion.14
  71.7 0.2 bitcast_dynamic-update-slice_fusion.5
  72.5 0.3 copy-done.4
  72.8 0.4 convolution_bitcast_fusion.11
  73.2 0.4 convolution_bitcast_fusion.12
  73.6 0.4 convolution_bitcast_fusion.13
  73.9 0.4 convolution_bitcast_fusion.14
  74.3 0.4 convolution_bitcast_fusion.15
  74.7 0.4 convolution_bitcast_fusion.16
  75.0 0.2 fusion.139
  75.4 0.4 convolution_bitcast_fusion.23
  75.8 0.4 convolution_bitcast_fusion.24
  76.2 0.5 copy-done.5
  76.7 0.4 convolution_bitcast_fusion.18
  77.1 0.4 convolution_bitcast_fusion.19
  77.4 0.4 convolution_bitcast_fusion.20
  77.8 0.4 convolution_bitcast_fusion.21
  78.2 0.5 compare_select_fusion.3
  78.6 0.8 compare_select_fusion.1
  79.4 1.1 %compare_select_fusion = f32[64,18,256]{2,0,1:T(8,128)S(1)} fusion(f32[18,256,64]{1,2,0:T(8,128)S(1)} %convolution_bitcast_fusion, f32[18,256,64]{1,2,0:T(8,128)S(1)} %convolution_bitcast_fusion.1, f32[18,256,64]{1,2,0:T(8,128)S(1)} %convolution_bitcast_fusion.2, f32[18,256,64]{1,2,0:T(8,128)S(1)} %convolution_bitcast_fusion.3, ...), kind=kOutput, calls=%fused_computation | convolution fusion | flops 107937792 | bytes 15544832 | tf_op jit(solution)/shard_map/doi,dirw->orw/dot_general | solution.py:62
  80.5 0.9 %fusion.106 = bf16[64,18,256]{2,0,1:T(8,128)(2,1)S(1)} fusion(f32[64,18,256]{2,0,1:T(8,128)S(1)} %compare_select_fusion, f32[64,18,256]{2,0,1:T(8,128)S(1)} %compare_select_fusion.1, f32[64,18,256]{2,0,1:T(8,128)S(1)} %compare_select_fusion.3, f32[18,256,64]{1,2,0:T(8,128)S(1)} %convolution_bitcast_fusion.18, ...), kind=kOutput, calls=%fused_computation.123 | convolution fusion | flops 51609600 | bytes 10605568 | tf_op jit(solution)/shard_map/doi,dirw->orw/dot_general | solution.py:62
  81.5 0.5 fusion.117
  82.0 0.2 pad_maximum_fusion
  82.2 0.7 copy-done.6
  82.9 0.4 fusion.12
  83.3 0.5 fusion.51
  84.0 0.6 fusion.109
  84.6 1.1 %copy.86 = bf16[1,64,16,256]{3,2,1,0:T(8,128)(2,1)} copy(bf16[1,64,16,256]{3,1,2,0:T(8,128)(2,1)S(1)} %fusion.109) | data formatting | bytes 1048576 | tf_op jit(solution)/shard_map/broadcast_in_dim | solution.py:98
  (64 shorter events, 4.7 us)
Async XLA Ops:
  0.0 38.6 %copy-start = (bf16[128,1024]{1,0:T(8,128)(2,1)S(1)}, bf16[128,1024]{1,0:T(8,128)(2,1)}, u32[]{:S(2)}) copy-start(bf16[128,1024]{1,0:T(8,128)(2,1)} %param.15) | copy-start | bytes 786436
  0.0 12.3 %copy-start.1 = (bf16[1,64,16,256]{3,2,1,0:T(8,128)(2,1)S(1)}, bf16[1,64,16,256]{3,2,1,0:T(8,128)(2,1)}, u32[]{:S(2)}) copy-start(bf16[1,64,16,256]{3,2,1,0:T(8,128)(2,1)} %param.12) | copy-start | bytes 1572868
  1.2 13.4 %collective-permute-start = (bf16[1,64,2,256]{3,1,2,0:T(8,128)(2,1)S(1)}, bf16[1,64,2,256]{3,1,2,0:T(8,128)(2,1)S(1)}, u32[]{:S(2)}, u32[]{:S(2)}) collective-permute-start(bf16[1,64,2,256]{3,1,2,0:T(8,128)(2,1)S(1)} %copy.135), channel_id=1, source_target_pairs={{0,1},{1,2},{2,3},{3,4},{4,5},{5,6},{6,7},{7,8},{8,9},{9,10},{10,1... | collective-permute-start | bytes 196616 | tf_op jit(solution)/shard_map/ppermute | solution.py:13
  3.2 12.6 %collective-permute-start.1 = (bf16[1,64,2,256]{3,1,2,0:T(8,128)(2,1)S(1)}, bf16[1,64,2,256]{3,1,2,0:T(8,128)(2,1)S(1)}, u32[]{:S(2)}, u32[]{:S(2)}) collective-permute-start(bf16[1,64,2,256]{3,1,2,0:T(8,128)(2,1)S(1)} %copy.136), channel_id=1, source_target_pairs={{1,0},{2,1},{3,2},{4,3},{5,4},{6,5},{7,6},{8,7},{9,8},{10,9},{11,1... | collective-permute-start | bytes 196616 | tf_op jit(solution)/shard_map/ppermute | solution.py:16
  12.9 0.9 %copy-start.2 = (bf16[3,3,64,64]{3,2,1,0:T(8,128)(2,1)S(1)}, bf16[3,3,64,64]{3,2,1,0:T(8,128)(2,1)}, u32[]{:S(2)}) copy-start(bf16[3,3,64,64]{3,2,1,0:T(8,128)(2,1)} %param.13) | copy-start | bytes 221188
  15.3 1.0 %copy-start.10 = (f32[64]{0:T(128)S(1)}, f32[64]{0:T(128)}, u32[]{:S(2)}) copy-start(f32[64]{0:T(128)} %param.14) | copy-start | bytes 772
  17.4 9.3 %copy-start.8 = (f32[4,64]{1,0:T(4,128)S(1)}, f32[4,64]{1,0:T(4,128)}, u32[]{:S(2)}) copy-start(f32[4,64]{1,0:T(4,128)} %param.21) | copy-start | bytes 3076
  17.4 21.3 %copy-start.9 = (f32[128]{0:T(128)S(1)}, f32[128]{0:T(128)}, u32[]{:S(2)}) copy-start(f32[128]{0:T(128)} %param.16) | copy-start | bytes 1540
  18.5 20.2 %all-to-all-start = ((bf16[16,64,1,256]{3,1,2,0:T(8,128)(2,1)}), bf16[16,64,1,256]{3,1,2,0:T(8,128)(2,1)S(1)}, u32[]{:S(2)}, u32[]{:S(2)}) async-start(bf16[16,64,1,256]{3,1,2,0:T(8,128)(2,1)} %maximum_bitcast_fusion), calls=%async_computation | async-start | bytes 1048576 | tf_op jit(solution)/shard_map/all_to_all | solution.py:37
  39.6 12.6 %all-to-all-start.1 = ((bf16[16,16,1,256]{3,1,2,0:T(8,128)(2,1)}), bf16[16,16,1,256]{3,1,2,0:T(8,128)(2,1)S(1)}, u32[]{:S(2)}, u32[]{:S(2)}) async-start(bf16[16,16,1,256]{3,1,2,0:T(8,128)(2,1)} %bitcast.48), calls=%async_computation.1 | async-start | bytes 262144 | tf_op jit(solution)/shard_map/all_to_all | solution.py:45
  52.2 5.5 %collective-permute-start.3 = (bf16[16,6,256]{2,0,1:T(8,128)(2,1)S(1)}, bf16[16,6,256]{2,0,1:T(8,128)(2,1)S(1)}, u32[]{:S(2)}, u32[]{:S(2)}) collective-permute-start(bf16[16,6,256]{2,0,1:T(8,128)(2,1)S(1)} %get-tuple-element.27), channel_id=1, source_target_pairs={{1,0},{2,1},{3,2},{4,3},{5,4},{6,5},{7,6},{8,7},{9,8},{10,9},{11,1... | collective-permute-start | bytes 147464 | tf_op jit(solution)/shard_map/ppermute | solution.py:28
  55.4 9.6 %collective-permute-start.2 = (bf16[16,6,256]{2,0,1:T(8,128)(2,1)S(1)}, bf16[16,6,256]{2,0,1:T(8,128)(2,1)S(1)}, u32[]{:S(2)}, u32[]{:S(2)}) collective-permute-start(bf16[16,6,256]{2,0,1:T(8,128)(2,1)S(1)} %get-tuple-element.26), channel_id=1, source_target_pairs={{0,1},{1,2},{2,3},{3,4},{4,5},{5,6},{6,7},{7,8},{8,9},{9,10},{10,1... | collective-permute-start | bytes 147464 | tf_op jit(solution)/shard_map/ppermute | solution.py:25
  65.7 1.0 %copy-start.3 = (bf16[11,11,64,16]{2,3,1,0:T(8,128)(2,1)S(1)}, bf16[11,11,64,16]{2,3,1,0:T(8,128)(2,1)}, u32[]{:S(2)}) copy-start(bf16[11,11,64,16]{2,3,1,0:T(8,128)(2,1)} %param.20) | copy-start | bytes 743428
  71.9 0.9 %copy-start.4 = (bf16[7,7,64,16]{2,3,1,0:T(8,128)(2,1)S(1)}, bf16[7,7,64,16]{2,3,1,0:T(8,128)(2,1)}, u32[]{:S(2)}) copy-start(bf16[7,7,64,16]{2,3,1,0:T(8,128)(2,1)} %param.19) | copy-start | bytes 301060
  74.7 0.8 copy-start.7
  75.8 0.9 %copy-start.5 = (bf16[5,5,64,16]{2,3,1,0:T(8,128)(2,1)S(1)}, bf16[5,5,64,16]{2,3,1,0:T(8,128)(2,1)}, u32[]{:S(2)}) copy-start(bf16[5,5,64,16]{2,3,1,0:T(8,128)(2,1)} %param.18) | copy-start | bytes 153604
  82.0 0.9 %copy-start.6 = (bf16[3,3,64,64]{3,2,1,0:T(8,128)(2,1)S(1)}, bf16[3,3,64,64]{3,2,1,0:T(8,128)(2,1)}, u32[]{:S(2)}) copy-start(bf16[3,3,64,64]{3,2,1,0:T(8,128)(2,1)} %param.22) | copy-start | bytes 221188
  83.3 0.7 copy-start.11

commit v11 on v7

--- a/solution.py
+++ b/solution.py
@@ -89,12 +89,14 @@
     shifted = jnp.stack(
         [lax.slice_in_dim(padded, b, b + col_count, axis=2) for b in range(weight.shape[1])]
     )
-    summed = jnp.zeros((weight.shape[2], row_count, col_count), jnp.float32)
+    summed = jnp.zeros((weight.shape[2], row_count * col_count), jnp.float32)
     for a in range(weight.shape[0]):
         window = lax.slice_in_dim(shifted, a, a + row_count, axis=2)
+        window = window.reshape(window.shape[0], window.shape[1], row_count * col_count)
         summed = summed + jnp.einsum(
-            "doi,dirw->orw", weight[a], window, preferred_element_type=jnp.float32
+            "doi,dip->op", weight[a], window, preferred_element_type=jnp.float32
         )
+    summed = summed.reshape(weight.shape[2], row_count, col_count)
     return jax.nn.silu(summed + bias[:, None, None]).astype(jnp.bfloat16)[None]
 
 

time: 84.5 us -> 109 us (1.29)
  the two profiles are of different devices: /device:TPU:456 before, /device:TPU:256 now
where the time goes in v11:
time: 109 us; the launch traced here: 108 us
  local copies, waits for them, and re-layouts  23.7 us (22%)
  matrix products  21.9 us (20%)
  blocking collectives  20 us (18%)
  starting transfers between devices  19 us (17%)
  waiting for transfers between devices  16 us (15%)
  other arithmetic  6.74 us (6%)
    all_to_all x1, blocking collectives, project(): stacked = lax.all_to_all(blocks, 'frame', 0, 0, tiled=False)  20 us
    dot_general x26, matrix products, branches(): jnp.einsum('doi,dirw->orw', weight[a], window, preferred_element_type=jnp...  12.1 us
    dot_general x12, matrix products, finish(): jnp.einsum('doi,dip->op', weight[a], window, preferred_element_type=jnp.f...  9.54 us
    all_to_all x1, waiting for transfers between devices, project(): own = lax.all_to_all(hidden, 'frame', 0, 0, tiled=False)  8.55 us
    reshape x12, local copies, waits for them, and re-layouts, finish(): window.reshape(window.shape[0], window.shape[1], row_count * col_count)  7.95 us
    ppermute x1, starting transfers between devices, halo_rows(): lax.ppermute(lax.slice_in_dim(block, 0, width, axis=dim), axis, backward)  7.86 us
    ppermute x1, waiting for transfers between devices, padded_2(): lax.ppermute(lax.slice_in_dim(block, block.shape[dim] - width, None, axis...  7.49 us
    unnamed x44, local copies, waits for them, and re-layouts  5.26 us
  transfers between devices with their start and end apart: 5, of which 2 were waited for; matrix products, arithmetic and copies ran while one was open for 22% of the time, Pallas kernels for 0%

profile of v11, /device:TPU:256, one launch (start us, length us, event | category | flops | bytes accessed | tf_op | source)
XLA Modules:
  0.0 108.1 jit_solution(7972310747571788451)
XLA Ops:
  0.0 1.9 %fusion.144 = (bf16[1,64,2,256]{3,2,1,0:T(2,128)(2,1)}, bf16[1,64,2,256]{3,2,1,0:T(2,128)(2,1)}) fusion(bf16[1,64,16,256]{3,2,1,0:T(8,128)(2,1)} %param.12), kind=kLoop, calls=%fused_computation.250 | loop fusion | bytes 262144 | tf_op jit(solution)/shard_map/slice | solution.py:14
  1.9 1.9 %collective-permute-start = (bf16[1,64,2,256]{3,2,1,0:T(2,128)(2,1)}, bf16[1,64,2,256]{3,2,1,0:T(2,128)(2,1)}, u32[]{:S(2)}, u32[]{:S(2)}) collective-permute-start(bf16[1,64,2,256]{3,2,1,0:T(2,128)(2,1)} %get-tuple-element.15), channel_id=1, source_target_pairs={{0,1},{1,2},{2,3},{3,4},{4,5},{5,6},{6,7},{7,8},{8,9},{9,10},{10,1... | collective-permute-start | bytes 196616 | tf_op jit(solution)/shard_map/ppermute | solution.py:13
  3.8 7.9 %collective-permute-start.1 = (bf16[1,64,2,256]{3,2,1,0:T(2,128)(2,1)}, bf16[1,64,2,256]{3,2,1,0:T(2,128)(2,1)}, u32[]{:S(2)}, u32[]{:S(2)}) collective-permute-start(bf16[1,64,2,256]{3,2,1,0:T(2,128)(2,1)} %get-tuple-element.16), channel_id=1, source_target_pairs={{1,0},{2,1},{3,2},{4,3},{5,4},{6,5},{7,6},{8,7},{9,8},{10,9},{11,1... | collective-permute-start | bytes 196616 | tf_op jit(solution)/shard_map/ppermute | solution.py:16
  11.7 1.6 %fusion.50 = (bf16[1,64,16,256]{3,2,1,0:T(8,128)(2,1)S(1)}, bf16[1,64,16,256]{3,2,1,0:T(8,128)(2,1)S(1)}) fusion(bf16[64,16,256]{2,1,0:T(8,128)(2,1)} %bitcast.568), kind=kLoop, calls=%fused_computation.108 | loop fusion | bytes 1572864 | tf_op jit(solution)/shard_map/stack | solution.py:89
  13.5 2.2 %fusion.143 = (bf16[3,64,14,256]{3,2,1,0:T(8,128)(2,1)S(1)}, bf16[3,64,14,256]{3,2,1,0:T(8,128)(2,1)}, bf16[3,64,14,256]{3,2,1,0:T(8,128)(2,1)S(1)}) fusion(bf16[3,64,16,256]{3,2,1,0:T(8,128)(2,1)S(1)} %pad_maximum_fusion.1), kind=kLoop, calls=%fused_computation.249 | loop fusion | bytes 8257536 | tf_op jit(solution)/shard_map/slice | solution.py:94
  15.7 3.7 %reshape.216 = bf16[3,64,3584]{2,1,0:T(8,128)(2,1)} reshape(bf16[3,64,14,256]{3,2,1,0:T(8,128)(2,1)} %get-tuple-element.9) | data formatting | bytes 2752512 | tf_op jit(solution)/shard_map/reshape | solution.py:95
  19.4 1.9 %reshape.215 = bf16[3,64,3584]{2,1,0:T(8,128)(2,1)} reshape(bf16[3,64,14,256]{3,2,1,0:T(8,128)(2,1)S(1)} %get-tuple-element.10) | data formatting | bytes 2752512 | tf_op jit(solution)/shard_map/reshape | solution.py:95
  21.3 2.8 %convolution_bitcast_fusion.3 = f32[3584,64]{0,1:T(8,128)} fusion(bf16[3,64,3584]{2,1,0:T(8,128)(2,1)} %reshape.216, bf16[3,3,64,64]{3,2,1,0:T(8,128)(2,1)S(1)} %copy-done.4), kind=kOutput, calls=%fused_computation.3 | convolution fusion | flops 88080384 | bytes 2342912 | tf_op jit(solution)/shard_map/doi,dip->op/dot_general | solution.py:96
  24.1 1.4 %convolution_bitcast_fusion.4 = f32[3584,64]{0,1:T(8,128)} fusion(bf16[3,64,3584]{2,1,0:T(8,128)(2,1)S(1)} %copy-done.2, bf16[3,3,64,64]{3,2,1,0:T(8,128)(2,1)S(1)} %copy-done.4), kind=kOutput, calls=%fused_computation.4 | convolution fusion | flops 88080384 | bytes 2342912 | tf_op jit(solution)/shard_map/doi,dip->op/dot_general | solution.py:96
  25.4 1.1 reshape.214
  26.5 2.8 %fusion.2 = f32[64,3584]{1,0:T(8,128)} fusion(f32[3584,64]{0,1:T(8,128)} %convolution_bitcast_fusion.3, f32[3584,64]{0,1:T(8,128)} %convolution_bitcast_fusion.4, bf16[3,64,3584]{2,1,0:T(8,128)(2,1)S(1)} %reshape.214, bf16[3,3,64,64]{3,2,1,0:T(8,128)(2,1)S(1)} %copy-done.4), kind=kOutput, calls=%fused_computation.8 | convolution fusion | flops 88539136 | bytes 4177920 | tf_op jit(solution)/shard_map/doi,dip->op/dot_general | solution.py:96
  29.3 1.5 %reshape.217 = f32[1,64,14,256]{3,2,1,0:T(8,128)S(1)} reshape(f32[64,3584]{1,0:T(8,128)} %fusion.2) | data formatting | bytes 1835008 | tf_op jit(solution)/shard_map/reshape | solution.py:99
  30.8 0.7 multiply_convert_fusion.1
  31.5 1.0 maximum_bitcast_fusion
  32.7 1.1 %pad_maximum_fusion.4 = bf16[3,64,4,256]{3,2,1,0:T(4,128)(2,1)S(1)} fusion(bf16[1,64,4,256]{3,2,1,0:T(4,128)(2,1)S(1)} %get-tuple-element.36, bf16[1,64,2,256]{3,2,1,0:T(2,128)(2,1)} %get-tuple-element.16, bf16[1,64,2,256]{3,2,1,0:T(2,128)(2,1)} %collective-permute-done, bf16[1,64,4,256]{3,2,1,0:T(4,128)(2,1)S(1)} %get-tuple-element.35), kind=kLoop, calls=%fused_computation.121 | loop fusion | flops 1572864 | bytes 786432 | tf_op jit(solution)/shard_map/stack | solution.py:89
  33.9 0.4 fusion.145
  35.4 1.0 maximum_bitcast_fusion.1
  36.7 1.1 %pad_maximum_fusion.5 = bf16[3,64,4,256]{3,2,1,0:T(4,128)(2,1)S(1)} fusion(bf16[1,64,4,256]{3,2,1,0:T(4,128)(2,1)S(1)} %get-tuple-element.38, bf16[1,64,2,256]{3,2,1,0:T(2,128)(2,1)} %collective-permute-done.1, bf16[1,64,2,256]{3,2,1,0:T(2,128)(2,1)} %get-tuple-element.15, bf16[1,64,4,256]{3,2,1,0:T(4,128)(2,1)S(1)} %get-tuple-element.37), kind=kLoop, calls=%fused_computation.122 | loop fusion | flops 1572864 | bytes 786432 | tf_op jit(solution)/shard_map/stack | solution.py:89
  37.8 0.4 fusion.146
  39.6 20.0 %all_to_all.10 = bf16[16,64,1,256]{3,1,2,0:T(8,128)(2,1)S(1)} all-to-all(bf16[16,64,1,256]{3,1,2,0:T(8,128)(2,1)S(1)} %slice_bitcast_fusion.3), channel_id=1, replica_groups=mesh['frame'=16,'space'=32] {'frame'}, dimensions={0} | all-to-all | bytes 1048576 | tf_op jit(solution)/shard_map/all_to_all | solution.py:37
  59.8 0.7 broadcast_in_dim.15
  60.5 4.0 %all-to-all-start.1 = ((bf16[16,16,1,256]{3,1,2,0:T(8,128)(2,1)}), bf16[16,16,1,256]{3,1,2,0:T(8,128)(2,1)S(1)}, u32[]{:S(2)}, u32[]{:S(2)}) async-start(bf16[16,16,1,256]{3,1,2,0:T(8,128)(2,1)} %bitcast.30), calls=%async_computation.1 | async-start | bytes 262144 | tf_op jit(solution)/shard_map/all_to_all | solution.py:45
  64.6 8.5 %all-to-all-done.1 = bf16[16,16,1,256]{3,1,2,0:T(8,128)(2,1)S(1)} async-done(((bf16[16,16,1,256]{3,1,2,0:T(8,128)(2,1)}), bf16[16,16,1,256]{3,1,2,0:T(8,128)(2,1)S(1)}, u32[]{:S(2)}, u32[]{:S(2)}) %all-to-all-start.1) | async-done | bytes 131104 | tf_op jit(solution)/shard_map/all_to_all | solution.py:45
  73.1 3.1 %collective-permute-start.3 = (bf16[16,6,256]{2,0,1:T(8,128)(2,1)S(1)}, bf16[16,6,256]{2,0,1:T(8,128)(2,1)S(1)}, u32[]{:S(2)}, u32[]{:S(2)}) collective-permute-start(bf16[16,6,256]{2,0,1:T(8,128)(2,1)S(1)} %get-tuple-element.34), channel_id=1, source_target_pairs={{1,0},{2,1},{3,2},{4,3},{5,4},{6,5},{7,6},{8,7},{9,8},{10,9},{11,1... | collective-permute-start | bytes 147464 | tf_op jit(solution)/shard_map/ppermute | solution.py:28
  76.2 2.1 %collective-permute-start.2 = (bf16[16,6,256]{2,0,1:T(8,128)(2,1)S(1)}, bf16[16,6,256]{2,0,1:T(8,128)(2,1)S(1)}, u32[]{:S(2)}, u32[]{:S(2)}) collective-permute-start(bf16[16,6,256]{2,0,1:T(8,128)(2,1)S(1)} %get-tuple-element.33), channel_id=1, source_target_pairs={{0,1},{1,2},{2,3},{3,4},{4,5},{5,6},{6,7},{7,8},{8,9},{9,10},{10,1... | collective-permute-start | bytes 147464 | tf_op jit(solution)/shard_map/ppermute | solution.py:25
  78.4 7.5 %collective-permute-done.2 = bf16[16,6,256]{2,0,1:T(8,128)(2,1)S(1)} collective-permute-done((bf16[16,6,256]{2,0,1:T(8,128)(2,1)S(1)}, bf16[16,6,256]{2,0,1:T(8,128)(2,1)S(1)}, u32[]{:S(2)}, u32[]{:S(2)}) %collective-permute-start.2) | collective-permute-done | bytes 49184 | tf_op jit(solution)/shard_map/ppermute | solution.py:25
  87.3 0.3 copy-done.5
  87.6 0.4 convolution_bitcast_fusion.6
  88.1 0.5 convolution_bitcast_fusion.7
  88.5 0.5 convolution_bitcast_fusion.8
  89.0 0.5 convolution_bitcast_fusion.9
  89.5 0.5 convolution_bitcast_fusion.10
  89.9 0.5 convolution_bitcast_fusion.11
  90.4 0.5 convolution_bitcast_fusion.12
  90.8 0.5 convolution_bitcast_fusion.13
  91.3 0.5 convolution_bitcast_fusion.14
  91.7 0.5 convolution_bitcast_fusion.15
  93.4 0.3 copy-done.6
  93.7 0.4 convolution_bitcast_fusion.17
  94.1 0.4 convolution_bitcast_fusion.18
  94.4 0.4 convolution_bitcast_fusion.19
  94.8 0.4 convolution_bitcast_fusion.20
  95.2 0.4 convolution_bitcast_fusion.21
  95.5 0.4 convolution_bitcast_fusion.22
  96.3 0.3 convolution_bitcast_fusion.29
  96.7 0.4 convolution_bitcast_fusion.30
  97.0 0.5 copy-done.8
  97.5 0.4 convolution_bitcast_fusion.24
  97.9 0.4 convolution_bitcast_fusion.25
  98.3 0.4 convolution_bitcast_fusion.26
  98.7 0.4 convolution_bitcast_fusion.27
  99.0 0.4 compare_select_fusion.3
  99.5 0.8 compare_select_fusion.1
  100.2 1.1 %compare_select_fusion = f32[64,18,256]{2,0,1:T(8,128)S(1)} fusion(f32[18,256,64]{1,2,0:T(8,128)S(1)} %convolution_bitcast_fusion.6, f32[18,256,64]{1,2,0:T(8,128)S(1)} %convolution_bitcast_fusion.7, f32[18,256,64]{1,2,0:T(8,128)S(1)} %convolution_bitcast_fusion.8, f32[18,256,64]{1,2,0:T(8,128)S(1)} %convolution_bitcast_fusion.9, ...), kind=kOutput, calls=%fused_computation.11 | convolution fusion | flops 107937792 | bytes 15544832 | tf_op jit(solution)/shard_map/doi,dirw->orw/dot_general | solution.py:62
  101.4 1.0 fusion.47
  102.3 0.5 fusion.48
  103.0 0.6 slice_bitcast_fusion.2
  104.0 0.7 copy-done.7
  104.7 0.5 convolution_bitcast_fusion
  105.2 0.5 convolution_bitcast_fusion.1
  105.8 0.5 fusion.4
  106.3 0.3 copy.122
  106.7 0.3 copy-done.13
  107.0 1.1 %multiply_convert_fusion = bf16[1,64,16,256]{3,2,1,0:T(8,128)(2,1)} fusion(f32[64]{0:T(128)S(1)} %copy-done.13, f32[1,64,16,256]{3,2,1,0:T(8,128)S(1)} %bitcast.566), kind=kLoop, calls=%fused_computation.97 | loop fusion | flops 1572864 | bytes 1573120 | tf_op jit(solution)/shard_map/convert_element_type | solution.py:100
  (76 shorter events, 6.9 us)
Async XLA Ops:
  0.0 59.6 %copy-start = (bf16[128,1024]{1,0:T(8,128)(2,1)S(1)}, bf16[128,1024]{1,0:T(8,128)(2,1)}, u32[]{:S(2)}) copy-start(bf16[128,1024]{1,0:T(8,128)(2,1)} %param.15) | copy-start | bytes 786436
  0.0 13.3 %copy-start.3 = (bf16[1,64,16,256]{3,2,1,0:T(8,128)(2,1)S(1)}, bf16[1,64,16,256]{3,2,1,0:T(8,128)(2,1)}, u32[]{:S(2)}) copy-start(bf16[1,64,16,256]{3,2,1,0:T(8,128)(2,1)} %param.12) | copy-start | bytes 1572868
  1.9 29.6 %collective-permute-start = (bf16[1,64,2,256]{3,2,1,0:T(2,128)(2,1)}, bf16[1,64,2,256]{3,2,1,0:T(2,128)(2,1)}, u32[]{:S(2)}, u32[]{:S(2)}) collective-permute-start(bf16[1,64,2,256]{3,2,1,0:T(2,128)(2,1)} %get-tuple-element.15), channel_id=1, source_target_pairs={{0,1},{1,2},{2,3},{3,4},{4,5},{5,6},{6,7},{7,8},{8,9},{9,10},{10,1... | collective-permute-start | bytes 196616 | tf_op jit(solution)/shard_map/ppermute | solution.py:13
  3.8 31.6 %collective-permute-start.1 = (bf16[1,64,2,256]{3,2,1,0:T(2,128)(2,1)}, bf16[1,64,2,256]{3,2,1,0:T(2,128)(2,1)}, u32[]{:S(2)}, u32[]{:S(2)}) collective-permute-start(bf16[1,64,2,256]{3,2,1,0:T(2,128)(2,1)} %get-tuple-element.16), channel_id=1, source_target_pairs={{1,0},{2,1},{3,2},{4,3},{5,4},{6,5},{7,6},{8,7},{9,8},{10,9},{11,1... | collective-permute-start | bytes 196616 | tf_op jit(solution)/shard_map/ppermute | solution.py:16
  19.3 1.9 %copy-start.4 = (bf16[3,3,64,64]{3,2,1,0:T(8,128)(2,1)S(1)}, bf16[3,3,64,64]{3,2,1,0:T(8,128)(2,1)}, u32[]{:S(2)}) copy-start(bf16[3,3,64,64]{3,2,1,0:T(8,128)(2,1)} %param.13) | copy-start | bytes 221188
  21.3 2.8 %copy-start.2 = (bf16[3,64,3584]{2,1,0:T(8,128)(2,1)S(1)}, bf16[3,64,3584]{2,1,0:T(8,128)(2,1)}, u32[]{:S(2)}) copy-start(bf16[3,64,3584]{2,1,0:T(8,128)(2,1)} %reshape.215) | copy-start | bytes 4128772
  29.3 1.5 %copy-start.10 = (f32[64]{0:T(128)S(1)}, f32[64]{0:T(128)}, u32[]{:S(2)}) copy-start(f32[64]{0:T(128)} %param.14) | copy-start | bytes 772
  39.5 20.1 %copy-start.12 = (f32[128]{0:T(128)S(1)}, f32[128]{0:T(128)}, u32[]{:S(2)}) copy-start(f32[128]{0:T(128)} %param.16) | copy-start | bytes 1540
  39.6 24.9 %copy-start.11 = (f32[4,64]{1,0:T(4,128)S(1)}, f32[4,64]{1,0:T(4,128)}, u32[]{:S(2)}) copy-start(f32[4,64]{1,0:T(4,128)} %param.21) | copy-start | bytes 3076
  60.5 12.6 %all-to-all-start.1 = ((bf16[16,16,1,256]{3,1,2,0:T(8,128)(2,1)}), bf16[16,16,1,256]{3,1,2,0:T(8,128)(2,1)S(1)}, u32[]{:S(2)}, u32[]{:S(2)}) async-start(bf16[16,16,1,256]{3,1,2,0:T(8,128)(2,1)} %bitcast.30), calls=%async_computation.1 | async-start | bytes 262144 | tf_op jit(solution)/shard_map/all_to_all | solution.py:45
  73.1 5.3 %collective-permute-start.3 = (bf16[16,6,256]{2,0,1:T(8,128)(2,1)S(1)}, bf16[16,6,256]{2,0,1:T(8,128)(2,1)S(1)}, u32[]{:S(2)}, u32[]{:S(2)}) collective-permute-start(bf16[16,6,256]{2,0,1:T(8,128)(2,1)S(1)} %get-tuple-element.34), channel_id=1, source_target_pairs={{1,0},{2,1},{3,2},{4,3},{5,4},{6,5},{7,6},{8,7},{9,8},{10,9},{11,1... | collective-permute-start | bytes 147464 | tf_op jit(solution)/shard_map/ppermute | solution.py:28
  76.2 9.6 %collective-permute-start.2 = (bf16[16,6,256]{2,0,1:T(8,128)(2,1)S(1)}, bf16[16,6,256]{2,0,1:T(8,128)(2,1)S(1)}, u32[]{:S(2)}, u32[]{:S(2)}) collective-permute-start(bf16[16,6,256]{2,0,1:T(8,128)(2,1)S(1)} %get-tuple-element.33), channel_id=1, source_target_pairs={{0,1},{1,2},{2,3},{3,4},{4,5},{5,6},{6,7},{7,8},{8,9},{9,10},{10,1... | collective-permute-start | bytes 147464 | tf_op jit(solution)/shard_map/ppermute | solution.py:25
  86.6 1.0 copy-start.5
  92.8 0.9 copy-start.6
  95.5 0.8 copy-start.9
  96.6 0.9 copy-start.8
  103.8 0.9 copy-start.7
  106.3 0.7 copy-start.13
  106.3 1.8 %copy-start.1 = (bf16[128,1024]{1,0:T(8,128)(2,1)S(1)}, bf16[128,1024]{1,0:T(8,128)(2,1)}, u32[]{:S(2)}) copy-start(bf16[128,1024]{1,0:T(8,128)(2,1)} %param.15) | copy-start | bytes 786436
